TPU v7x, 256 devices: a whole 4x4x8 slice. The times are simulated.
256 devices in a mesh: scen: 8 (over y, z_hi), grid: 32 (over x, z_lo, core).
Axes of the slice: x: 4, y: 4, z: 8 (z_hi: 2, z_lo: 4; z = z_hi * 4 + z_lo), core: 2. Of those that a mesh axis runs over, the one named last changes fastest.
Arguments:
- adjoint_in: float32 [16, 2, 50, 512, 128], P('scen', None, None, 'grid'), may hold values from -6 to 6
- surface_carbon: float32 [16, 512, 128], P('scen', 'grid'), may hold values from 1.9 to 2.1
- surface_alkalinity: float32 [16, 512, 128], P('scen', 'grid'), may hold values from 2.2 to 2.4
- east_velocity: float32 [50, 512, 128], P(None, 'grid'), may hold values from -0.1 to 0.1
- north_velocity: float32 [50, 512, 128], P(None, 'grid'), may hold values from -0.1 to 0.1
- east_diffusion: float32 [50], replicated, may hold values from 0.08 to 0.25
- north_diffusion: float32 [50], replicated, may hold values from 0.02 to 0.1
- vertical_mix: float32 [50, 512, 128], P(None, 'grid'), may hold values from 0.05 to 5
- thickness: float32 [50], replicated, may hold values from 0.5 to 4
- export_flux: float32 [50, 512, 128], P(None, 'grid'), may hold values from 0.1 to 1
- piston: float32 [512, 128], P('grid'), may hold values from 0.0005 to 0.005
- wet_mask: int32 [512, 128], P('grid'), may hold values 0 or 1
- bottom_level: int32 [512, 128], P('grid'), may hold values from 41 to 50
Outputs:
- adjoint_out: float32 [16, 2, 50, 512, 128], P('scen', None, None, 'grid')
- rate_gradient: float32 [50, 512, 128], P(None, 'grid')
All inputs are finite; a program needn't handle non-finite values. No bound on the sum of `wet_mask` on one device may be relied on, other than what follows from the above.
Results may differ from a plain program's by a relative error of at most 0.00002.
Values sent between devices are 32-bit elements; how exact they have to be, the bound alone decides.
No kernel may reach another device: no remote copies, remote signals or barrier semaphores. Data moves between devices by JAX's collectives and lax.ppermute only.
A program may use at most 64 MiB of HBM per device.

v0:
```python
import jax
import jax.numpy as jnp
from jax import lax
from jax.sharding import PartitionSpec as P
from jax.experimental import pallas as pl
from jax.experimental.pallas import tpu as pltpu

SUBSTEPS = 6


alk_ratio = 0.137


def face_pairs(velocity, mask_here, mask_next, diffusion):
    opened = mask_here * mask_next
    moving = velocity * opened
    mixing = diffusion[:, None, None] * opened
    return (mixing + jnp.maximum(moving, 0.0), jnp.minimum(moving, 0.0) - mixing)


def column_coefficients(vertical_mix, thickness, wet_cube):
    zero_layer = jnp.zeros((1,) + wet_cube.shape[1:], jnp.float32)
    opened = jnp.concatenate([wet_cube[:-1] * wet_cube[1:], zero_layer], 0)
    mixing = vertical_mix * opened
    mixing_above = jnp.concatenate([zero_layer, mixing[:-1]], 0)
    height = thickness[:, None, None]
    height_above = jnp.concatenate([thickness[:1], thickness[:-1]])[:, None, None]
    height_below = jnp.concatenate([thickness[1:], thickness[-1:]])[:, None, None]
    diagonal = 1.0 + (mixing + mixing_above) / height
    below_band = -mixing_above / height_above
    above_band = -mixing / height_below
    return (below_band, diagonal, above_band)


def solve_kernel(rhs_ref, below_ref, diagonal_ref, above_ref, out_ref, factor_ref):
    levels = diagonal_ref.shape[0]
    pivots = diagonal_ref[0]
    factor_ref[0] = above_ref[0] / pivots
    reduced = rhs_ref[:, 0] / pivots
    out_ref[:, 0] = reduced
    for level in range(1, levels):
        below = below_ref[level]
        pivots = diagonal_ref[level] - below * factor_ref[level - 1]
        factor_ref[level] = above_ref[level] / pivots
        reduced = (rhs_ref[:, level] - below * reduced) / pivots
        out_ref[:, level] = reduced
    solved = reduced
    for level in range(levels - 2, -1, -1):
        solved = out_ref[:, level] - factor_ref[level] * solved
        out_ref[:, level] = solved


def transposed_solve(right_side, below_band, diagonal, above_band):
    shape = right_side.shape
    rhs = right_side.reshape((-1,) + shape[-3:])
    out = pl.pallas_call(
        solve_kernel,
        out_shape=jax.ShapeDtypeStruct(rhs.shape, jnp.float32),
        scratch_shapes=[pltpu.VMEM(diagonal.shape, jnp.float32)],
    )(rhs, below_band, diagonal, above_band)
    return out.reshape(shape)


def carbonate_slopes(carbon, alkalinity):
    excess = 2.0 * carbon - alkalinity
    spread = alkalinity - carbon
    square = spread * spread
    return (
        (4.0 * excess * spread + excess * excess) / square,
        (-2.0 * excess * spread - excess * excess) / square,
    )


def scenario_sum(field):
    size = lax.axis_size("scen")
    index = lax.axis_index("scen")
    shape = field.shape
    rows = field.reshape(-1, shape[-1])
    bits = [b for b in (2, 4, 1) if b < size]
    bits += [b for b in (8, 16, 32) if b < size]
    kept_bits = []
    for bit in bits:
        half = rows.shape[0] // 2
        upper = (index // bit) % 2 == 1
        low, high = rows[:half], rows[half:]
        keep = jnp.where(upper, high, low)
        send = jnp.where(upper, low, high)
        pairs = [(i, i ^ bit) for i in range(size)]
        rows = keep + lax.ppermute(send, "scen", pairs)
        kept_bits.append((bit, upper))
    for bit, upper in kept_bits[::-1]:
        pairs = [(i, i ^ bit) for i in range(size)]
        other = lax.ppermute(rows, "scen", pairs)
        rows = jnp.where(
            upper,
            jnp.concatenate([other, rows], 0),
            jnp.concatenate([rows, other], 0),
        )
    return rows.reshape(shape)


def substep_kernel(adjoint_ref, east_a_ref, east_b_ref, north_a_ref, north_b_ref, out_ref):
    columns = adjoint_ref.shape[-2]
    lanes = adjoint_ref.shape[-1]
    east_a = east_a_ref[...]
    east_b_behind = pltpu.roll(east_b_ref[...], 1, 1)
    north_a = north_a_ref[...]
    north_b_behind = pltpu.roll(north_b_ref[...], 1, 2)
    for field in range(adjoint_ref.shape[0]):
        adjoint = adjoint_ref[field]
        for repeat in range(SUBSTEPS):
            ahead = pltpu.roll(adjoint, columns - 1, 1)
            behind = pltpu.roll(adjoint, 1, 1)
            north_ahead = pltpu.roll(adjoint, lanes - 1, 2)
            north_behind = pltpu.roll(adjoint, 1, 2)
            adjoint = (
                adjoint
                - east_a * (adjoint - ahead)
                - east_b_behind * (behind - adjoint)
                - (north_a * (adjoint - north_ahead) + north_b_behind * (north_behind - adjoint))
            )
        aligned = pltpu.roll(adjoint, columns - SUBSTEPS, 1)
        out_ref[field] = aligned[:, : out_ref.shape[-2]]


def transport_substeps(adjoint, east_a, east_b, north_a, north_b, width):
    fields, levels, columns, lanes = adjoint.shape
    chunk = 5 if levels % 5 == 0 else levels
    field_block = pl.BlockSpec((fields, chunk, columns, lanes), lambda j: (0, j, 0, 0))
    face_block = pl.BlockSpec((chunk, columns, lanes), lambda j: (j, 0, 0))
    return pl.pallas_call(
        substep_kernel,
        grid=(levels // chunk,),
        in_specs=[field_block, face_block, face_block, face_block, face_block],
        out_specs=pl.BlockSpec((fields, chunk, width, lanes), lambda j: (0, j, 0, 0)),
        out_shape=jax.ShapeDtypeStruct((fields, levels, width, lanes), jnp.float32),
    )(adjoint, east_a, east_b, north_a, north_b)


def padded_halo(pieces, width, halo, padded):
    size = lax.axis_size("grid")
    up = [(i, (i + 1) % size) for i in range(size)]
    down = [(j, i) for i, j in up]
    last = jnp.concatenate([piece[:, width - halo :] for piece in pieces], 0)
    initial = jnp.concatenate([piece[:, :halo] for piece in pieces], 0)
    before = lax.ppermute(last, "grid", up)
    after = lax.ppermute(initial, "grid", down)
    wide = []
    offset = 0
    for piece in pieces:
        rows = piece.shape[0]
        fill = jnp.zeros((rows, padded - width - 2 * halo, piece.shape[-1]), jnp.float32)
        wide.append(
            jnp.concatenate(
                [before[offset : offset + rows], piece, after[offset : offset + rows], fill], 1
            )
        )
        offset += rows
    return wide


def on_device(
    adjoint_in,
    surface_carbon,
    surface_alkalinity,
    east_velocity,
    north_velocity,
    east_diffusion,
    north_diffusion,
    vertical_mix,
    thickness,
    export_flux,
    piston,
    wet_mask,
    bottom_level,
):
    levels = vertical_mix.shape[0]
    width = east_velocity.shape[1]
    halo = SUBSTEPS
    padded = -(-(width + 2 * halo) // 8) * 8
    wet_bottom = jnp.where(wet_mask > 0, bottom_level, 0).astype(jnp.float32)
    wide_east, wide_north, wide_bottom = padded_halo(
        [east_velocity, north_velocity, wet_bottom[None]], width, halo, padded
    )
    depth_index = lax.broadcasted_iota(jnp.int32, (levels,) + wide_bottom.shape[1:], 0)
    wide_wet = (depth_index.astype(jnp.float32) < wide_bottom).astype(jnp.float32)
    wet_cube = (depth_index[:, :width] < wet_bottom[None]).astype(jnp.float32)

    below_band, diagonal, above_band = column_coefficients(vertical_mix, thickness, wet_cube)
    adjoint = transposed_solve(adjoint_in, below_band, diagonal, above_band)
    (adjoint,) = padded_halo(
        [adjoint.reshape((-1,) + adjoint.shape[-2:])], width, halo, padded
    )

    east_a, east_b = face_pairs(
        wide_east, wide_wet, jnp.roll(wide_wet, -1, axis=1), east_diffusion
    )
    zero_row = jnp.zeros(wide_wet.shape[:-1] + (1,), jnp.float32)
    north_next = jnp.concatenate([wide_wet[..., 1:], zero_row], -1)
    north_a, north_b = face_pairs(wide_north, wide_wet, north_next, north_diffusion)

    fields = adjoint_in.shape[0] * adjoint_in.shape[1]
    adjoint = transport_substeps(
        adjoint.reshape((fields, levels) + adjoint.shape[-2:]),
        east_a,
        east_b,
        north_a,
        north_b,
        width,
    ).reshape(adjoint_in.shape)
    rate_term = jnp.sum(adjoint[:, 0] - alk_ratio * adjoint[:, 1], axis=0)
    summed = scenario_sum(rate_term)
    rate_gradient = export_flux * wet_cube * summed
    slope_carbon, slope_alkalinity = carbonate_slopes(surface_carbon, surface_alkalinity)
    exchange_scale = wet_cube[0] * piston * adjoint[:, 0, 0]
    adjoint = (
        adjoint.at[:, 0, 0]
        .add(-exchange_scale * slope_carbon)
        .at[:, 1, 0]
        .add(-exchange_scale * slope_alkalinity)
    )
    return (adjoint, rate_gradient)


def solution(mesh):
    in_specs = (
        P("scen", None, None, "grid", None),
        P("scen", "grid", None),
        P("scen", "grid", None),
        P(None, "grid", None),
        P(None, "grid", None),
        P(),
        P(),
        P(None, "grid", None),
        P(),
        P(None, "grid", None),
        P("grid", None),
        P("grid", None),
        P("grid", None),
    )
    out_specs = (P("scen", None, None, "grid", None), P(None, "grid", None))
    return jax.shard_map(
        on_device, mesh=mesh, in_specs=in_specs, out_specs=out_specs, check_vma=False
    )
```

profile of v0, /device:TPU:8, one launch (start us, length us, event | category | flops | bytes accessed | tf_op | source)
XLA Modules:
  0.0 106.6 jit_solution(9570329839343118612)
XLA Ops:
  0.6 0.7 select_convert_fusion
  1.4 1.3 %fusion.11 = (f32[50,6,128]{2,1,0:T(8,128)S(1)}, f32[50,6,128]{2,1,0:T(8,128)S(1)}, f32[50,6,128]{2,1,0:T(8,128)S(1)}, f32[50,6,128]{2,1,0:T(8,128)S(1)}) fusion(f32[50,16,128]{2,1,0:T(8,128)} %param.20, f32[50,16,128]{2,1,0:T(8,128)} %param.21), kind=kLoop, calls=%fused_computation.51 | loop fusion | bytes 1228800 | tf_op jit(solution)/shard_map/slice | solution.py:144
  2.7 0.8 pad_maximum_fusion
  3.5 0.8 pad_maximum_fusion.1
  4.3 6.3 %collective-permute-start.3 = (f32[101,6,128]{2,1,0:T(8,128)}, f32[101,6,128]{2,1,0:T(8,128)}, u32[]{:S(2)}, u32[]{:S(2)}) collective-permute-start(f32[101,6,128]{2,1,0:T(8,128)} %pad_maximum_fusion.1), channel_id=1, source_target_pairs={{1,0},{2,1},{3,2},{4,3},{5,4},{6,5},{7,6},{8,7},{9,8},{10,9},{11,1... | collective-permute-start | bytes 930824 | tf_op jit(solution)/shard_map/ppermute | solution.py:147
  10.6 0.6 fusion.14
  11.2 0.1 compare_convert_fusion.1
  11.4 1.4 %pad_maximum_fusion.2 = (f32[50]{0:T(128)S(1)}, f32[50]{0:T(128)S(1)}) fusion(f32[49]{0:T(128)S(1)} %get-tuple-element.50, f32[1]{0:T(128)} %get-tuple-element.48, f32[1]{0:T(128)} %get-tuple-element.49, f32[49]{0:T(128)S(1)} %get-tuple-element.51), kind=kLoop, calls=%fused_computation.45 | loop fusion | flops 100 | bytes 800 | tf_op jit(solution)/shard_map/concatenate | solution.py:27
  12.8 0.9 negate_divide_fusion
  13.7 1.1 divide_add_fusion
  14.7 3.5 %shard_map.140 = f32[4,50,16,128]{3,2,1,0:T(8,128)} custom-call(f32[4,50,16,128]{3,2,1,0:T(8,128)} %bitcast.45, f32[50,16,128]{2,1,0:T(8,128)} %get-tuple-element.45.below_ref, f32[50,16,128]{2,1,0:T(8,128)} %get-tuple-element.44.diagonal_ref, f32[50,16,128]{2,1,0:T(8,128)} %get-tuple-element.26.above_ref), custom_call_target="tpu_custom_call" | custom-call | tf_op jit(solution)/shard_map/pallas_call | solution.py:56
  18.2 1.5 %fusion.8 = (f32[200,6,128]{2,1,0:T(8,128)S(1)}, f32[200,6,128]{2,1,0:T(8,128)S(1)}) fusion(f32[200,16,128]{2,1,0:T(8,128)} %bitcast.42), kind=kLoop, calls=%fused_computation.48 | loop fusion | bytes 2457600 | tf_op jit(solution)/shard_map/slice | solution.py:144
  19.7 0.1 copy.23
  19.8 0.1 collective-permute-start
  19.9 0.1 copy.24
  20.1 5.7 %collective-permute-start.1 = (f32[200,6,128]{2,0,1:T(8,128)S(1)}, f32[200,6,128]{2,0,1:T(8,128)S(1)}, u32[]{:S(2)}, u32[]{:S(2)}) collective-permute-start(f32[200,6,128]{2,0,1:T(8,128)S(1)} %copy.24), channel_id=1, source_target_pairs={{1,0},{2,1},{3,2},{4,3},{5,4},{6,5},{7,6},{8,7},{9,8},{10,9},{11,1... | collective-permute-start | bytes 1843208 | tf_op jit(solution)/shard_map/ppermute | solution.py:147
  25.8 0.1 pad.46.clone
  25.8 0.7 slice.219
  26.5 0.7 slice.221
  27.2 0.1 maximum_bitcast_fusion
  27.3 0.1 compare_convert_fusion
  27.4 1.1 fusion.9
  28.5 1.1 fusion.10
  29.6 0.1 slice.222
  29.7 0.3 slice.226
  30.0 0.6 copy-done.3
  30.5 1.8 %minimum_subtract_fusion = (f32[50,32,128]{2,1,0:T(8,128)}, f32[50,32,128]{2,1,0:T(8,128)}) fusion(f32[50,32,127]{2,1,0:T(8,128)S(1)} %slice.226, f32[50,6,128]{2,1,0:T(8,128)S(1)} %get-tuple-element.36, f32[50,16,128]{2,1,0:T(8,128)S(1)} %copy-done.3, f32[50,6,128]{2,1,0:T(8,128)S(1)} %get-tuple-element.34, f32[32]{0:T(128)S(1)} %pad.46.clone, ...), kind=kLoop, calls=%fused_computation.9 | loop fusion | flops 2252800 | bytes 3184912 | tf_op jit(solution)/shard_map/sub | solution.py:18
  32.3 1.8 %minimum_subtract_fusion.1 = (f32[50,32,128]{2,1,0:T(8,128)}, f32[50,32,128]{2,1,0:T(8,128)}) fusion(f32[32]{0:T(128)S(1)} %pad.46.clone, f32[50,6,128]{2,1,0:T(8,128)S(1)} %get-tuple-element.37, f32[50,16,128]{2,1,0:T(8,128)S(1)} %copy-done.4, f32[50,6,128]{2,1,0:T(8,128)S(1)} %get-tuple-element.35, f32[50,1,128]{2,1,0:T(1,128)S(1)} %slice.223, ...), kind=kLoop, calls=%fused_computation.11 | loop fusion | flops 2457600 | bytes 3191312 | tf_op jit(solution)/shard_map/sub | solution.py:18
  34.1 4.8 %collective-permute-done = f32[200,6,128]{2,0,1:T(8,128)S(1)} collective-permute-done((f32[200,6,128]{2,0,1:T(8,128)S(1)}, f32[200,6,128]{2,0,1:T(8,128)S(1)}, u32[]{:S(2)}, u32[]{:S(2)}) %collective-permute-start) | collective-permute-done | bytes 614432 | tf_op jit(solution)/shard_map/ppermute | solution.py:146
  38.9 0.2 copy.18
  39.0 0.2 copy.20
  39.2 2.3 %maximum_maximum_fusion.adjoint_ref = f32[4,50,32,128]{3,2,1,0:T(8,128)} fusion(f32[4,50,6,128]{3,2,1,0:T(8,128)S(1)} %bitcast.44, f32[4,50,16,128]{3,2,1,0:T(8,128)S(1)} %copy-done.1, f32[4,50,6,128]{3,2,1,0:T(8,128)S(1)} %bitcast.43, f32[32]{0:T(128)S(1)} %pad.46.clone), kind=kLoop, calls=%fused_computation | loop fusion | flops 2457600 | bytes 6144128 | tf_op jit(solution)/shard_map/concatenate | solution.py:154
  41.5 21.8 %shard_map.141 = f32[4,50,16,128]{3,2,1,0:T(8,128)} custom-call(f32[4,50,32,128]{3,2,1,0:T(8,128)} %maximum_maximum_fusion.adjoint_ref, f32[50,32,128]{2,1,0:T(8,128)} %get-tuple-element.29.east_a_ref, f32[50,32,128]{2,1,0:T(8,128)} %get-tuple-element.28.east_b_ref, f32[50,32,128]{2,1,0:T(8,128)} %get-tuple-element.31.north_a_ref, ...), custom_call_target="tpu_custom_call" | custom-call | tf_op jit(solution)/shard_map/pallas_call | solution.py:131
  63.4 1.6 %fusion.1 = f32[50,16,128]{2,1,0:T(8,128)S(1)} fusion(f32[2,2,50,16,128]{4,3,2,1,0:T(8,128)} %bitcast.37), kind=kLoop, calls=%fused_computation.6 | loop fusion | flops 512000 | bytes 2048000 | tf_op jit(solution)/shard_map/reduce_sum | solution.py:211
  65.0 0.5 collective-permute-start.4
  65.5 5.3 %collective-permute-done.4 = f32[400,128]{1,0:T(8,128)S(1)} collective-permute-done((f32[400,128]{1,0:T(8,128)S(1)}, f32[400,128]{1,0:T(8,128)S(1)}, u32[]{:S(2)}, u32[]{:S(2)}) %collective-permute-start.4) | collective-permute-done | bytes 204832 | tf_op jit(solution)/shard_map/ppermute | solution.py:89
  70.9 2.4 %collective-permute-start.5 = (f32[200,128]{1,0:T(8,128)S(1)}, f32[200,128]{1,0:T(8,128)S(1)}, u32[]{:S(2)}, u32[]{:S(2)}) collective-permute-start(f32[200,128]{1,0:T(8,128)S(1)} %slice_select_fusion.2), channel_id=1, source_target_pairs={{0,128},{32,160},{64,192},{96,224},{128,0},{160,32},{192,64},{224,... | collective-permute-start | bytes 307208 | tf_op jit(solution)/shard_map/ppermute | solution.py:89
  73.3 3.9 %collective-permute-done.5 = f32[200,128]{1,0:T(8,128)S(1)} collective-permute-done((f32[200,128]{1,0:T(8,128)S(1)}, f32[200,128]{1,0:T(8,128)S(1)}, u32[]{:S(2)}, u32[]{:S(2)}) %collective-permute-start.5) | collective-permute-done | bytes 102432 | tf_op jit(solution)/shard_map/ppermute | solution.py:89
  77.2 4.6 %collective-permute-start.6 = (f32[100,128]{1,0:T(8,128)S(1)}, f32[100,128]{1,0:T(8,128)S(1)}, u32[]{:S(2)}, u32[]{:S(2)}) collective-permute-start(f32[100,128]{1,0:T(8,128)S(1)} %slice_select_fusion.3), channel_id=1, source_target_pairs={{0,32},{32,0},{64,96},{96,64},{128,160},{160,128},{192,224},{224,1... | collective-permute-start | bytes 153608 | tf_op jit(solution)/shard_map/ppermute | solution.py:89
  81.8 3.6 %collective-permute-done.6 = f32[100,128]{1,0:T(8,128)S(1)} collective-permute-done((f32[100,128]{1,0:T(8,128)S(1)}, f32[100,128]{1,0:T(8,128)S(1)}, u32[]{:S(2)}, u32[]{:S(2)}) %collective-permute-start.6) | collective-permute-done | bytes 51232 | tf_op jit(solution)/shard_map/ppermute | solution.py:89
  85.4 5.2 %collective-permute-start.7 = (f32[100,128]{1,0:T(8,128)S(1)}, f32[100,128]{1,0:T(8,128)S(1)}, u32[]{:S(2)}, u32[]{:S(2)}) collective-permute-start(f32[100,128]{1,0:T(8,128)S(1)} %select_add_fusion.1), channel_id=1, source_target_pairs={{0,32},{32,0},{64,96},{96,64},{128,160},{160,128},{192,224},{224,1... | collective-permute-start | bytes 153608 | tf_op jit(solution)/shard_map/ppermute | solution.py:93
  90.7 0.1 copy.26
  90.8 2.7 %collective-permute-done.7 = f32[100,128]{1,0:T(8,128)S(1)} collective-permute-done((f32[100,128]{1,0:T(8,128)S(1)}, f32[100,128]{1,0:T(8,128)S(1)}, u32[]{:S(2)}, u32[]{:S(2)}) %collective-permute-start.7) | collective-permute-done | bytes 51232 | tf_op jit(solution)/shard_map/ppermute | solution.py:93
  93.6 2.4 %collective-permute-start.8 = (f32[200,128]{1,0:T(8,128)S(1)}, f32[200,128]{1,0:T(8,128)S(1)}, u32[]{:S(2)}, u32[]{:S(2)}) collective-permute-start(f32[200,128]{1,0:T(8,128)S(1)} %maximum_select_fusion.2), channel_id=1, source_target_pairs={{0,128},{32,160},{64,192},{96,224},{128,0},{160,32},{192,64},{224,... | collective-permute-start | bytes 307208 | tf_op jit(solution)/shard_map/ppermute | solution.py:93
  96.0 3.8 %collective-permute-done.8 = f32[200,128]{1,0:T(8,128)S(1)} collective-permute-done((f32[200,128]{1,0:T(8,128)S(1)}, f32[200,128]{1,0:T(8,128)S(1)}, u32[]{:S(2)}, u32[]{:S(2)}) %collective-permute-start.8) | collective-permute-done | bytes 102432 | tf_op jit(solution)/shard_map/ppermute | solution.py:93
  99.8 0.5 collective-permute-start.9
  100.4 5.3 %collective-permute-done.9 = f32[400,128]{1,0:T(8,128)S(1)} collective-permute-done((f32[400,128]{1,0:T(8,128)S(1)}, f32[400,128]{1,0:T(8,128)S(1)}, u32[]{:S(2)}, u32[]{:S(2)}) %collective-permute-start.9) | collective-permute-done | bytes 204832 | tf_op jit(solution)/shard_map/ppermute | solution.py:93
  105.7 0.9 fusion.2
  (50 shorter events, 0.5 us)
Async XLA Ops:
  1.4 9.2 %copy-start.9 = (f32[50]{0:T(128)S(1)}, f32[50]{0:T(128)}, u32[]{:S(2)}) copy-start(f32[50]{0:T(128)} %param.25) | copy-start | bytes 604
  2.7 10.1 %copy-start.5 = (f32[50,16,128]{2,1,0:T(8,128)S(1)}, f32[50,16,128]{2,1,0:T(8,128)}, u32[]{:S(2)}) copy-start(f32[50,16,128]{2,1,0:T(8,128)} %param.24) | copy-start | bytes 1228804
  3.5 22.3 %collective-permute-start.2 = (f32[101,6,128]{2,1,0:T(8,128)}, f32[101,6,128]{2,1,0:T(8,128)}, u32[]{:S(2)}, u32[]{:S(2)}) collective-permute-start(f32[101,6,128]{2,1,0:T(8,128)} %pad_maximum_fusion), channel_id=1, source_target_pairs={{0,1},{1,2},{2,3},{3,4},{4,5},{5,6},{6,7},{7,8},{8,9},{9,10},{10,1... | collective-permute-start | bytes 930824 | tf_op jit(solution)/shard_map/ppermute | solution.py:146
  4.3 22.2 %collective-permute-start.3 = (f32[101,6,128]{2,1,0:T(8,128)}, f32[101,6,128]{2,1,0:T(8,128)}, u32[]{:S(2)}, u32[]{:S(2)}) collective-permute-start(f32[101,6,128]{2,1,0:T(8,128)} %pad_maximum_fusion.1), channel_id=1, source_target_pairs={{1,0},{2,1},{3,2},{4,3},{5,4},{6,5},{7,6},{8,7},{9,8},{10,9},{11,1... | collective-permute-start | bytes 930824 | tf_op jit(solution)/shard_map/ppermute | solution.py:147
  19.8 19.0 %collective-permute-start = (f32[200,6,128]{2,0,1:T(8,128)S(1)}, f32[200,6,128]{2,0,1:T(8,128)S(1)}, u32[]{:S(2)}, u32[]{:S(2)}) collective-permute-start(f32[200,6,128]{2,0,1:T(8,128)S(1)} %copy.23), channel_id=1, source_target_pairs={{0,1},{1,2},{2,3},{3,4},{4,5},{5,6},{6,7},{7,8},{8,9},{9,10},{10,1... | collective-permute-start | bytes 1843208 | tf_op jit(solution)/shard_map/ppermute | solution.py:146
  20.1 19.0 %collective-permute-start.1 = (f32[200,6,128]{2,0,1:T(8,128)S(1)}, f32[200,6,128]{2,0,1:T(8,128)S(1)}, u32[]{:S(2)}, u32[]{:S(2)}) collective-permute-start(f32[200,6,128]{2,0,1:T(8,128)S(1)} %copy.24), channel_id=1, source_target_pairs={{1,0},{2,1},{3,2},{4,3},{5,4},{6,5},{7,6},{8,7},{9,8},{10,9},{11,1... | collective-permute-start | bytes 1843208 | tf_op jit(solution)/shard_map/ppermute | solution.py:147
  29.5 1.0 copy-start.3
  29.5 1.0 copy-start.11
  30.5 1.8 %copy-start.4 = (f32[50,16,128]{2,1,0:T(8,128)S(1)}, f32[50,16,128]{2,1,0:T(8,128)}, u32[]{:S(2)}) copy-start(f32[50,16,128]{2,1,0:T(8,128)} %param.20) | copy-start | bytes 1228804
  30.5 1.8 %copy-start.12 = (f32[50]{0:T(128)S(1)}, f32[50]{0:T(128)}, u32[]{:S(2)}) copy-start(f32[50]{0:T(128)} %param.22) | copy-start | bytes 604
  34.1 5.1 %copy-start.1 = (f32[4,50,16,128]{3,2,1,0:T(8,128)S(1)}, f32[4,50,16,128]{3,2,1,0:T(8,128)}, u32[]{:S(2)}) copy-start(f32[4,50,16,128]{3,2,1,0:T(8,128)} %shard_map.140) | copy-start | bytes 4915204
  64.9 16.8 %copy-start.10 = (f32[16,128]{1,0:T(8,128)S(1)}, f32[16,128]{1,0:T(8,128)}, u32[]{:S(2)}) copy-start(f32[16,128]{1,0:T(8,128)} %param.27) | copy-start | bytes 24580
  64.9 25.7 %copy-start = (f32[4,50,16,128]{3,2,1,0:T(8,128)S(1)}, f32[4,50,16,128]{3,2,1,0:T(8,128)}, u32[]{:S(2)}) copy-start(f32[4,50,16,128]{3,2,1,0:T(8,128)} %shard_map.141) | copy-start | bytes 4915204
  65.0 5.8 %collective-permute-start.4 = (f32[400,128]{1,0:T(8,128)S(1)}, f32[400,128]{1,0:T(8,128)S(1)}, u32[]{:S(2)}, u32[]{:S(2)}) collective-permute-start(f32[400,128]{1,0:T(8,128)S(1)} %bitcast.49), channel_id=1, source_target_pairs={{0,64},{32,96},{64,0},{96,32},{128,192},{160,224},{192,128},{224,1... | collective-permute-start | bytes 614408 | tf_op jit(solution)/shard_map/ppermute | solution.py:89
  70.9 6.3 %collective-permute-start.5 = (f32[200,128]{1,0:T(8,128)S(1)}, f32[200,128]{1,0:T(8,128)S(1)}, u32[]{:S(2)}, u32[]{:S(2)}) collective-permute-start(f32[200,128]{1,0:T(8,128)S(1)} %slice_select_fusion.2), channel_id=1, source_target_pairs={{0,128},{32,160},{64,192},{96,224},{128,0},{160,32},{192,64},{224,... | collective-permute-start | bytes 307208 | tf_op jit(solution)/shard_map/ppermute | solution.py:89
  77.2 8.2 %collective-permute-start.6 = (f32[100,128]{1,0:T(8,128)S(1)}, f32[100,128]{1,0:T(8,128)S(1)}, u32[]{:S(2)}, u32[]{:S(2)}) collective-permute-start(f32[100,128]{1,0:T(8,128)S(1)} %slice_select_fusion.3), channel_id=1, source_target_pairs={{0,32},{32,0},{64,96},{96,64},{128,160},{160,128},{192,224},{224,1... | collective-permute-start | bytes 153608 | tf_op jit(solution)/shard_map/ppermute | solution.py:89
  85.4 8.1 %collective-permute-start.7 = (f32[100,128]{1,0:T(8,128)S(1)}, f32[100,128]{1,0:T(8,128)S(1)}, u32[]{:S(2)}, u32[]{:S(2)}) collective-permute-start(f32[100,128]{1,0:T(8,128)S(1)} %select_add_fusion.1), channel_id=1, source_target_pairs={{0,32},{32,0},{64,96},{96,64},{128,160},{160,128},{192,224},{224,1... | collective-permute-start | bytes 153608 | tf_op jit(solution)/shard_map/ppermute | solution.py:93
  90.7 5.3 %copy-start.7 = (f32[2,16,128]{2,1,0:T(8,128)S(1)}, f32[2,16,128]{2,1,0:T(8,128)}, u32[]{:S(2)}) copy-start(f32[2,16,128]{2,1,0:T(8,128)} %param.19) | copy-start | bytes 49156
  90.7 5.3 %copy-start.8 = (f32[2,16,128]{2,1,0:T(8,128)S(1)}, f32[2,16,128]{2,1,0:T(8,128)}, u32[]{:S(2)}) copy-start(f32[2,16,128]{2,1,0:T(8,128)} %param.18) | copy-start | bytes 49156
  90.8 14.9 %copy-start.6 = (f32[50,16,128]{2,1,0:T(8,128)S(1)}, f32[50,16,128]{2,1,0:T(8,128)}, u32[]{:S(2)}) copy-start(f32[50,16,128]{2,1,0:T(8,128)} %param.26) | copy-start | bytes 1228804
  93.6 6.3 %collective-permute-start.8 = (f32[200,128]{1,0:T(8,128)S(1)}, f32[200,128]{1,0:T(8,128)S(1)}, u32[]{:S(2)}, u32[]{:S(2)}) collective-permute-start(f32[200,128]{1,0:T(8,128)S(1)} %maximum_select_fusion.2), channel_id=1, source_target_pairs={{0,128},{32,160},{64,192},{96,224},{128,0},{160,32},{192,64},{224,... | collective-permute-start | bytes 307208 | tf_op jit(solution)/shard_map/ppermute | solution.py:93
  99.8 5.8 %collective-permute-start.9 = (f32[400,128]{1,0:T(8,128)S(1)}, f32[400,128]{1,0:T(8,128)S(1)}, u32[]{:S(2)}, u32[]{:S(2)}) collective-permute-start(f32[400,128]{1,0:T(8,128)S(1)} %maximum_select_fusion.1), channel_id=1, source_target_pairs={{0,64},{32,96},{64,0},{96,32},{128,192},{160,224},{192,128},{224,1... | collective-permute-start | bytes 614408 | tf_op jit(solution)/shard_map/ppermute | solution.py:93
  100.4 6.2 %copy-start.2 = (f32[2,2,50,16,128]{4,3,2,1,0:T(8,128)}, f32[2,2,50,16,128]{4,3,2,1,0:T(8,128)S(1)}, u32[]{:S(2)}) copy-start(f32[2,2,50,16,128]{4,3,2,1,0:T(8,128)S(1)} %fusion.3) | copy-start | bytes 4915204
where the time goes:
time: 107 us
  waiting for transfers between devices  29.5 us (28%)
  starting transfers between devices  27.7 us (26%)
  Pallas kernels  25.3 us (24%)
  other arithmetic  14.5 us (14%)
  local copies, waits for them, and re-layouts  8.75 us (8%)
    pallas_call x1, Pallas kernels, transport_substeps(): pl.pallas_call(substep_kernel, grid=(levels // chunk,), in_specs=[field_b...  21.8 us
    ppermute x3, waiting for transfers between devices, scenario_sum(): rows = keep + lax.ppermute(send, 'scen', pairs)  12.8 us
    ppermute x2, starting transfers between devices, padded_halo(): after = lax.ppermute(initial, 'grid', down)  12 us
    ppermute x3, waiting for transfers between devices, scenario_sum(): other = lax.ppermute(rows, 'scen', pairs)  11.8 us
    ppermute x3, starting transfers between devices, scenario_sum(): other = lax.ppermute(rows, 'scen', pairs)  8.14 us
    ppermute x3, starting transfers between devices, scenario_sum(): rows = keep + lax.ppermute(send, 'scen', pairs)  7.5 us
    ppermute x2, waiting for transfers between devices, padded_halo(): before = lax.ppermute(last, 'grid', up)  4.78 us
    sub x2, other arithmetic, face_pairs(): jnp.minimum(moving, 0.0) - mixing  3.53 us
  transfers between devices with their start and end apart: 10, of which 7 were waited for; matrix products, arithmetic and copies ran while one was open for 14% of the time, Pallas kernels for 3%

commit v1 on v0

--- a/solution.py
+++ b/solution.py
@@ -102,25 +102,30 @@
 def substep_kernel(adjoint_ref, east_a_ref, east_b_ref, north_a_ref, north_b_ref, out_ref):
     columns = adjoint_ref.shape[-2]
     lanes = adjoint_ref.shape[-1]
-    east_a = east_a_ref[...]
-    east_b_behind = pltpu.roll(east_b_ref[...], 1, 1)
-    north_a = north_a_ref[...]
-    north_b_behind = pltpu.roll(north_b_ref[...], 1, 2)
-    for field in range(adjoint_ref.shape[0]):
-        adjoint = adjoint_ref[field]
-        for repeat in range(SUBSTEPS):
-            ahead = pltpu.roll(adjoint, columns - 1, 1)
-            behind = pltpu.roll(adjoint, 1, 1)
-            north_ahead = pltpu.roll(adjoint, lanes - 1, 2)
-            north_behind = pltpu.roll(adjoint, 1, 2)
-            adjoint = (
-                adjoint
-                - east_a * (adjoint - ahead)
-                - east_b_behind * (behind - adjoint)
-                - (north_a * (adjoint - north_ahead) + north_b_behind * (north_behind - adjoint))
-            )
-        aligned = pltpu.roll(adjoint, columns - SUBSTEPS, 1)
-        out_ref[field] = aligned[:, : out_ref.shape[-2]]
+
+    def one_level(level, carry):
+        east_a = east_a_ref[level]
+        east_b_behind = pltpu.roll(east_b_ref[level], 1, 0)
+        north_a = north_a_ref[level]
+        north_b_behind = pltpu.roll(north_b_ref[level], 1, 1)
+        for field in range(adjoint_ref.shape[0]):
+            adjoint = adjoint_ref[field, level]
+            for repeat in range(SUBSTEPS):
+                ahead = pltpu.roll(adjoint, columns - 1, 0)
+                behind = pltpu.roll(adjoint, 1, 0)
+                north_ahead = pltpu.roll(adjoint, lanes - 1, 1)
+                north_behind = pltpu.roll(adjoint, 1, 1)
+                adjoint = (
+                    adjoint
+                    - east_a * (adjoint - ahead)
+                    - east_b_behind * (behind - adjoint)
+                    - (north_a * (adjoint - north_ahead) + north_b_behind * (north_behind - adjoint))
+                )
+            aligned = pltpu.roll(adjoint, columns - SUBSTEPS, 0)
+            out_ref[field, level] = aligned[: out_ref.shape[-2]]
+        return carry
+
+    lax.fori_loop(0, adjoint_ref.shape[1], one_level, 0)
 
 
 def transport_substeps(adjoint, east_a, east_b, north_a, north_b, width):

time: 107 us -> 112 us (1.047)
  Pallas kernels: 25.3 us -> 30.3 us
    pallas_call x1, Pallas kernels: 21.8 us -> 26.8 us  [transport_substeps(): pl.pallas_call(substep_kernel, grid=(levels // chunk,), in_specs=[field_b...]
  transfers between devices with their start and end apart: 10 -> 10, of which waited for: 7 -> 7; matrix products, arithmetic and copies ran while one was open for 14% -> 13% of each run, Pallas kernels for 3% -> 3%
where the time goes in v1:
time: 112 us
  Pallas kernels  30.3 us (27%)
  waiting for transfers between devices  29.5 us (26%)
  starting transfers between devices  27.7 us (25%)
  other arithmetic  14.5 us (13%)
  local copies, waits for them, and re-layouts  8.75 us (8%)
    pallas_call x1, Pallas kernels, transport_substeps(): pl.pallas_call(substep_kernel, grid=(levels // chunk,), in_specs=[field_b...  26.8 us
    ppermute x3, waiting for transfers between devices, scenario_sum(): rows = keep + lax.ppermute(send, 'scen', pairs)  12.8 us
    ppermute x2, starting transfers between devices, padded_halo(): after = lax.ppermute(initial, 'grid', down)  12 us
    ppermute x3, waiting for transfers between devices, scenario_sum(): other = lax.ppermute(rows, 'scen', pairs)  11.8 us
    ppermute x3, starting transfers between devices, scenario_sum(): other = lax.ppermute(rows, 'scen', pairs)  8.14 us
    ppermute x3, starting transfers between devices, scenario_sum(): rows = keep + lax.ppermute(send, 'scen', pairs)  7.5 us
    ppermute x2, waiting for transfers between devices, padded_halo(): before = lax.ppermute(last, 'grid', up)  4.78 us
    sub x2, other arithmetic, face_pairs(): jnp.minimum(moving, 0.0) - mixing  3.53 us
  transfers between devices with their start and end apart: 10, of which 7 were waited for; matrix products, arithmetic and copies ran while one was open for 13% of the time, Pallas kernels for 3%

profile of v1, /device:TPU:8, one launch (start us, length us, event | category | flops | bytes accessed | tf_op | source)
XLA Modules:
  0.0 111.6 jit_solution(7884155259139715113)
XLA Ops:
  0.6 0.7 select_convert_fusion
  1.4 1.3 %fusion.11 = (f32[50,6,128]{2,1,0:T(8,128)S(1)}, f32[50,6,128]{2,1,0:T(8,128)S(1)}, f32[50,6,128]{2,1,0:T(8,128)S(1)}, f32[50,6,128]{2,1,0:T(8,128)S(1)}) fusion(f32[50,16,128]{2,1,0:T(8,128)} %param.20, f32[50,16,128]{2,1,0:T(8,128)} %param.21), kind=kLoop, calls=%fused_computation.51 | loop fusion | bytes 1228800 | tf_op jit(solution)/shard_map/slice | solution.py:149
  2.7 0.8 pad_maximum_fusion
  3.5 0.8 pad_maximum_fusion.1
  4.3 6.3 %collective-permute-start.3 = (f32[101,6,128]{2,1,0:T(8,128)}, f32[101,6,128]{2,1,0:T(8,128)}, u32[]{:S(2)}, u32[]{:S(2)}) collective-permute-start(f32[101,6,128]{2,1,0:T(8,128)} %pad_maximum_fusion.1), channel_id=1, source_target_pairs={{1,0},{2,1},{3,2},{4,3},{5,4},{6,5},{7,6},{8,7},{9,8},{10,9},{11,1... | collective-permute-start | bytes 930824 | tf_op jit(solution)/shard_map/ppermute | solution.py:152
  10.6 0.6 fusion.14
  11.2 0.1 compare_convert_fusion.1
  11.4 1.4 %pad_maximum_fusion.2 = (f32[50]{0:T(128)S(1)}, f32[50]{0:T(128)S(1)}) fusion(f32[49]{0:T(128)S(1)} %get-tuple-element.50, f32[1]{0:T(128)} %get-tuple-element.48, f32[1]{0:T(128)} %get-tuple-element.49, f32[49]{0:T(128)S(1)} %get-tuple-element.51), kind=kLoop, calls=%fused_computation.45 | loop fusion | flops 100 | bytes 800 | tf_op jit(solution)/shard_map/concatenate | solution.py:27
  12.8 0.9 negate_divide_fusion
  13.7 1.1 divide_add_fusion
  14.7 3.5 %shard_map.140 = f32[4,50,16,128]{3,2,1,0:T(8,128)} custom-call(f32[4,50,16,128]{3,2,1,0:T(8,128)} %bitcast.45, f32[50,16,128]{2,1,0:T(8,128)} %get-tuple-element.45.below_ref, f32[50,16,128]{2,1,0:T(8,128)} %get-tuple-element.44.diagonal_ref, f32[50,16,128]{2,1,0:T(8,128)} %get-tuple-element.26.above_ref), custom_call_target="tpu_custom_call" | custom-call | tf_op jit(solution)/shard_map/pallas_call | solution.py:56
  18.2 1.5 %fusion.8 = (f32[200,6,128]{2,1,0:T(8,128)S(1)}, f32[200,6,128]{2,1,0:T(8,128)S(1)}) fusion(f32[200,16,128]{2,1,0:T(8,128)} %bitcast.42), kind=kLoop, calls=%fused_computation.48 | loop fusion | bytes 2457600 | tf_op jit(solution)/shard_map/slice | solution.py:149
  19.7 0.1 copy.23
  19.8 0.1 collective-permute-start
  19.9 0.1 copy.24
  20.1 5.7 %collective-permute-start.1 = (f32[200,6,128]{2,0,1:T(8,128)S(1)}, f32[200,6,128]{2,0,1:T(8,128)S(1)}, u32[]{:S(2)}, u32[]{:S(2)}) collective-permute-start(f32[200,6,128]{2,0,1:T(8,128)S(1)} %copy.24), channel_id=1, source_target_pairs={{1,0},{2,1},{3,2},{4,3},{5,4},{6,5},{7,6},{8,7},{9,8},{10,9},{11,1... | collective-permute-start | bytes 1843208 | tf_op jit(solution)/shard_map/ppermute | solution.py:152
  25.8 0.1 pad.46.clone
  25.8 0.7 slice.219
  26.5 0.7 slice.221
  27.2 0.1 maximum_bitcast_fusion
  27.3 0.1 compare_convert_fusion
  27.4 1.1 fusion.9
  28.5 1.1 fusion.10
  29.6 0.1 slice.222
  29.7 0.3 slice.226
  30.0 0.6 copy-done.3
  30.5 1.8 %minimum_subtract_fusion = (f32[50,32,128]{2,1,0:T(8,128)}, f32[50,32,128]{2,1,0:T(8,128)}) fusion(f32[50,32,127]{2,1,0:T(8,128)S(1)} %slice.226, f32[50,6,128]{2,1,0:T(8,128)S(1)} %get-tuple-element.36, f32[50,16,128]{2,1,0:T(8,128)S(1)} %copy-done.3, f32[50,6,128]{2,1,0:T(8,128)S(1)} %get-tuple-element.34, f32[32]{0:T(128)S(1)} %pad.46.clone, ...), kind=kLoop, calls=%fused_computation.9 | loop fusion | flops 2252800 | bytes 3184912 | tf_op jit(solution)/shard_map/sub | solution.py:18
  32.3 1.8 %minimum_subtract_fusion.1 = (f32[50,32,128]{2,1,0:T(8,128)}, f32[50,32,128]{2,1,0:T(8,128)}) fusion(f32[32]{0:T(128)S(1)} %pad.46.clone, f32[50,6,128]{2,1,0:T(8,128)S(1)} %get-tuple-element.37, f32[50,16,128]{2,1,0:T(8,128)S(1)} %copy-done.4, f32[50,6,128]{2,1,0:T(8,128)S(1)} %get-tuple-element.35, f32[50,1,128]{2,1,0:T(1,128)S(1)} %slice.223, ...), kind=kLoop, calls=%fused_computation.11 | loop fusion | flops 2457600 | bytes 3191312 | tf_op jit(solution)/shard_map/sub | solution.py:18
  34.1 4.8 %collective-permute-done = f32[200,6,128]{2,0,1:T(8,128)S(1)} collective-permute-done((f32[200,6,128]{2,0,1:T(8,128)S(1)}, f32[200,6,128]{2,0,1:T(8,128)S(1)}, u32[]{:S(2)}, u32[]{:S(2)}) %collective-permute-start) | collective-permute-done | bytes 614432 | tf_op jit(solution)/shard_map/ppermute | solution.py:151
  38.9 0.2 copy.18
  39.0 0.2 copy.20
  39.2 2.3 %maximum_maximum_fusion.adjoint_ref = f32[4,50,32,128]{3,2,1,0:T(8,128)} fusion(f32[4,50,6,128]{3,2,1,0:T(8,128)S(1)} %bitcast.44, f32[4,50,16,128]{3,2,1,0:T(8,128)S(1)} %copy-done.1, f32[4,50,6,128]{3,2,1,0:T(8,128)S(1)} %bitcast.43, f32[32]{0:T(128)S(1)} %pad.46.clone), kind=kLoop, calls=%fused_computation | loop fusion | flops 2457600 | bytes 6144128 | tf_op jit(solution)/shard_map/concatenate | solution.py:159
  41.5 26.8 %shard_map.141 = f32[4,50,16,128]{3,2,1,0:T(8,128)} custom-call(f32[4,50,32,128]{3,2,1,0:T(8,128)} %maximum_maximum_fusion.adjoint_ref, f32[50,32,128]{2,1,0:T(8,128)} %get-tuple-element.29.east_a_ref, f32[50,32,128]{2,1,0:T(8,128)} %get-tuple-element.28.east_b_ref, f32[50,32,128]{2,1,0:T(8,128)} %get-tuple-element.31.north_a_ref, ...), custom_call_target="tpu_custom_call" | custom-call | tf_op jit(solution)/shard_map/pallas_call | solution.py:136
  68.3 1.6 %fusion.1 = f32[50,16,128]{2,1,0:T(8,128)S(1)} fusion(f32[2,2,50,16,128]{4,3,2,1,0:T(8,128)} %bitcast.37), kind=kLoop, calls=%fused_computation.6 | loop fusion | flops 512000 | bytes 2048000 | tf_op jit(solution)/shard_map/reduce_sum | solution.py:216
  70.0 0.5 collective-permute-start.4
  70.5 5.3 %collective-permute-done.4 = f32[400,128]{1,0:T(8,128)S(1)} collective-permute-done((f32[400,128]{1,0:T(8,128)S(1)}, f32[400,128]{1,0:T(8,128)S(1)}, u32[]{:S(2)}, u32[]{:S(2)}) %collective-permute-start.4) | collective-permute-done | bytes 204832 | tf_op jit(solution)/shard_map/ppermute | solution.py:89
  75.9 2.4 %collective-permute-start.5 = (f32[200,128]{1,0:T(8,128)S(1)}, f32[200,128]{1,0:T(8,128)S(1)}, u32[]{:S(2)}, u32[]{:S(2)}) collective-permute-start(f32[200,128]{1,0:T(8,128)S(1)} %slice_select_fusion.2), channel_id=1, source_target_pairs={{0,128},{32,160},{64,192},{96,224},{128,0},{160,32},{192,64},{224,... | collective-permute-start | bytes 307208 | tf_op jit(solution)/shard_map/ppermute | solution.py:89
  78.2 3.9 %collective-permute-done.5 = f32[200,128]{1,0:T(8,128)S(1)} collective-permute-done((f32[200,128]{1,0:T(8,128)S(1)}, f32[200,128]{1,0:T(8,128)S(1)}, u32[]{:S(2)}, u32[]{:S(2)}) %collective-permute-start.5) | collective-permute-done | bytes 102432 | tf_op jit(solution)/shard_map/ppermute | solution.py:89
  82.2 4.6 %collective-permute-start.6 = (f32[100,128]{1,0:T(8,128)S(1)}, f32[100,128]{1,0:T(8,128)S(1)}, u32[]{:S(2)}, u32[]{:S(2)}) collective-permute-start(f32[100,128]{1,0:T(8,128)S(1)} %slice_select_fusion.3), channel_id=1, source_target_pairs={{0,32},{32,0},{64,96},{96,64},{128,160},{160,128},{192,224},{224,1... | collective-permute-start | bytes 153608 | tf_op jit(solution)/shard_map/ppermute | solution.py:89
  86.7 3.6 %collective-permute-done.6 = f32[100,128]{1,0:T(8,128)S(1)} collective-permute-done((f32[100,128]{1,0:T(8,128)S(1)}, f32[100,128]{1,0:T(8,128)S(1)}, u32[]{:S(2)}, u32[]{:S(2)}) %collective-permute-start.6) | collective-permute-done | bytes 51232 | tf_op jit(solution)/shard_map/ppermute | solution.py:89
  90.4 5.2 %collective-permute-start.7 = (f32[100,128]{1,0:T(8,128)S(1)}, f32[100,128]{1,0:T(8,128)S(1)}, u32[]{:S(2)}, u32[]{:S(2)}) collective-permute-start(f32[100,128]{1,0:T(8,128)S(1)} %select_add_fusion.1), channel_id=1, source_target_pairs={{0,32},{32,0},{64,96},{96,64},{128,160},{160,128},{192,224},{224,1... | collective-permute-start | bytes 153608 | tf_op jit(solution)/shard_map/ppermute | solution.py:93
  95.7 0.1 copy.26
  95.8 2.7 %collective-permute-done.7 = f32[100,128]{1,0:T(8,128)S(1)} collective-permute-done((f32[100,128]{1,0:T(8,128)S(1)}, f32[100,128]{1,0:T(8,128)S(1)}, u32[]{:S(2)}, u32[]{:S(2)}) %collective-permute-start.7) | collective-permute-done | bytes 51232 | tf_op jit(solution)/shard_map/ppermute | solution.py:93
  98.5 2.4 %collective-permute-start.8 = (f32[200,128]{1,0:T(8,128)S(1)}, f32[200,128]{1,0:T(8,128)S(1)}, u32[]{:S(2)}, u32[]{:S(2)}) collective-permute-start(f32[200,128]{1,0:T(8,128)S(1)} %maximum_select_fusion.2), channel_id=1, source_target_pairs={{0,128},{32,160},{64,192},{96,224},{128,0},{160,32},{192,64},{224,... | collective-permute-start | bytes 307208 | tf_op jit(solution)/shard_map/ppermute | solution.py:93
  101.0 3.8 %collective-permute-done.8 = f32[200,128]{1,0:T(8,128)S(1)} collective-permute-done((f32[200,128]{1,0:T(8,128)S(1)}, f32[200,128]{1,0:T(8,128)S(1)}, u32[]{:S(2)}, u32[]{:S(2)}) %collective-permute-start.8) | collective-permute-done | bytes 102432 | tf_op jit(solution)/shard_map/ppermute | solution.py:93
  104.8 0.5 collective-permute-start.9
  105.4 5.3 %collective-permute-done.9 = f32[400,128]{1,0:T(8,128)S(1)} collective-permute-done((f32[400,128]{1,0:T(8,128)S(1)}, f32[400,128]{1,0:T(8,128)S(1)}, u32[]{:S(2)}, u32[]{:S(2)}) %collective-permute-start.9) | collective-permute-done | bytes 204832 | tf_op jit(solution)/shard_map/ppermute | solution.py:93
  110.7 0.9 fusion.2
  (50 shorter events, 0.5 us)
Async XLA Ops:
  1.4 9.2 %copy-start.9 = (f32[50]{0:T(128)S(1)}, f32[50]{0:T(128)}, u32[]{:S(2)}) copy-start(f32[50]{0:T(128)} %param.25) | copy-start | bytes 604
  2.7 10.1 %copy-start.5 = (f32[50,16,128]{2,1,0:T(8,128)S(1)}, f32[50,16,128]{2,1,0:T(8,128)}, u32[]{:S(2)}) copy-start(f32[50,16,128]{2,1,0:T(8,128)} %param.24) | copy-start | bytes 1228804
  3.5 22.3 %collective-permute-start.2 = (f32[101,6,128]{2,1,0:T(8,128)}, f32[101,6,128]{2,1,0:T(8,128)}, u32[]{:S(2)}, u32[]{:S(2)}) collective-permute-start(f32[101,6,128]{2,1,0:T(8,128)} %pad_maximum_fusion), channel_id=1, source_target_pairs={{0,1},{1,2},{2,3},{3,4},{4,5},{5,6},{6,7},{7,8},{8,9},{9,10},{10,1... | collective-permute-start | bytes 930824 | tf_op jit(solution)/shard_map/ppermute | solution.py:151
  4.3 22.2 %collective-permute-start.3 = (f32[101,6,128]{2,1,0:T(8,128)}, f32[101,6,128]{2,1,0:T(8,128)}, u32[]{:S(2)}, u32[]{:S(2)}) collective-permute-start(f32[101,6,128]{2,1,0:T(8,128)} %pad_maximum_fusion.1), channel_id=1, source_target_pairs={{1,0},{2,1},{3,2},{4,3},{5,4},{6,5},{7,6},{8,7},{9,8},{10,9},{11,1... | collective-permute-start | bytes 930824 | tf_op jit(solution)/shard_map/ppermute | solution.py:152
  19.8 19.0 %collective-permute-start = (f32[200,6,128]{2,0,1:T(8,128)S(1)}, f32[200,6,128]{2,0,1:T(8,128)S(1)}, u32[]{:S(2)}, u32[]{:S(2)}) collective-permute-start(f32[200,6,128]{2,0,1:T(8,128)S(1)} %copy.23), channel_id=1, source_target_pairs={{0,1},{1,2},{2,3},{3,4},{4,5},{5,6},{6,7},{7,8},{8,9},{9,10},{10,1... | collective-permute-start | bytes 1843208 | tf_op jit(solution)/shard_map/ppermute | solution.py:151
  20.1 19.0 %collective-permute-start.1 = (f32[200,6,128]{2,0,1:T(8,128)S(1)}, f32[200,6,128]{2,0,1:T(8,128)S(1)}, u32[]{:S(2)}, u32[]{:S(2)}) collective-permute-start(f32[200,6,128]{2,0,1:T(8,128)S(1)} %copy.24), channel_id=1, source_target_pairs={{1,0},{2,1},{3,2},{4,3},{5,4},{6,5},{7,6},{8,7},{9,8},{10,9},{11,1... | collective-permute-start | bytes 1843208 | tf_op jit(solution)/shard_map/ppermute | solution.py:152
  29.5 1.0 copy-start.3
  29.5 1.0 copy-start.11
  30.5 1.8 %copy-start.4 = (f32[50,16,128]{2,1,0:T(8,128)S(1)}, f32[50,16,128]{2,1,0:T(8,128)}, u32[]{:S(2)}) copy-start(f32[50,16,128]{2,1,0:T(8,128)} %param.20) | copy-start | bytes 1228804
  30.5 1.8 %copy-start.12 = (f32[50]{0:T(128)S(1)}, f32[50]{0:T(128)}, u32[]{:S(2)}) copy-start(f32[50]{0:T(128)} %param.22) | copy-start | bytes 604
  34.1 5.1 %copy-start.1 = (f32[4,50,16,128]{3,2,1,0:T(8,128)S(1)}, f32[4,50,16,128]{3,2,1,0:T(8,128)}, u32[]{:S(2)}) copy-start(f32[4,50,16,128]{3,2,1,0:T(8,128)} %shard_map.140) | copy-start | bytes 4915204
  69.9 16.8 %copy-start.10 = (f32[16,128]{1,0:T(8,128)S(1)}, f32[16,128]{1,0:T(8,128)}, u32[]{:S(2)}) copy-start(f32[16,128]{1,0:T(8,128)} %param.27) | copy-start | bytes 24580
  69.9 25.7 %copy-start = (f32[4,50,16,128]{3,2,1,0:T(8,128)S(1)}, f32[4,50,16,128]{3,2,1,0:T(8,128)}, u32[]{:S(2)}) copy-start(f32[4,50,16,128]{3,2,1,0:T(8,128)} %shard_map.141) | copy-start | bytes 4915204
  70.0 5.8 %collective-permute-start.4 = (f32[400,128]{1,0:T(8,128)S(1)}, f32[400,128]{1,0:T(8,128)S(1)}, u32[]{:S(2)}, u32[]{:S(2)}) collective-permute-start(f32[400,128]{1,0:T(8,128)S(1)} %bitcast.49), channel_id=1, source_target_pairs={{0,64},{32,96},{64,0},{96,32},{128,192},{160,224},{192,128},{224,1... | collective-permute-start | bytes 614408 | tf_op jit(solution)/shard_map/ppermute | solution.py:89
  75.9 6.3 %collective-permute-start.5 = (f32[200,128]{1,0:T(8,128)S(1)}, f32[200,128]{1,0:T(8,128)S(1)}, u32[]{:S(2)}, u32[]{:S(2)}) collective-permute-start(f32[200,128]{1,0:T(8,128)S(1)} %slice_select_fusion.2), channel_id=1, source_target_pairs={{0,128},{32,160},{64,192},{96,224},{128,0},{160,32},{192,64},{224,... | collective-permute-start | bytes 307208 | tf_op jit(solution)/shard_map/ppermute | solution.py:89
  82.2 8.2 %collective-permute-start.6 = (f32[100,128]{1,0:T(8,128)S(1)}, f32[100,128]{1,0:T(8,128)S(1)}, u32[]{:S(2)}, u32[]{:S(2)}) collective-permute-start(f32[100,128]{1,0:T(8,128)S(1)} %slice_select_fusion.3), channel_id=1, source_target_pairs={{0,32},{32,0},{64,96},{96,64},{128,160},{160,128},{192,224},{224,1... | collective-permute-start | bytes 153608 | tf_op jit(solution)/shard_map/ppermute | solution.py:89
  90.4 8.1 %collective-permute-start.7 = (f32[100,128]{1,0:T(8,128)S(1)}, f32[100,128]{1,0:T(8,128)S(1)}, u32[]{:S(2)}, u32[]{:S(2)}) collective-permute-start(f32[100,128]{1,0:T(8,128)S(1)} %select_add_fusion.1), channel_id=1, source_target_pairs={{0,32},{32,0},{64,96},{96,64},{128,160},{160,128},{192,224},{224,1... | collective-permute-start | bytes 153608 | tf_op jit(solution)/shard_map/ppermute | solution.py:93
  95.6 5.3 %copy-start.7 = (f32[2,16,128]{2,1,0:T(8,128)S(1)}, f32[2,16,128]{2,1,0:T(8,128)}, u32[]{:S(2)}) copy-start(f32[2,16,128]{2,1,0:T(8,128)} %param.19) | copy-start | bytes 49156
  95.6 5.3 %copy-start.8 = (f32[2,16,128]{2,1,0:T(8,128)S(1)}, f32[2,16,128]{2,1,0:T(8,128)}, u32[]{:S(2)}) copy-start(f32[2,16,128]{2,1,0:T(8,128)} %param.18) | copy-start | bytes 49156
  95.8 14.9 %copy-start.6 = (f32[50,16,128]{2,1,0:T(8,128)S(1)}, f32[50,16,128]{2,1,0:T(8,128)}, u32[]{:S(2)}) copy-start(f32[50,16,128]{2,1,0:T(8,128)} %param.26) | copy-start | bytes 1228804
  98.5 6.3 %collective-permute-start.8 = (f32[200,128]{1,0:T(8,128)S(1)}, f32[200,128]{1,0:T(8,128)S(1)}, u32[]{:S(2)}, u32[]{:S(2)}) collective-permute-start(f32[200,128]{1,0:T(8,128)S(1)} %maximum_select_fusion.2), channel_id=1, source_target_pairs={{0,128},{32,160},{64,192},{96,224},{128,0},{160,32},{192,64},{224,... | collective-permute-start | bytes 307208 | tf_op jit(solution)/shard_map/ppermute | solution.py:93
  104.8 5.8 %collective-permute-start.9 = (f32[400,128]{1,0:T(8,128)S(1)}, f32[400,128]{1,0:T(8,128)S(1)}, u32[]{:S(2)}, u32[]{:S(2)}) collective-permute-start(f32[400,128]{1,0:T(8,128)S(1)} %maximum_select_fusion.1), channel_id=1, source_target_pairs={{0,64},{32,96},{64,0},{96,32},{128,192},{160,224},{192,128},{224,1... | collective-permute-start | bytes 614408 | tf_op jit(solution)/shard_map/ppermute | solution.py:93
  105.4 6.2 %copy-start.2 = (f32[2,2,50,16,128]{4,3,2,1,0:T(8,128)}, f32[2,2,50,16,128]{4,3,2,1,0:T(8,128)S(1)}, u32[]{:S(2)}) copy-start(f32[2,2,50,16,128]{4,3,2,1,0:T(8,128)S(1)} %fusion.3) | copy-start | bytes 4915204

commit v2 on v0

--- a/solution.py
+++ b/solution.py
@@ -186,11 +186,18 @@
     wide_wet = (depth_index.astype(jnp.float32) < wide_bottom).astype(jnp.float32)
     wet_cube = (depth_index[:, :width] < wet_bottom[None]).astype(jnp.float32)
 
+    lanes = adjoint_in.shape[-1]
+    combined = jnp.sum(adjoint_in[:, 0] - alk_ratio * adjoint_in[:, 1], axis=0)
+    combined = scenario_sum(combined)
+
     below_band, diagonal, above_band = column_coefficients(vertical_mix, thickness, wet_cube)
     adjoint = transposed_solve(adjoint_in, below_band, diagonal, above_band)
-    (adjoint,) = padded_halo(
-        [adjoint.reshape((-1,) + adjoint.shape[-2:])], width, halo, padded
-    )
+    combined = transposed_solve(combined[None], below_band, diagonal, above_band)
+    fields = adjoint_in.shape[0] * adjoint_in.shape[1]
+    stacked = jnp.concatenate(
+        [adjoint.reshape((fields, levels, width, lanes)), combined], 0
+    )
+    (stacked,) = padded_halo([stacked.reshape((-1, width, lanes))], width, halo, padded)
 
     east_a, east_b = face_pairs(
         wide_east, wide_wet, jnp.roll(wide_wet, -1, axis=1), east_diffusion
@@ -199,17 +206,16 @@
     north_next = jnp.concatenate([wide_wet[..., 1:], zero_row], -1)
     north_a, north_b = face_pairs(wide_north, wide_wet, north_next, north_diffusion)
 
-    fields = adjoint_in.shape[0] * adjoint_in.shape[1]
-    adjoint = transport_substeps(
-        adjoint.reshape((fields, levels) + adjoint.shape[-2:]),
+    stacked = transport_substeps(
+        stacked.reshape((fields + 1, levels, padded, lanes)),
         east_a,
         east_b,
         north_a,
         north_b,
         width,
-    ).reshape(adjoint_in.shape)
-    rate_term = jnp.sum(adjoint[:, 0] - alk_ratio * adjoint[:, 1], axis=0)
-    summed = scenario_sum(rate_term)
+    )
+    adjoint = stacked[:fields].reshape(adjoint_in.shape)
+    summed = stacked[fields]
     rate_gradient = export_flux * wet_cube * summed
     slope_carbon, slope_alkalinity = carbonate_slopes(surface_carbon, surface_alkalinity)
     exchange_scale = wet_cube[0] * piston * adjoint[:, 0, 0]

time: 107 us -> 114 us (1.065); the launches traced: 107 us -> 112 us
  Pallas kernels: 25.3 us -> 33.1 us
  local copies, waits for them, and re-layouts: 8.75 us -> 5.9 us
  waiting for transfers between devices: 29.5 us -> 27.1 us
  starting transfers between devices: 27.7 us -> 29.2 us
  other arithmetic: 14.5 us -> 15.9 us
    ppermute x3, waiting for transfers between devices: 12.8 us -> 3.89 us  [scenario_sum(): rows = keep + lax.ppermute(send, 'scen', pairs)]
    ppermute x2, waiting for transfers between devices: 4.78 us -> 12.1 us  [padded_halo(): before = lax.ppermute(last, 'grid', up)]
    pallas_call x1, Pallas kernels: 21.8 us -> 27 us  [transport_substeps(): pl.pallas_call(substep_kernel, grid=(levels // chunk,), in_specs=[field_b...]
    pallas_call x1 -> x2, Pallas kernels: 3.48 us -> 6.17 us  [transposed_solve(): pl.pallas_call(solve_kernel, out_shape=jax.ShapeDtypeStruct(rhs.shape, jn...]
    slice x3, local copies, waits for them, and re-layouts: 2.8 us -> 0.2 us  [padded_halo(): last = jnp.concatenate([piece[:, width - halo:] for piece in pieces], 0)]
    slice x2, local copies, waits for them, and re-layouts: 1.74 us -> 0.03 us  [padded_halo(): after[offset:offset + rows]]
    ppermute x3, starting transfers between devices: 7.5 us -> 9.12 us  [scenario_sum(): rows = keep + lax.ppermute(send, 'scen', pairs)]
    slice x0 -> x1, local copies, waits for them, and re-layouts: none -> 1.55 us  [on_device(): adjoint = stacked[:fields].reshape(adjoint_in.shape)]
  transfers between devices with their start and end apart: 10 -> 10, of which waited for: 7 -> 5; matrix products, arithmetic and copies ran while one was open for 14% -> 9% of each run, Pallas kernels for 3% -> 3%
where the time goes in v2:
time: 114 us; the launch traced here: 112 us
  Pallas kernels  33.1 us (29%)
  starting transfers between devices  29.2 us (26%)
  waiting for transfers between devices  27.1 us (24%)
  other arithmetic  15.9 us (14%)
  local copies, waits for them, and re-layouts  5.9 us (5%)
    pallas_call x1, Pallas kernels, transport_substeps(): pl.pallas_call(substep_kernel, grid=(levels // chunk,), in_specs=[field_b...  27 us
    ppermute x2, waiting for transfers between devices, padded_halo(): before = lax.ppermute(last, 'grid', up)  12.1 us
    ppermute x2, starting transfers between devices, padded_halo(): after = lax.ppermute(initial, 'grid', down)  11.6 us
    ppermute x3, waiting for transfers between devices, scenario_sum(): other = lax.ppermute(rows, 'scen', pairs)  11.2 us
    ppermute x3, starting transfers between devices, scenario_sum(): rows = keep + lax.ppermute(send, 'scen', pairs)  9.12 us
    ppermute x3, starting transfers between devices, scenario_sum(): other = lax.ppermute(rows, 'scen', pairs)  8.29 us
    pallas_call x2, Pallas kernels, transposed_solve(): pl.pallas_call(solve_kernel, out_shape=jax.ShapeDtypeStruct(rhs.shape, jn...  6.17 us
    ppermute x3, waiting for transfers between devices, scenario_sum(): rows = keep + lax.ppermute(send, 'scen', pairs)  3.89 us
  transfers between devices with their start and end apart: 10, of which 5 were waited for; matrix products, arithmetic and copies ran while one was open for 9% of the time, Pallas kernels for 3%

profile of v2, /device:TPU:8, one launch (start us, length us, event | category | flops | bytes accessed | tf_op | source)
XLA Modules:
  0.0 112.4 jit_solution(14787457121835332654)
XLA Ops:
  0.7 1.6 %subtract_reduce_fusion = f32[50,16,128]{2,1,0:T(8,128)S(1)} fusion(f32[2,2,50,16,128]{4,3,2,1,0:T(8,128)} %param.17), kind=kLoop, calls=%fused_computation.11 | loop fusion | flops 512000 | bytes 2048000 | tf_op jit(solution)/shard_map/reduce_sum | solution.py:190
  2.4 2.2 %collective-permute-start = (f32[400,128]{1,0:T(8,128)S(1)}, f32[400,128]{1,0:T(8,128)S(1)}, u32[]{:S(2)}, u32[]{:S(2)}) collective-permute-start(f32[400,128]{1,0:T(8,128)S(1)} %bitcast.52), channel_id=1, source_target_pairs={{0,64},{32,96},{64,0},{96,32},{128,192},{160,224},{192,128},{224,1... | collective-permute-start | bytes 614408 | tf_op jit(solution)/shard_map/ppermute | solution.py:89
  4.7 0.1 fusion.9
  4.8 0.1 collective-permute-start.8
  4.9 5.7 %collective-permute-start.9 = (f32[101,6,128]{2,1,0:T(8,128)S(1)}, f32[101,6,128]{2,1,0:T(8,128)S(1)}, u32[]{:S(2)}, u32[]{:S(2)}) collective-permute-start(f32[101,6,128]{2,1,0:T(8,128)S(1)} %pad_maximum_fusion.2), channel_id=1, source_target_pairs={{1,0},{2,1},{3,2},{4,3},{5,4},{6,5},{7,6},{8,7},{9,8},{10,9},{11,1... | collective-permute-start | bytes 930824 | tf_op jit(solution)/shard_map/ppermute | solution.py:147
  10.7 0.6 fusion.12
  11.2 0.1 fusion.13
  11.3 0.1 compare_convert_fusion.1
  11.5 1.4 %pad_maximum_fusion.3 = (f32[50]{0:T(128)S(1)}, f32[50]{0:T(128)S(1)}) fusion(f32[49]{0:T(128)S(1)} %get-tuple-element.50, f32[1]{0:T(128)} %get-tuple-element.48, f32[1]{0:T(128)} %get-tuple-element.49, f32[49]{0:T(128)S(1)} %get-tuple-element.51), kind=kLoop, calls=%fused_computation.45 | loop fusion | flops 100 | bytes 800 | tf_op jit(solution)/shard_map/concatenate | solution.py:27
  12.8 0.9 negate_divide_fusion
  13.8 1.3 %collective-permute-start.1 = (f32[200,128]{1,0:T(8,128)S(1)}, f32[200,128]{1,0:T(8,128)S(1)}, u32[]{:S(2)}, u32[]{:S(2)}) collective-permute-start(f32[200,128]{1,0:T(8,128)S(1)} %slice_select_fusion.2), channel_id=1, source_target_pairs={{0,128},{32,160},{64,192},{96,224},{128,0},{160,32},{192,64},{224,... | collective-permute-start | bytes 307208 | tf_op jit(solution)/shard_map/ppermute | solution.py:89
  15.1 1.1 divide_add_fusion
  16.2 3.9 %collective-permute-done.1 = f32[200,128]{1,0:T(8,128)S(1)} collective-permute-done((f32[200,128]{1,0:T(8,128)S(1)}, f32[200,128]{1,0:T(8,128)S(1)}, u32[]{:S(2)}, u32[]{:S(2)}) %collective-permute-start.1) | collective-permute-done | bytes 102432 | tf_op jit(solution)/shard_map/ppermute | solution.py:89
  20.1 5.6 %collective-permute-start.2 = (f32[100,128]{1,0:T(8,128)S(1)}, f32[100,128]{1,0:T(8,128)S(1)}, u32[]{:S(2)}, u32[]{:S(2)}) collective-permute-start(f32[100,128]{1,0:T(8,128)S(1)} %slice_select_fusion.3), channel_id=1, source_target_pairs={{0,32},{32,0},{64,96},{96,64},{128,160},{160,128},{192,224},{224,1... | collective-permute-start | bytes 153608 | tf_op jit(solution)/shard_map/ppermute | solution.py:89
  25.7 0.1 pad.35.clone
  25.8 3.5 %shard_map.140 = f32[4,50,16,128]{3,2,1,0:T(8,128)} custom-call(f32[4,50,16,128]{3,2,1,0:T(8,128)} %bitcast.46, f32[50,16,128]{2,1,0:T(8,128)} %get-tuple-element.45.below_ref, f32[50,16,128]{2,1,0:T(8,128)} %get-tuple-element.44.diagonal_ref, f32[50,16,128]{2,1,0:T(8,128)} %get-tuple-element.26.above_ref), custom_call_target="tpu_custom_call" | custom-call | tf_op jit(solution)/shard_map/pallas_call | solution.py:56
  29.3 4.5 %collective-permute-start.3 = (f32[100,128]{1,0:T(8,128)S(1)}, f32[100,128]{1,0:T(8,128)S(1)}, u32[]{:S(2)}, u32[]{:S(2)}) collective-permute-start(f32[100,128]{1,0:T(8,128)S(1)} %select_add_fusion.1), channel_id=1, source_target_pairs={{0,32},{32,0},{64,96},{96,64},{128,160},{160,128},{192,224},{224,1... | collective-permute-start | bytes 153608 | tf_op jit(solution)/shard_map/ppermute | solution.py:93
  33.9 0.1 maximum_bitcast_fusion
  33.9 4.1 %collective-permute-done.3 = f32[100,128]{1,0:T(8,128)S(1)} collective-permute-done((f32[100,128]{1,0:T(8,128)S(1)}, f32[100,128]{1,0:T(8,128)S(1)}, u32[]{:S(2)}, u32[]{:S(2)}) %collective-permute-start.3) | collective-permute-done | bytes 51232 | tf_op jit(solution)/shard_map/ppermute | solution.py:93
  38.0 2.6 %collective-permute-start.4 = (f32[200,128]{1,0:T(8,128)S(1)}, f32[200,128]{1,0:T(8,128)S(1)}, u32[]{:S(2)}, u32[]{:S(2)}) collective-permute-start(f32[200,128]{1,0:T(8,128)S(1)} %maximum_select_fusion.2), channel_id=1, source_target_pairs={{0,128},{32,160},{64,192},{96,224},{128,0},{160,32},{192,64},{224,... | collective-permute-start | bytes 307208 | tf_op jit(solution)/shard_map/ppermute | solution.py:93
  40.6 0.1 compare_convert_fusion
  40.7 0.1 slice.236
  40.9 0.3 slice.240
  41.2 3.1 %collective-permute-done.4 = f32[200,128]{1,0:T(8,128)S(1)} collective-permute-done((f32[200,128]{1,0:T(8,128)S(1)}, f32[200,128]{1,0:T(8,128)S(1)}, u32[]{:S(2)}, u32[]{:S(2)}) %collective-permute-start.4) | collective-permute-done | bytes 102432 | tf_op jit(solution)/shard_map/ppermute | solution.py:93
  44.3 1.2 %collective-permute-start.5 = (f32[400,128]{1,0:T(8,128)S(1)}, f32[400,128]{1,0:T(8,128)S(1)}, u32[]{:S(2)}, u32[]{:S(2)}) collective-permute-start(f32[400,128]{1,0:T(8,128)S(1)} %maximum_select_fusion.1), channel_id=1, source_target_pairs={{0,64},{32,96},{64,0},{96,32},{128,192},{160,224},{192,128},{224,1... | collective-permute-start | bytes 614408 | tf_op jit(solution)/shard_map/ppermute | solution.py:93
  45.5 0.7 fusion.7
  46.2 4.0 %collective-permute-done.5 = f32[400,128]{1,0:T(8,128)S(1)} collective-permute-done((f32[400,128]{1,0:T(8,128)S(1)}, f32[400,128]{1,0:T(8,128)S(1)}, u32[]{:S(2)}, u32[]{:S(2)}) %collective-permute-start.5) | collective-permute-done | bytes 204832 | tf_op jit(solution)/shard_map/ppermute | solution.py:93
  50.2 0.8 maximum_select_fusion
  50.9 2.7 %shard_map.141 = f32[1,50,16,128]{3,2,1,0:T(8,128)} custom-call(f32[1,50,16,128]{3,2,1,0:T(8,128)} %bitcast.49, f32[50,16,128]{2,1,0:T(8,128)} %get-tuple-element.45.below_ref, f32[50,16,128]{2,1,0:T(8,128)} %get-tuple-element.44.diagonal_ref, f32[50,16,128]{2,1,0:T(8,128)} %get-tuple-element.26.above_ref), custom_call_target="tpu_custom_call" | custom-call | tf_op jit(solution)/shard_map/pallas_call | solution.py:56
  53.6 1.1 %pad_maximum_fusion = f32[5,50,16,128]{3,2,1,0:T(8,128)S(1)} fusion(f32[1,50,16,128]{3,2,1,0:T(8,128)} %shard_map.141, f32[4,50,16,128]{3,2,1,0:T(8,128)S(1)} %copy-done), kind=kLoop, calls=%fused_computation.1 | loop fusion | flops 512000 | bytes 4096000 | tf_op jit(solution)/shard_map/concatenate | solution.py:197
  54.8 0.1 fusion.6
  55.0 0.2 copy.23
  55.1 0.1 collective-permute-start.6
  55.2 0.2 copy.24
  55.4 5.9 %collective-permute-start.7 = (f32[250,6,128]{2,0,1:T(8,128)S(1)}, f32[250,6,128]{2,0,1:T(8,128)S(1)}, u32[]{:S(2)}, u32[]{:S(2)}) collective-permute-start(f32[250,6,128]{2,0,1:T(8,128)S(1)} %copy.24), channel_id=1, source_target_pairs={{1,0},{2,1},{3,2},{4,3},{5,4},{6,5},{7,6},{8,7},{9,8},{10,9},{11,1... | collective-permute-start | bytes 2304008 | tf_op jit(solution)/shard_map/ppermute | solution.py:147
  61.3 1.8 %minimum_subtract_fusion = (f32[50,32,128]{2,1,0:T(8,128)}, f32[50,32,128]{2,1,0:T(8,128)}) fusion(f32[50,32,127]{2,1,0:T(8,128)S(1)} %slice.240, f32[50,6,128]{2,1,0:T(8,128)S(1)} %get-tuple-element.36, f32[50,16,128]{2,1,0:T(8,128)S(1)} %copy-done.4, f32[50,6,128]{2,1,0:T(8,128)S(1)} %copy-done.7, f32[32]{0:T(128)S(1)} %pad.35.clone, f32[50]{0:T(128)S(1)} %copy-done.20, ...), kind=kLoop, calls=%fused_computation.7 | loop fusion | flops 2252800 | bytes 3184912 | tf_op jit(solution)/shard_map/sub | solution.py:18
  63.2 1.7 %minimum_subtract_fusion.1 = (f32[50,32,128]{2,1,0:T(8,128)}, f32[50,32,128]{2,1,0:T(8,128)}) fusion(f32[32]{0:T(128)S(1)} %pad.35.clone, f32[50,6,128]{2,1,0:T(8,128)S(1)} %get-tuple-element.37, f32[50,16,128]{2,1,0:T(8,128)S(1)} %copy-done.6, f32[50,6,128]{2,1,0:T(8,128)S(1)} %get-tuple-element.35, f32[50,1,128]{2,1,0:T(1,128)S(1)} %slice.237, ...), kind=kLoop, calls=%fused_computation.9 | loop fusion | flops 2457600 | bytes 3191312 | tf_op jit(solution)/shard_map/sub | solution.py:18
  64.9 12.1 %collective-permute-done.6 = f32[250,6,128]{2,0,1:T(8,128)S(1)} collective-permute-done((f32[250,6,128]{2,0,1:T(8,128)S(1)}, f32[250,6,128]{2,0,1:T(8,128)S(1)}, u32[]{:S(2)}, u32[]{:S(2)}) %collective-permute-start.6) | collective-permute-done | bytes 768032 | tf_op jit(solution)/shard_map/ppermute | solution.py:146
  77.0 0.5 copy.18
  77.5 0.5 copy.20
  78.0 2.7 %maximum_maximum_fusion.adjoint_ref = f32[5,50,32,128]{3,2,1,0:T(8,128)} fusion(f32[5,50,6,128]{3,2,1,0:T(8,128)S(1)} %bitcast.48, f32[1,50,16,128]{3,2,1,0:T(8,128)S(1)} %copy-done.1, f32[4,50,16,128]{3,2,1,0:T(8,128)S(1)} %copy-done, f32[5,50,6,128]{3,2,1,0:T(8,128)S(1)} %bitcast.47, f32[32]{0:T(128)S(1)} %pad.35.clone), kind=kLoop, calls=%fused_computation | loop fusion | flops 4096000 | bytes 7680128 | tf_op jit(solution)/shard_map/concatenate | solution.py:154
  80.7 27.0 %shard_map.142 = f32[5,50,16,128]{3,2,1,0:T(8,128)} custom-call(f32[5,50,32,128]{3,2,1,0:T(8,128)} %maximum_maximum_fusion.adjoint_ref, f32[50,32,128]{2,1,0:T(8,128)} %get-tuple-element.31.east_a_ref, f32[50,32,128]{2,1,0:T(8,128)} %get-tuple-element.30.east_b_ref, f32[50,32,128]{2,1,0:T(8,128)} %get-tuple-element.33.north_a_ref, ...), custom_call_target="tpu_custom_call" | custom-call | tf_op jit(solution)/shard_map/pallas_call | solution.py:131
  107.7 1.5 %slice.243 = f32[4,50,16,128]{3,2,1,0:T(8,128)S(1)} slice(f32[5,50,16,128]{3,2,1,0:T(8,128)} %shard_map.142), slice={[0:4], [0:50], [0:16], [0:128]} | slice | bytes 3276800 | tf_op jit(solution)/shard_map/slice | solution.py:217
  109.3 0.1 copy.26
  109.4 0.5 copy-done.14
  109.9 0.0 copy-done.15
  110.0 0.3 copy-done.13
  110.3 2.1 %fusion = f32[50,16,128]{2,1,0:T(8,128)} fusion(f32[50,16,128]{2,1,0:T(8,128)S(1)} %copy-done.13, f32[5,50,16,128]{3,2,1,0:T(8,128)} %shard_map.142, f32[16,128]{1,0:T(8,128)S(1)} %select_convert_fusion, f32[50]{0:T(128)S(1)} %iota_convert_fusion), kind=kLoop, calls=%fused_computation.16 | loop fusion | flops 307200 | bytes 1237192 | tf_op jit(solution)/shard_map/mul | solution.py:219
  (71 shorter events, 0.5 us)
Async XLA Ops:
  0.6 4.0 %copy-start.18 = (s32[16,128]{1,0:T(8,128)S(1)}, s32[16,128]{1,0:T(8,128)}, u32[]{:S(2)}) copy-start(s32[16,128]{1,0:T(8,128)} %param.28) | copy-start | bytes 24580
  0.6 4.0 %copy-start.17 = (s32[16,128]{1,0:T(8,128)S(1)}, s32[16,128]{1,0:T(8,128)}, u32[]{:S(2)}) copy-start(s32[16,128]{1,0:T(8,128)} %param.29) | copy-start | bytes 24580
  0.6 4.0 %copy-start.5 = (f32[50,16,128]{2,1,0:T(8,128)S(1)}, f32[50,16,128]{2,1,0:T(8,128)}, u32[]{:S(2)}) copy-start(f32[50,16,128]{2,1,0:T(8,128)} %param.20) | copy-start | bytes 1228804
  0.7 4.0 %copy-start.3 = (f32[50,16,128]{2,1,0:T(8,128)S(1)}, f32[50,16,128]{2,1,0:T(8,128)}, u32[]{:S(2)}) copy-start(f32[50,16,128]{2,1,0:T(8,128)} %param.21) | copy-start | bytes 1228804
  2.3 8.3 %copy-start.16 = (f32[50]{0:T(128)S(1)}, f32[50]{0:T(128)}, u32[]{:S(2)}) copy-start(f32[50]{0:T(128)} %param.25) | copy-start | bytes 604
  2.4 11.4 %collective-permute-start = (f32[400,128]{1,0:T(8,128)S(1)}, f32[400,128]{1,0:T(8,128)S(1)}, u32[]{:S(2)}, u32[]{:S(2)}) collective-permute-start(f32[400,128]{1,0:T(8,128)S(1)} %bitcast.52), channel_id=1, source_target_pairs={{0,64},{32,96},{64,0},{96,32},{128,192},{160,224},{192,128},{224,1... | collective-permute-start | bytes 614408 | tf_op jit(solution)/shard_map/ppermute | solution.py:89
  4.7 8.1 %copy-start.12 = (f32[50,16,128]{2,1,0:T(8,128)S(1)}, f32[50,16,128]{2,1,0:T(8,128)}, u32[]{:S(2)}) copy-start(f32[50,16,128]{2,1,0:T(8,128)} %param.24) | copy-start | bytes 1228804
  4.8 24.5 %collective-permute-start.8 = (f32[101,6,128]{2,1,0:T(8,128)S(1)}, f32[101,6,128]{2,1,0:T(8,128)S(1)}, u32[]{:S(2)}, u32[]{:S(2)}) collective-permute-start(f32[101,6,128]{2,1,0:T(8,128)S(1)} %pad_maximum_fusion.1), channel_id=1, source_target_pairs={{0,1},{1,2},{2,3},{3,4},{4,5},{5,6},{6,7},{7,8},{8,9},{9,10},{10,1... | collective-permute-start | bytes 930824 | tf_op jit(solution)/shard_map/ppermute | solution.py:146
  4.9 24.3 %collective-permute-start.9 = (f32[101,6,128]{2,1,0:T(8,128)S(1)}, f32[101,6,128]{2,1,0:T(8,128)S(1)}, u32[]{:S(2)}, u32[]{:S(2)}) collective-permute-start(f32[101,6,128]{2,1,0:T(8,128)S(1)} %pad_maximum_fusion.2), channel_id=1, source_target_pairs={{1,0},{2,1},{3,2},{4,3},{5,4},{6,5},{7,6},{8,7},{9,8},{10,9},{11,1... | collective-permute-start | bytes 930824 | tf_op jit(solution)/shard_map/ppermute | solution.py:147
  13.7 12.0 %copy-start.19 = (f32[16,128]{1,0:T(8,128)S(1)}, f32[16,128]{1,0:T(8,128)}, u32[]{:S(2)}) copy-start(f32[16,128]{1,0:T(8,128)} %param.27) | copy-start | bytes 24580
  13.8 6.3 %collective-permute-start.1 = (f32[200,128]{1,0:T(8,128)S(1)}, f32[200,128]{1,0:T(8,128)S(1)}, u32[]{:S(2)}, u32[]{:S(2)}) collective-permute-start(f32[200,128]{1,0:T(8,128)S(1)} %slice_select_fusion.2), channel_id=1, source_target_pairs={{0,128},{32,160},{64,192},{96,224},{128,0},{160,32},{192,64},{224,... | collective-permute-start | bytes 307208 | tf_op jit(solution)/shard_map/ppermute | solution.py:89
  20.1 9.2 %collective-permute-start.2 = (f32[100,128]{1,0:T(8,128)S(1)}, f32[100,128]{1,0:T(8,128)S(1)}, u32[]{:S(2)}, u32[]{:S(2)}) collective-permute-start(f32[100,128]{1,0:T(8,128)S(1)} %slice_select_fusion.3), channel_id=1, source_target_pairs={{0,32},{32,0},{64,96},{96,64},{128,160},{160,128},{192,224},{224,1... | collective-permute-start | bytes 153608 | tf_op jit(solution)/shard_map/ppermute | solution.py:89
  29.3 11.4 %copy-start.10 = (f32[101,6,128]{2,1,0:T(8,128)}, f32[101,6,128]{2,1,0:T(8,128)S(1)}, u32[]{:S(2)}) copy-start(f32[101,6,128]{2,1,0:T(8,128)S(1)} %collective-permute-done.8) | copy-start | bytes 930820
  29.3 11.3 %copy-start.8 = (f32[101,6,128]{2,1,0:T(8,128)}, f32[101,6,128]{2,1,0:T(8,128)S(1)}, u32[]{:S(2)}) copy-start(f32[101,6,128]{2,1,0:T(8,128)S(1)} %collective-permute-done.9) | copy-start | bytes 930820
  29.3 8.7 %collective-permute-start.3 = (f32[100,128]{1,0:T(8,128)S(1)}, f32[100,128]{1,0:T(8,128)S(1)}, u32[]{:S(2)}, u32[]{:S(2)}) collective-permute-start(f32[100,128]{1,0:T(8,128)S(1)} %select_add_fusion.1), channel_id=1, source_target_pairs={{0,32},{32,0},{64,96},{96,64},{128,160},{160,128},{192,224},{224,1... | collective-permute-start | bytes 153608 | tf_op jit(solution)/shard_map/ppermute | solution.py:93
  38.0 6.3 %collective-permute-start.4 = (f32[200,128]{1,0:T(8,128)S(1)}, f32[200,128]{1,0:T(8,128)S(1)}, u32[]{:S(2)}, u32[]{:S(2)}) collective-permute-start(f32[200,128]{1,0:T(8,128)S(1)} %maximum_select_fusion.2), channel_id=1, source_target_pairs={{0,128},{32,160},{64,192},{96,224},{128,0},{160,32},{192,64},{224,... | collective-permute-start | bytes 307208 | tf_op jit(solution)/shard_map/ppermute | solution.py:93
  40.7 4.8 %copy-start.11 = (f32[101,6,128]{2,1,0:T(8,128)S(1)}, f32[101,6,128]{2,1,0:T(8,128)}, u32[]{:S(2)}) copy-start(f32[101,6,128]{2,1,0:T(8,128)} %copy-done.10) | copy-start | bytes 930820
  41.2 12.5 %copy-start = (f32[4,50,16,128]{3,2,1,0:T(8,128)S(1)}, f32[4,50,16,128]{3,2,1,0:T(8,128)}, u32[]{:S(2)}) copy-start(f32[4,50,16,128]{3,2,1,0:T(8,128)} %shard_map.140) | copy-start | bytes 4915204
  44.3 5.8 %collective-permute-start.5 = (f32[400,128]{1,0:T(8,128)S(1)}, f32[400,128]{1,0:T(8,128)S(1)}, u32[]{:S(2)}, u32[]{:S(2)}) collective-permute-start(f32[400,128]{1,0:T(8,128)S(1)} %maximum_select_fusion.1), channel_id=1, source_target_pairs={{0,64},{32,96},{64,0},{96,32},{128,192},{160,224},{192,128},{224,1... | collective-permute-start | bytes 614408 | tf_op jit(solution)/shard_map/ppermute | solution.py:93
  54.9 6.4 %copy-start.9 = (f32[101,6,128]{2,1,0:T(8,128)S(1)}, f32[101,6,128]{2,1,0:T(8,128)}, u32[]{:S(2)}) copy-start(f32[101,6,128]{2,1,0:T(8,128)} %copy-done.8) | copy-start | bytes 930820
  54.9 6.4 %copy-start.4 = (f32[50,16,128]{2,1,0:T(8,128)S(1)}, f32[50,16,128]{2,1,0:T(8,128)}, u32[]{:S(2)}) copy-start(f32[50,16,128]{2,1,0:T(8,128)} %param.21) | copy-start | bytes 1228804
  54.9 6.4 %copy-start.7 = (f32[50,6,128]{2,1,0:T(8,128)S(1)}, f32[50,6,128]{2,1,0:T(8,128)}, u32[]{:S(2)}) copy-start(f32[50,6,128]{2,1,0:T(8,128)} %get-tuple-element.34) | copy-start | bytes 460804
  54.9 6.4 %copy-start.20 = (f32[50]{0:T(128)S(1)}, f32[50]{0:T(128)}, u32[]{:S(2)}) copy-start(f32[50]{0:T(128)} %param.23) | copy-start | bytes 604
  55.1 21.9 %collective-permute-start.6 = (f32[250,6,128]{2,0,1:T(8,128)S(1)}, f32[250,6,128]{2,0,1:T(8,128)S(1)}, u32[]{:S(2)}, u32[]{:S(2)}) collective-permute-start(f32[250,6,128]{2,0,1:T(8,128)S(1)} %copy.23), channel_id=1, source_target_pairs={{0,1},{1,2},{2,3},{3,4},{4,5},{5,6},{6,7},{7,8},{8,9},{9,10},{10,1... | collective-permute-start | bytes 2304008 | tf_op jit(solution)/shard_map/ppermute | solution.py:146
  55.4 7.8 %copy-start.6 = (f32[50,16,128]{2,1,0:T(8,128)S(1)}, f32[50,16,128]{2,1,0:T(8,128)}, u32[]{:S(2)}) copy-start(f32[50,16,128]{2,1,0:T(8,128)} %param.20) | copy-start | bytes 1228804
  55.4 7.8 %copy-start.21 = (f32[50]{0:T(128)S(1)}, f32[50]{0:T(128)}, u32[]{:S(2)}) copy-start(f32[50]{0:T(128)} %param.22) | copy-start | bytes 604
  55.4 22.1 %collective-permute-start.7 = (f32[250,6,128]{2,0,1:T(8,128)S(1)}, f32[250,6,128]{2,0,1:T(8,128)S(1)}, u32[]{:S(2)}, u32[]{:S(2)}) collective-permute-start(f32[250,6,128]{2,0,1:T(8,128)S(1)} %copy.24), channel_id=1, source_target_pairs={{1,0},{2,1},{3,2},{4,3},{5,4},{6,5},{7,6},{8,7},{9,8},{10,9},{11,1... | collective-permute-start | bytes 2304008 | tf_op jit(solution)/shard_map/ppermute | solution.py:147
  64.9 13.0 %copy-start.1 = (f32[1,50,16,128]{3,2,1,0:T(8,128)S(1)}, f32[1,50,16,128]{3,2,1,0:T(8,128)}, u32[]{:S(2)}) copy-start(f32[1,50,16,128]{3,2,1,0:T(8,128)} %shard_map.141) | copy-start | bytes 1228804
  109.2 0.7 copy-start.14
  109.2 0.7 copy-start.15
  109.2 1.0 copy-start.13
  110.3 2.1 %copy-start.2 = (f32[2,2,50,16,128]{4,3,2,1,0:T(8,128)}, f32[2,2,50,16,128]{4,3,2,1,0:T(8,128)S(1)}, u32[]{:S(2)}) copy-start(f32[2,2,50,16,128]{4,3,2,1,0:T(8,128)S(1)} %fusion.1) | copy-start | bytes 4915204

commit v3 on v2

--- a/solution.py
+++ b/solution.py
@@ -99,42 +99,53 @@
     return rows.reshape(shape)
 
 
-def substep_kernel(adjoint_ref, east_a_ref, east_b_ref, north_a_ref, north_b_ref, out_ref):
-    columns = adjoint_ref.shape[-2]
-    lanes = adjoint_ref.shape[-1]
+def substep_kernel(*refs):
+    count = (len(refs) - 4) // 2
+    field_refs, faces, out_refs = refs[:count], refs[count : count + 4], refs[count + 4 :]
+    east_a_ref, east_b_ref, north_a_ref, north_b_ref = faces
+    columns = field_refs[0].shape[-2]
+    lanes = field_refs[0].shape[-1]
     east_a = east_a_ref[...]
     east_b_behind = pltpu.roll(east_b_ref[...], 1, 1)
     north_a = north_a_ref[...]
     north_b_behind = pltpu.roll(north_b_ref[...], 1, 2)
-    for field in range(adjoint_ref.shape[0]):
-        adjoint = adjoint_ref[field]
-        for repeat in range(SUBSTEPS):
-            ahead = pltpu.roll(adjoint, columns - 1, 1)
-            behind = pltpu.roll(adjoint, 1, 1)
-            north_ahead = pltpu.roll(adjoint, lanes - 1, 2)
-            north_behind = pltpu.roll(adjoint, 1, 2)
-            adjoint = (
-                adjoint
-                - east_a * (adjoint - ahead)
-                - east_b_behind * (behind - adjoint)
-                - (north_a * (adjoint - north_ahead) + north_b_behind * (north_behind - adjoint))
-            )
-        aligned = pltpu.roll(adjoint, columns - SUBSTEPS, 1)
-        out_ref[field] = aligned[:, : out_ref.shape[-2]]
-
-
-def transport_substeps(adjoint, east_a, east_b, north_a, north_b, width):
-    fields, levels, columns, lanes = adjoint.shape
+    for adjoint_ref, out_ref in zip(field_refs, out_refs):
+        for field in range(adjoint_ref.shape[0]):
+            adjoint = adjoint_ref[field]
+            for repeat in range(SUBSTEPS):
+                ahead = pltpu.roll(adjoint, columns - 1, 1)
+                behind = pltpu.roll(adjoint, 1, 1)
+                north_ahead = pltpu.roll(adjoint, lanes - 1, 2)
+                north_behind = pltpu.roll(adjoint, 1, 2)
+                adjoint = (
+                    adjoint
+                    - east_a * (adjoint - ahead)
+                    - east_b_behind * (behind - adjoint)
+                    - (north_a * (adjoint - north_ahead) + north_b_behind * (north_behind - adjoint))
+                )
+            aligned = pltpu.roll(adjoint, columns - SUBSTEPS, 1)
+            out_ref[field] = aligned[:, : out_ref.shape[-2]]
+
+
+def transport_substeps(adjoints, east_a, east_b, north_a, north_b, width):
+    levels, columns, lanes = adjoints[0].shape[1:]
     chunk = 5 if levels % 5 == 0 else levels
-    field_block = pl.BlockSpec((fields, chunk, columns, lanes), lambda j: (0, j, 0, 0))
     face_block = pl.BlockSpec((chunk, columns, lanes), lambda j: (j, 0, 0))
+    in_blocks = [
+        pl.BlockSpec((a.shape[0], chunk, columns, lanes), lambda j: (0, j, 0, 0)) for a in adjoints
+    ]
+    out_blocks = [
+        pl.BlockSpec((a.shape[0], chunk, width, lanes), lambda j: (0, j, 0, 0)) for a in adjoints
+    ]
     return pl.pallas_call(
         substep_kernel,
         grid=(levels // chunk,),
-        in_specs=[field_block, face_block, face_block, face_block, face_block],
-        out_specs=pl.BlockSpec((fields, chunk, width, lanes), lambda j: (0, j, 0, 0)),
-        out_shape=jax.ShapeDtypeStruct((fields, levels, width, lanes), jnp.float32),
-    )(adjoint, east_a, east_b, north_a, north_b)
+        in_specs=in_blocks + [face_block] * 4,
+        out_specs=out_blocks,
+        out_shape=[
+            jax.ShapeDtypeStruct((a.shape[0], levels, width, lanes), jnp.float32) for a in adjoints
+        ],
+    )(*adjoints, east_a, east_b, north_a, north_b)
 
 
 def padded_halo(pieces, width, halo, padded):
@@ -192,12 +203,10 @@
 
     below_band, diagonal, above_band = column_coefficients(vertical_mix, thickness, wet_cube)
     adjoint = transposed_solve(adjoint_in, below_band, diagonal, above_band)
+    fields = adjoint_in.shape[0] * adjoint_in.shape[1]
+    (adjoint,) = padded_halo([adjoint.reshape((-1, width, lanes))], width, halo, padded)
     combined = transposed_solve(combined[None], below_band, diagonal, above_band)
-    fields = adjoint_in.shape[0] * adjoint_in.shape[1]
-    stacked = jnp.concatenate(
-        [adjoint.reshape((fields, levels, width, lanes)), combined], 0
-    )
-    (stacked,) = padded_halo([stacked.reshape((-1, width, lanes))], width, halo, padded)
+    (combined,) = padded_halo([combined[0]], width, halo, padded)
 
     east_a, east_b = face_pairs(
         wide_east, wide_wet, jnp.roll(wide_wet, -1, axis=1), east_diffusion
@@ -206,16 +215,16 @@
     north_next = jnp.concatenate([wide_wet[..., 1:], zero_row], -1)
     north_a, north_b = face_pairs(wide_north, wide_wet, north_next, north_diffusion)
 
-    stacked = transport_substeps(
-        stacked.reshape((fields + 1, levels, padded, lanes)),
+    adjoint, summed = transport_substeps(
+        [adjoint.reshape((fields, levels, padded, lanes)), combined[None]],
         east_a,
         east_b,
         north_a,
         north_b,
         width,
     )
-    adjoint = stacked[:fields].reshape(adjoint_in.shape)
-    summed = stacked[fields]
+    adjoint = adjoint.reshape(adjoint_in.shape)
+    summed = summed[0]
     rate_gradient = export_flux * wet_cube * summed
     slope_carbon, slope_alkalinity = carbonate_slopes(surface_carbon, surface_alkalinity)
     exchange_scale = wet_cube[0] * piston * adjoint[:, 0, 0]

time: 114 us -> 118 us (1.035)
  local copies, waits for them, and re-layouts: 5.9 us -> 16.8 us
  starting transfers between devices: 29.2 us -> 25.6 us
  waiting for transfers between devices: 27.1 us -> 24.9 us
    ppermute x3, waiting for transfers between devices: 11.2 us -> 7.55 us  [scenario_sum(): other = lax.ppermute(rows, 'scen', pairs)]
    ppermute x2 -> x3, waiting for transfers between devices: 0.01 us -> 3.42 us  [padded_halo(): after = lax.ppermute(initial, 'grid', down)]
    ppermute x2 -> x3, waiting for transfers between devices: 12.1 us -> 8.67 us  [padded_halo(): before = lax.ppermute(last, 'grid', up)]
    ppermute x3, starting transfers between devices: 8.29 us -> 5.36 us  [scenario_sum(): other = lax.ppermute(rows, 'scen', pairs)]
    slice x3 -> x4, local copies, waits for them, and re-layouts: 0.2 us -> 2.61 us  [padded_halo(): last = jnp.concatenate([piece[:, width - halo:] for piece in pieces], 0)]
    unnamed x47 -> x37, local copies, waits for them, and re-layouts: 1.34 us -> 3.28 us
    slice x2, local copies, waits for them, and re-layouts: 0.71 us -> 2.42 us  [padded_halo(): before[offset:offset + rows]]
    slice x2, local copies, waits for them, and re-layouts: 0.03 us -> 1.74 us  [padded_halo(): after[offset:offset + rows]]
  transfers between devices with their start and end apart: 10 -> 12, of which waited for: 5 -> 9; matrix products, arithmetic and copies ran while one was open for 9% -> 13% of each run, Pallas kernels for 3% -> 0%
where the time goes in v3:
time: 118 us; the launch traced here: 117 us
  Pallas kernels  33.3 us (28%)
  starting transfers between devices  25.6 us (22%)
  waiting for transfers between devices  24.9 us (21%)
  local copies, waits for them, and re-layouts  16.8 us (14%)
  other arithmetic  15.3 us (13%)
    pallas_call x1, Pallas kernels, transport_substeps(): pl.pallas_call(substep_kernel, grid=(levels // chunk,), in_specs=in_block...  27 us
    ppermute x3, starting transfers between devices, padded_halo(): after = lax.ppermute(initial, 'grid', down)  11.5 us
    ppermute x3, waiting for transfers between devices, padded_halo(): before = lax.ppermute(last, 'grid', up)  8.67 us
    ppermute x3, starting transfers between devices, scenario_sum(): rows = keep + lax.ppermute(send, 'scen', pairs)  8.14 us
    ppermute x3, waiting for transfers between devices, scenario_sum(): other = lax.ppermute(rows, 'scen', pairs)  7.55 us
    pallas_call x2, Pallas kernels, transposed_solve(): pl.pallas_call(solve_kernel, out_shape=jax.ShapeDtypeStruct(rhs.shape, jn...  6.29 us
    ppermute x3, starting transfers between devices, scenario_sum(): other = lax.ppermute(rows, 'scen', pairs)  5.36 us
    ppermute x3, waiting for transfers between devices, scenario_sum(): rows = keep + lax.ppermute(send, 'scen', pairs)  5.25 us
  transfers between devices with their start and end apart: 12, of which 9 were waited for; matrix products, arithmetic and copies ran while one was open for 13% of the time, Pallas kernels for 0%

profile of v3, /device:TPU:8, one launch (start us, length us, event | category | flops | bytes accessed | tf_op | source)
XLA Modules:
  0.0 116.9 jit_solution(9516796893795369474)
XLA Ops:
  0.6 0.8 fusion.14
  1.4 1.3 %fusion.13 = (f32[1]{0:T(128)}, f32[1]{0:T(128)}) fusion(f32[50]{0:T(128)} %param.25), kind=kLoop, calls=%fused_computation.54 | loop fusion | bytes 16 | tf_op jit(solution)/shard_map/slice | solution.py:27
  2.8 0.7 select_convert_fusion
  3.7 1.4 %pad_maximum_fusion.2 = (f32[50]{0:T(128)S(1)}, f32[50]{0:T(128)S(1)}) fusion(f32[49]{0:T(128)S(1)} %get-tuple-element.57, f32[1]{0:T(128)} %get-tuple-element.55, f32[1]{0:T(128)} %get-tuple-element.56, f32[49]{0:T(128)S(1)} %get-tuple-element.58), kind=kLoop, calls=%fused_computation.44 | loop fusion | flops 100 | bytes 800 | tf_op jit(solution)/shard_map/concatenate | solution.py:27
  5.0 0.9 negate_divide_fusion
  6.0 1.1 divide_add_fusion
  7.0 3.5 %shard_map.140 = f32[4,50,16,128]{3,2,1,0:T(8,128)} custom-call(f32[4,50,16,128]{3,2,1,0:T(8,128)} %bitcast.43, f32[50,16,128]{2,1,0:T(8,128)} %get-tuple-element.51.below_ref, f32[50,16,128]{2,1,0:T(8,128)} %get-tuple-element.50.diagonal_ref, f32[50,16,128]{2,1,0:T(8,128)} %get-tuple-element.30.above_ref), custom_call_target="tpu_custom_call" | custom-call | tf_op jit(solution)/shard_map/pallas_call | solution.py:56
  10.5 1.5 %fusion.6 = (f32[200,6,128]{2,1,0:T(8,128)S(1)}, f32[200,6,128]{2,1,0:T(8,128)S(1)}) fusion(f32[200,16,128]{2,1,0:T(8,128)} %bitcast.42), kind=kLoop, calls=%fused_computation.47 | loop fusion | bytes 2457600 | tf_op jit(solution)/shard_map/slice | solution.py:155
  12.1 6.3 %collective-permute-start.1 = (f32[200,6,128]{2,0,1:T(8,128)S(1)}, f32[200,6,128]{2,0,1:T(8,128)}, u32[]{:S(2)}, u32[]{:S(2)}) collective-permute-start(f32[200,6,128]{2,0,1:T(8,128)S(1)} %copy.24), channel_id=1, source_target_pairs={{1,0},{2,1},{3,2},{4,3},{5,4},{6,5},{7,6},{8,7},{9,8},{10,9},{11,1... | collective-permute-start | bytes 1843208 | tf_op jit(solution)/shard_map/ppermute | solution.py:158
  18.5 0.9 copy.23
  19.6 0.5 collective-permute-start.2
  20.1 0.3 copy-done.4
  20.4 0.1 copy-done.5
  20.6 5.1 %collective-permute-start.11 = (f32[101,6,128]{2,1,0:T(8,128)S(1)}, f32[101,6,128]{2,1,0:T(8,128)}, u32[]{:S(2)}, u32[]{:S(2)}) collective-permute-start(f32[101,6,128]{2,1,0:T(8,128)S(1)} %pad_maximum_fusion.1), channel_id=1, source_target_pairs={{1,0},{2,1},{3,2},{4,3},{5,4},{6,5},{7,6},{8,7},{9,8},{10,9},{11,1... | collective-permute-start | bytes 930824 | tf_op jit(solution)/shard_map/ppermute | solution.py:158
  25.9 3.0 %collective-permute-start.3 = (f32[200,128]{1,0:T(8,128)S(1)}, f32[200,128]{1,0:T(8,128)S(1)}, u32[]{:S(2)}, u32[]{:S(2)}) collective-permute-start(f32[200,128]{1,0:T(8,128)S(1)} %slice_select_fusion.2), channel_id=1, source_target_pairs={{0,128},{32,160},{64,192},{96,224},{128,0},{160,32},{192,64},{224,... | collective-permute-start | bytes 307208 | tf_op jit(solution)/shard_map/ppermute | solution.py:89
  29.1 3.1 %collective-permute-done.3 = f32[200,128]{1,0:T(8,128)S(1)} collective-permute-done((f32[200,128]{1,0:T(8,128)S(1)}, f32[200,128]{1,0:T(8,128)S(1)}, u32[]{:S(2)}, u32[]{:S(2)}) %collective-permute-start.3) | collective-permute-done | bytes 102432 | tf_op jit(solution)/shard_map/ppermute | solution.py:89
  32.2 4.6 %collective-permute-start.4 = (f32[100,128]{1,0:T(8,128)S(1)}, f32[100,128]{1,0:T(8,128)S(1)}, u32[]{:S(2)}, u32[]{:S(2)}) collective-permute-start(f32[100,128]{1,0:T(8,128)S(1)} %slice_select_fusion.3), channel_id=1, source_target_pairs={{0,32},{32,0},{64,96},{96,64},{128,160},{160,128},{192,224},{224,1... | collective-permute-start | bytes 153608 | tf_op jit(solution)/shard_map/ppermute | solution.py:89
  36.8 2.2 %collective-permute-done.11 = f32[101,6,128]{2,1,0:T(8,128)} collective-permute-done((f32[101,6,128]{2,1,0:T(8,128)S(1)}, f32[101,6,128]{2,1,0:T(8,128)}, u32[]{:S(2)}, u32[]{:S(2)}) %collective-permute-start.11) | collective-permute-done | bytes 310304 | tf_op jit(solution)/shard_map/ppermute | solution.py:158
  39.0 0.7 slice.237
  39.7 4.6 %collective-permute-done.10 = f32[101,6,128]{2,1,0:T(8,128)} collective-permute-done((f32[101,6,128]{2,1,0:T(8,128)S(1)}, f32[101,6,128]{2,1,0:T(8,128)}, u32[]{:S(2)}, u32[]{:S(2)}) %collective-permute-start.10) | collective-permute-done | bytes 310304 | tf_op jit(solution)/shard_map/ppermute | solution.py:157
  44.3 0.7 slice.235
  45.2 2.1 %collective-permute-done.4 = f32[100,128]{1,0:T(8,128)S(1)} collective-permute-done((f32[100,128]{1,0:T(8,128)S(1)}, f32[100,128]{1,0:T(8,128)S(1)}, u32[]{:S(2)}, u32[]{:S(2)}) %collective-permute-start.4) | collective-permute-done | bytes 51232 | tf_op jit(solution)/shard_map/ppermute | solution.py:89
  47.3 2.9 %collective-permute-start.5 = (f32[100,128]{1,0:T(8,128)S(1)}, f32[100,128]{1,0:T(8,128)S(1)}, u32[]{:S(2)}, u32[]{:S(2)}) collective-permute-start(f32[100,128]{1,0:T(8,128)S(1)} %select_add_fusion.1), channel_id=1, source_target_pairs={{0,32},{32,0},{64,96},{96,64},{128,160},{160,128},{192,224},{224,1... | collective-permute-start | bytes 153608 | tf_op jit(solution)/shard_map/ppermute | solution.py:93
  50.2 1.1 fusion.8
  51.2 4.2 %collective-permute-done.5 = f32[100,128]{1,0:T(8,128)S(1)} collective-permute-done((f32[100,128]{1,0:T(8,128)S(1)}, f32[100,128]{1,0:T(8,128)S(1)}, u32[]{:S(2)}, u32[]{:S(2)}) %collective-permute-start.5) | collective-permute-done | bytes 51232 | tf_op jit(solution)/shard_map/ppermute | solution.py:93
  55.5 2.4 %collective-permute-start.6 = (f32[200,128]{1,0:T(8,128)S(1)}, f32[200,128]{1,0:T(8,128)S(1)}, u32[]{:S(2)}, u32[]{:S(2)}) collective-permute-start(f32[200,128]{1,0:T(8,128)S(1)} %maximum_select_fusion.2), channel_id=1, source_target_pairs={{0,128},{32,160},{64,192},{96,224},{128,0},{160,32},{192,64},{224,... | collective-permute-start | bytes 307208 | tf_op jit(solution)/shard_map/ppermute | solution.py:93
  57.8 1.8 %fusion.7 = (f32[50,6,128]{2,1,0:T(8,128)}, f32[50,6,128]{2,1,0:T(8,128)S(1)}) fusion(f32[101,6,128]{2,1,0:T(8,128)} %collective-permute-done.10), kind=kLoop, calls=%fused_computation.48 | loop fusion | bytes 614400 | tf_op jit(solution)/shard_map/slice | solution.py:166
  59.6 0.3 slice.242
  60.0 2.8 %collective-permute-done.6 = f32[200,128]{1,0:T(8,128)S(1)} collective-permute-done((f32[200,128]{1,0:T(8,128)S(1)}, f32[200,128]{1,0:T(8,128)S(1)}, u32[]{:S(2)}, u32[]{:S(2)}) %collective-permute-start.6) | collective-permute-done | bytes 102432 | tf_op jit(solution)/shard_map/ppermute | solution.py:93
  62.9 1.8 %minimum_subtract_fusion.1 = (f32[50,32,128]{2,1,0:T(8,128)}, f32[50,32,128]{2,1,0:T(8,128)}) fusion(f32[32]{0:T(128)S(1)} %pad.50.clone, f32[50,6,128]{2,1,0:T(8,128)S(1)} %get-tuple-element.41, f32[50,16,128]{2,1,0:T(8,128)S(1)} %copy-done.4, f32[50,6,128]{2,1,0:T(8,128)S(1)} %get-tuple-element.39, f32[50,1,128]{2,1,0:T(1,128)S(1)} %slice.239, ...), kind=kLoop, calls=%fused_computation.9 | loop fusion | flops 2457600 | bytes 3191312 | tf_op jit(solution)/shard_map/sub | solution.py:18
  64.7 1.2 %copy.20 = f32[200,6,128]{2,1,0:T(8,128)S(1)} copy(f32[200,6,128]{2,0,1:T(8,128)} %collective-permute-done.1) | data formatting | bytes 1228800 | tf_op jit(solution)/shard_map/ppermute | solution.py:158
  66.0 2.1 %copy.18 = f32[200,6,128]{2,1,0:T(8,128)} copy(f32[200,6,128]{2,0,1:T(8,128)} %collective-permute-done) | data formatting | bytes 1228800 | tf_op jit(solution)/shard_map/ppermute | solution.py:157
  68.1 0.6 collective-permute-done.7
  68.7 0.8 maximum_select_fusion
  69.4 2.8 %shard_map.141 = f32[1,50,16,128]{3,2,1,0:T(8,128)} custom-call(f32[1,50,16,128]{3,2,1,0:T(8,128)} %bitcast.52, f32[50,16,128]{2,1,0:T(8,128)} %get-tuple-element.51.below_ref, f32[50,16,128]{2,1,0:T(8,128)} %get-tuple-element.50.diagonal_ref, f32[50,16,128]{2,1,0:T(8,128)} %get-tuple-element.30.above_ref), custom_call_target="tpu_custom_call" | custom-call | tf_op jit(solution)/shard_map/pallas_call | solution.py:56
  72.2 1.1 fusion.11
  73.4 0.5 collective-permute-start.8
  73.9 3.5 %maximum_maximum_fusion.refs_0_ = f32[4,50,32,128]{3,2,1,0:T(8,128)} fusion(f32[4,50,6,128]{3,2,1,0:T(8,128)S(1)} %bitcast.46, f32[4,50,16,128]{3,2,1,0:T(8,128)S(1)} %copy-done, f32[4,50,6,128]{3,2,1,0:T(8,128)} %bitcast.47, f32[32]{0:T(128)S(1)} %pad.50.clone), kind=kLoop, calls=%fused_computation | loop fusion | flops 2457600 | bytes 6144128 | tf_op jit(solution)/shard_map/concatenate | solution.py:165
  77.5 1.2 %collective-permute-done.9 = f32[50,6,128]{2,1,0:T(8,128)S(1)} collective-permute-done((f32[50,6,128]{2,1,0:T(8,128)S(1)}, f32[50,6,128]{2,1,0:T(8,128)S(1)}, u32[]{:S(2)}, u32[]{:S(2)}) %collective-permute-start.9) | collective-permute-done | bytes 153632 | tf_op jit(solution)/shard_map/ppermute | solution.py:158
  78.7 4.1 %collective-permute-done.8 = f32[50,6,128]{2,1,0:T(8,128)S(1)} collective-permute-done((f32[50,6,128]{2,1,0:T(8,128)S(1)}, f32[50,6,128]{2,1,0:T(8,128)S(1)}, u32[]{:S(2)}, u32[]{:S(2)}) %collective-permute-start.8) | collective-permute-done | bytes 153632 | tf_op jit(solution)/shard_map/ppermute | solution.py:157
  82.8 2.0 %minimum_subtract_fusion = (f32[50,32,128]{2,1,0:T(8,128)}, f32[50,32,128]{2,1,0:T(8,128)}, f32[1,50,32,128]{3,2,1,0:T(8,128)}) fusion(f32[50,32,127]{2,1,0:T(8,128)S(1)} %slice.242, f32[50,6,128]{2,1,0:T(8,128)S(1)} %get-tuple-element.40, f32[50,16,128]{2,1,0:T(8,128)S(1)} %copy-done.6, f32[50,6,128]{2,1,0:T(8,128)S(1)} %copy-done.7, f32[32]{0:T(128)S(1)} %pad.50.clone, ...), kind=kLoop, calls=%fused_computation.7 | loop fusion | flops 2867200 | bytes 4720912 | tf_op jit(solution)/shard_map/sub | solution.py:18
  84.8 27.0 %shard_map.142 = (f32[4,50,16,128]{3,2,1,0:T(8,128)}, f32[1,50,16,128]{3,2,1,0:T(8,128)}) custom-call(f32[4,50,32,128]{3,2,1,0:T(8,128)} %maximum_maximum_fusion.refs_0_, f32[1,50,32,128]{3,2,1,0:T(8,128)} %get-tuple-element.54.refs_1_, f32[50,32,128]{2,1,0:T(8,128)} %get-tuple-element.33.refs_2_, f32[50,32,128]{2,1,0:T(8,128)} %get-tuple-element.32.refs_3_, ...), custom_call_target="tpu_custom_call" | custom-call | tf_op jit(solution)/shard_map/pallas_call | solution.py:140
  111.8 1.5 %copy.26 = f32[2,2,50,16,128]{4,3,2,1,0:T(8,128)S(1)} copy(f32[2,2,50,16,128]{4,3,2,1,0:T(8,128)} %bitcast.48) | data formatting | bytes 3276800
  113.3 0.7 slice.245
  114.1 0.7 fusion.2
  114.8 0.7 fusion.1
  115.6 1.0 fusion
  116.6 0.3 copy-done.3
  (64 shorter events, 1.5 us)
Async XLA Ops:
  0.6 4.4 %copy-start.8 = (f32[50,16,128]{2,1,0:T(8,128)S(1)}, f32[50,16,128]{2,1,0:T(8,128)}, u32[]{:S(2)}) copy-start(f32[50,16,128]{2,1,0:T(8,128)} %param.24) | copy-start | bytes 1228804
  3.6 2.3 %copy-start.13 = (f32[50]{0:T(128)S(1)}, f32[50]{0:T(128)}, u32[]{:S(2)}) copy-start(f32[50]{0:T(128)} %param.25) | copy-start | bytes 604
  12.0 7.4 %copy-start.1 = (f32[2,2,50,16,128]{4,3,2,1,0:T(8,128)S(1)}, f32[2,2,50,16,128]{4,3,2,1,0:T(8,128)}, u32[]{:S(2)}) copy-start(f32[2,2,50,16,128]{4,3,2,1,0:T(8,128)} %param.17) | copy-start | bytes 4915204
  12.1 52.6 %collective-permute-start.1 = (f32[200,6,128]{2,0,1:T(8,128)S(1)}, f32[200,6,128]{2,0,1:T(8,128)}, u32[]{:S(2)}, u32[]{:S(2)}) collective-permute-start(f32[200,6,128]{2,0,1:T(8,128)S(1)} %copy.24), channel_id=1, source_target_pairs={{1,0},{2,1},{3,2},{4,3},{5,4},{6,5},{7,6},{8,7},{9,8},{10,9},{11,1... | collective-permute-start | bytes 1843208 | tf_op jit(solution)/shard_map/ppermute | solution.py:158
  19.4 1.0 copy-start.4
  19.4 1.1 copy-start.5
  19.4 46.5 %collective-permute-start = (f32[200,6,128]{2,0,1:T(8,128)}, f32[200,6,128]{2,0,1:T(8,128)}, u32[]{:S(2)}, u32[]{:S(2)}) collective-permute-start(f32[200,6,128]{2,0,1:T(8,128)} %copy.23), channel_id=1, source_target_pairs={{0,1},{1,2},{2,3},{3,4},{4,5},{5,6},{6,7},{7,8},{8,9},{9,10},{10,1... | collective-permute-start | bytes 1843208 | tf_op jit(solution)/shard_map/ppermute | solution.py:157
  19.6 6.3 %collective-permute-start.2 = (f32[400,128]{1,0:T(8,128)S(1)}, f32[400,128]{1,0:T(8,128)S(1)}, u32[]{:S(2)}, u32[]{:S(2)}) collective-permute-start(f32[400,128]{1,0:T(8,128)S(1)} %bitcast.55), channel_id=1, source_target_pairs={{0,64},{32,96},{64,0},{96,32},{128,192},{160,224},{192,128},{224,1... | collective-permute-start | bytes 614408 | tf_op jit(solution)/shard_map/ppermute | solution.py:89
  20.6 8.4 %copy-start.14 = (f32[16,128]{1,0:T(8,128)S(1)}, f32[16,128]{1,0:T(8,128)}, u32[]{:S(2)}) copy-start(f32[16,128]{1,0:T(8,128)} %param.27) | copy-start | bytes 24580
  20.6 18.4 %collective-permute-start.11 = (f32[101,6,128]{2,1,0:T(8,128)S(1)}, f32[101,6,128]{2,1,0:T(8,128)}, u32[]{:S(2)}, u32[]{:S(2)}) collective-permute-start(f32[101,6,128]{2,1,0:T(8,128)S(1)} %pad_maximum_fusion.1), channel_id=1, source_target_pairs={{1,0},{2,1},{3,2},{4,3},{5,4},{6,5},{7,6},{8,7},{9,8},{10,9},{11,1... | collective-permute-start | bytes 930824 | tf_op jit(solution)/shard_map/ppermute | solution.py:158
  25.8 18.5 %collective-permute-start.10 = (f32[101,6,128]{2,1,0:T(8,128)S(1)}, f32[101,6,128]{2,1,0:T(8,128)}, u32[]{:S(2)}, u32[]{:S(2)}) collective-permute-start(f32[101,6,128]{2,1,0:T(8,128)S(1)} %pad_maximum_fusion), channel_id=1, source_target_pairs={{0,1},{1,2},{2,3},{3,4},{4,5},{5,6},{6,7},{7,8},{8,9},{9,10},{10,1... | collective-permute-start | bytes 930824 | tf_op jit(solution)/shard_map/ppermute | solution.py:157
  25.9 6.3 %collective-permute-start.3 = (f32[200,128]{1,0:T(8,128)S(1)}, f32[200,128]{1,0:T(8,128)S(1)}, u32[]{:S(2)}, u32[]{:S(2)}) collective-permute-start(f32[200,128]{1,0:T(8,128)S(1)} %slice_select_fusion.2), channel_id=1, source_target_pairs={{0,128},{32,160},{64,192},{96,224},{128,0},{160,32},{192,64},{224,... | collective-permute-start | bytes 307208 | tf_op jit(solution)/shard_map/ppermute | solution.py:89
  32.2 15.0 %collective-permute-start.4 = (f32[100,128]{1,0:T(8,128)S(1)}, f32[100,128]{1,0:T(8,128)S(1)}, u32[]{:S(2)}, u32[]{:S(2)}) collective-permute-start(f32[100,128]{1,0:T(8,128)S(1)} %slice_select_fusion.3), channel_id=1, source_target_pairs={{0,32},{32,0},{64,96},{96,64},{128,160},{160,128},{192,224},{224,1... | collective-permute-start | bytes 153608 | tf_op jit(solution)/shard_map/ppermute | solution.py:89
  47.3 8.1 %collective-permute-start.5 = (f32[100,128]{1,0:T(8,128)S(1)}, f32[100,128]{1,0:T(8,128)S(1)}, u32[]{:S(2)}, u32[]{:S(2)}) collective-permute-start(f32[100,128]{1,0:T(8,128)S(1)} %select_add_fusion.1), channel_id=1, source_target_pairs={{0,32},{32,0},{64,96},{96,64},{128,160},{160,128},{192,224},{224,1... | collective-permute-start | bytes 153608 | tf_op jit(solution)/shard_map/ppermute | solution.py:93
  55.5 7.3 %collective-permute-start.6 = (f32[200,128]{1,0:T(8,128)S(1)}, f32[200,128]{1,0:T(8,128)S(1)}, u32[]{:S(2)}, u32[]{:S(2)}) collective-permute-start(f32[200,128]{1,0:T(8,128)S(1)} %maximum_select_fusion.2), channel_id=1, source_target_pairs={{0,128},{32,160},{64,192},{96,224},{128,0},{160,32},{192,64},{224,... | collective-permute-start | bytes 307208 | tf_op jit(solution)/shard_map/ppermute | solution.py:93
  59.6 3.3 %copy-start.15 = (f32[50]{0:T(128)S(1)}, f32[50]{0:T(128)}, u32[]{:S(2)}) copy-start(f32[50]{0:T(128)} %param.22) | copy-start | bytes 604
  62.8 5.8 %collective-permute-start.7 = (f32[400,128]{1,0:T(8,128)S(1)}, f32[400,128]{1,0:T(8,128)S(1)}, u32[]{:S(2)}, u32[]{:S(2)}) collective-permute-start(f32[400,128]{1,0:T(8,128)S(1)} %maximum_select_fusion.1), channel_id=1, source_target_pairs={{0,64},{32,96},{64,0},{96,32},{128,192},{160,224},{192,128},{224,1... | collective-permute-start | bytes 614408 | tf_op jit(solution)/shard_map/ppermute | solution.py:93
  69.4 4.5 %copy-start = (f32[4,50,16,128]{3,2,1,0:T(8,128)S(1)}, f32[4,50,16,128]{3,2,1,0:T(8,128)}, u32[]{:S(2)}) copy-start(f32[4,50,16,128]{3,2,1,0:T(8,128)} %shard_map.140) | copy-start | bytes 4915204
  73.3 5.4 %collective-permute-start.9 = (f32[50,6,128]{2,1,0:T(8,128)S(1)}, f32[50,6,128]{2,1,0:T(8,128)S(1)}, u32[]{:S(2)}, u32[]{:S(2)}) collective-permute-start(f32[50,6,128]{2,1,0:T(8,128)S(1)} %get-tuple-element.47), channel_id=1, source_target_pairs={{1,0},{2,1},{3,2},{4,3},{5,4},{6,5},{7,6},{8,7},{9,8},{10,9},{11,1... | collective-permute-start | bytes 460808 | tf_op jit(solution)/shard_map/ppermute | solution.py:158
  73.4 9.3 %collective-permute-start.8 = (f32[50,6,128]{2,1,0:T(8,128)S(1)}, f32[50,6,128]{2,1,0:T(8,128)S(1)}, u32[]{:S(2)}, u32[]{:S(2)}) collective-permute-start(f32[50,6,128]{2,1,0:T(8,128)S(1)} %get-tuple-element.46), channel_id=1, source_target_pairs={{0,1},{1,2},{2,3},{3,4},{4,5},{5,6},{6,7},{7,8},{8,9},{9,10},{10,1... | collective-permute-start | bytes 460808 | tf_op jit(solution)/shard_map/ppermute | solution.py:157
  73.9 8.9 %copy-start.2 = (f32[1,50,16,128]{3,2,1,0:T(8,128)S(1)}, f32[1,50,16,128]{3,2,1,0:T(8,128)}, u32[]{:S(2)}) copy-start(f32[1,50,16,128]{3,2,1,0:T(8,128)} %shard_map.141) | copy-start | bytes 1228804
  73.9 8.9 %copy-start.6 = (f32[50,16,128]{2,1,0:T(8,128)S(1)}, f32[50,16,128]{2,1,0:T(8,128)}, u32[]{:S(2)}) copy-start(f32[50,16,128]{2,1,0:T(8,128)} %param.21) | copy-start | bytes 1228804
  73.9 8.9 %copy-start.7 = (f32[50,6,128]{2,1,0:T(8,128)S(1)}, f32[50,6,128]{2,1,0:T(8,128)}, u32[]{:S(2)}) copy-start(f32[50,6,128]{2,1,0:T(8,128)} %get-tuple-element.38) | copy-start | bytes 460804
  73.9 8.9 %copy-start.16 = (f32[50]{0:T(128)S(1)}, f32[50]{0:T(128)}, u32[]{:S(2)}) copy-start(f32[50]{0:T(128)} %param.23) | copy-start | bytes 604
  111.8 3.0 %copy-start.11 = (f32[2,16,128]{2,1,0:T(8,128)S(1)}, f32[2,16,128]{2,1,0:T(8,128)}, u32[]{:S(2)}) copy-start(f32[2,16,128]{2,1,0:T(8,128)} %param.19) | copy-start | bytes 49156
  111.8 3.0 %copy-start.12 = (f32[2,16,128]{2,1,0:T(8,128)S(1)}, f32[2,16,128]{2,1,0:T(8,128)}, u32[]{:S(2)}) copy-start(f32[2,16,128]{2,1,0:T(8,128)} %param.18) | copy-start | bytes 49156
  111.8 3.8 %copy-start.9 = (f32[50,16,128]{2,1,0:T(8,128)S(1)}, f32[50,16,128]{2,1,0:T(8,128)}, u32[]{:S(2)}) copy-start(f32[50,16,128]{2,1,0:T(8,128)} %param.26) | copy-start | bytes 1228804
  111.8 3.8 %copy-start.10 = (f32[1,50,16,128]{3,2,1,0:T(8,128)S(1)}, f32[1,50,16,128]{3,2,1,0:T(8,128)}, u32[]{:S(2)}) copy-start(f32[1,50,16,128]{3,2,1,0:T(8,128)} %get-tuple-element.29) | copy-start | bytes 1228804
  115.5 1.3 %copy-start.3 = (f32[2,2,50,16,128]{4,3,2,1,0:T(8,128)}, f32[2,2,50,16,128]{4,3,2,1,0:T(8,128)S(1)}, u32[]{:S(2)}) copy-start(f32[2,2,50,16,128]{4,3,2,1,0:T(8,128)S(1)} %fusion.1) | copy-start | bytes 4915204

commit v4 on v0

--- a/solution.py
+++ b/solution.py
@@ -106,6 +106,7 @@
     east_b_behind = pltpu.roll(east_b_ref[...], 1, 1)
     north_a = north_a_ref[...]
     north_b_behind = pltpu.roll(north_b_ref[...], 1, 2)
+    centre = 1.0 - east_a + east_b_behind - north_a + north_b_behind
     for field in range(adjoint_ref.shape[0]):
         adjoint = adjoint_ref[field]
         for repeat in range(SUBSTEPS):
@@ -114,10 +115,11 @@
             north_ahead = pltpu.roll(adjoint, lanes - 1, 2)
             north_behind = pltpu.roll(adjoint, 1, 2)
             adjoint = (
-                adjoint
-                - east_a * (adjoint - ahead)
-                - east_b_behind * (behind - adjoint)
-                - (north_a * (adjoint - north_ahead) + north_b_behind * (north_behind - adjoint))
+                centre * adjoint
+                + east_a * ahead
+                - east_b_behind * behind
+                + north_a * north_ahead
+                - north_b_behind * north_behind
             )
         aligned = pltpu.roll(adjoint, columns - SUBSTEPS, 1)
         out_ref[field] = aligned[:, : out_ref.shape[-2]]

time: 107 us -> 107 us (level)
  no operation moved by 1% of the time
where the time goes in v4:
time: 107 us
  waiting for transfers between devices  29.5 us (28%)
  starting transfers between devices  27.7 us (26%)
  Pallas kernels  25.3 us (24%)
  other arithmetic  14.5 us (14%)
  local copies, waits for them, and re-layouts  8.75 us (8%)
    pallas_call x1, Pallas kernels, transport_substeps(): pl.pallas_call(substep_kernel, grid=(levels // chunk,), in_specs=[field_b...  21.8 us
    ppermute x3, waiting for transfers between devices, scenario_sum(): rows = keep + lax.ppermute(send, 'scen', pairs)  12.8 us
    ppermute x2, starting transfers between devices, padded_halo(): after = lax.ppermute(initial, 'grid', down)  12 us
    ppermute x3, waiting for transfers between devices, scenario_sum(): other = lax.ppermute(rows, 'scen', pairs)  11.8 us
    ppermute x3, starting transfers between devices, scenario_sum(): other = lax.ppermute(rows, 'scen', pairs)  8.14 us
    ppermute x3, starting transfers between devices, scenario_sum(): rows = keep + lax.ppermute(send, 'scen', pairs)  7.5 us
    ppermute x2, waiting for transfers between devices, padded_halo(): before = lax.ppermute(last, 'grid', up)  4.78 us
    sub x2, other arithmetic, face_pairs(): jnp.minimum(moving, 0.0) - mixing  3.53 us
  transfers between devices with their start and end apart: 10, of which 7 were waited for; matrix products, arithmetic and copies ran while one was open for 14% of the time, Pallas kernels for 3%

profile of v4, /device:TPU:8, one launch (start us, length us, event | category | flops | bytes accessed | tf_op | source)
XLA Modules:
  0.0 106.6 jit_solution(1495925298328304207)
XLA Ops:
  0.6 0.7 select_convert_fusion
  1.4 1.3 %fusion.11 = (f32[50,6,128]{2,1,0:T(8,128)S(1)}, f32[50,6,128]{2,1,0:T(8,128)S(1)}, f32[50,6,128]{2,1,0:T(8,128)S(1)}, f32[50,6,128]{2,1,0:T(8,128)S(1)}) fusion(f32[50,16,128]{2,1,0:T(8,128)} %param.20, f32[50,16,128]{2,1,0:T(8,128)} %param.21), kind=kLoop, calls=%fused_computation.51 | loop fusion | bytes 1228800 | tf_op jit(solution)/shard_map/slice | solution.py:146
  2.7 0.8 pad_maximum_fusion
  3.5 0.8 pad_maximum_fusion.1
  4.3 6.3 %collective-permute-start.3 = (f32[101,6,128]{2,1,0:T(8,128)}, f32[101,6,128]{2,1,0:T(8,128)}, u32[]{:S(2)}, u32[]{:S(2)}) collective-permute-start(f32[101,6,128]{2,1,0:T(8,128)} %pad_maximum_fusion.1), channel_id=1, source_target_pairs={{1,0},{2,1},{3,2},{4,3},{5,4},{6,5},{7,6},{8,7},{9,8},{10,9},{11,1... | collective-permute-start | bytes 930824 | tf_op jit(solution)/shard_map/ppermute | solution.py:149
  10.6 0.6 fusion.14
  11.2 0.1 compare_convert_fusion.1
  11.4 1.4 %pad_maximum_fusion.2 = (f32[50]{0:T(128)S(1)}, f32[50]{0:T(128)S(1)}) fusion(f32[49]{0:T(128)S(1)} %get-tuple-element.50, f32[1]{0:T(128)} %get-tuple-element.48, f32[1]{0:T(128)} %get-tuple-element.49, f32[49]{0:T(128)S(1)} %get-tuple-element.51), kind=kLoop, calls=%fused_computation.45 | loop fusion | flops 100 | bytes 800 | tf_op jit(solution)/shard_map/concatenate | solution.py:27
  12.8 0.9 negate_divide_fusion
  13.7 1.1 divide_add_fusion
  14.7 3.5 %shard_map.140 = f32[4,50,16,128]{3,2,1,0:T(8,128)} custom-call(f32[4,50,16,128]{3,2,1,0:T(8,128)} %bitcast.45, f32[50,16,128]{2,1,0:T(8,128)} %get-tuple-element.45.below_ref, f32[50,16,128]{2,1,0:T(8,128)} %get-tuple-element.44.diagonal_ref, f32[50,16,128]{2,1,0:T(8,128)} %get-tuple-element.26.above_ref), custom_call_target="tpu_custom_call" | custom-call | tf_op jit(solution)/shard_map/pallas_call | solution.py:56
  18.2 1.5 %fusion.8 = (f32[200,6,128]{2,1,0:T(8,128)S(1)}, f32[200,6,128]{2,1,0:T(8,128)S(1)}) fusion(f32[200,16,128]{2,1,0:T(8,128)} %bitcast.42), kind=kLoop, calls=%fused_computation.48 | loop fusion | bytes 2457600 | tf_op jit(solution)/shard_map/slice | solution.py:146
  19.7 0.1 copy.23
  19.8 0.1 collective-permute-start
  19.9 0.1 copy.24
  20.1 5.7 %collective-permute-start.1 = (f32[200,6,128]{2,0,1:T(8,128)S(1)}, f32[200,6,128]{2,0,1:T(8,128)S(1)}, u32[]{:S(2)}, u32[]{:S(2)}) collective-permute-start(f32[200,6,128]{2,0,1:T(8,128)S(1)} %copy.24), channel_id=1, source_target_pairs={{1,0},{2,1},{3,2},{4,3},{5,4},{6,5},{7,6},{8,7},{9,8},{10,9},{11,1... | collective-permute-start | bytes 1843208 | tf_op jit(solution)/shard_map/ppermute | solution.py:149
  25.8 0.1 pad.46.clone
  25.8 0.7 slice.219
  26.5 0.7 slice.221
  27.2 0.1 maximum_bitcast_fusion
  27.3 0.1 compare_convert_fusion
  27.4 1.1 fusion.9
  28.5 1.1 fusion.10
  29.6 0.1 slice.222
  29.7 0.3 slice.226
  30.0 0.6 copy-done.3
  30.5 1.8 %minimum_subtract_fusion = (f32[50,32,128]{2,1,0:T(8,128)}, f32[50,32,128]{2,1,0:T(8,128)}) fusion(f32[50,32,127]{2,1,0:T(8,128)S(1)} %slice.226, f32[50,6,128]{2,1,0:T(8,128)S(1)} %get-tuple-element.36, f32[50,16,128]{2,1,0:T(8,128)S(1)} %copy-done.3, f32[50,6,128]{2,1,0:T(8,128)S(1)} %get-tuple-element.34, f32[32]{0:T(128)S(1)} %pad.46.clone, ...), kind=kLoop, calls=%fused_computation.9 | loop fusion | flops 2252800 | bytes 3184912 | tf_op jit(solution)/shard_map/sub | solution.py:18
  32.3 1.8 %minimum_subtract_fusion.1 = (f32[50,32,128]{2,1,0:T(8,128)}, f32[50,32,128]{2,1,0:T(8,128)}) fusion(f32[32]{0:T(128)S(1)} %pad.46.clone, f32[50,6,128]{2,1,0:T(8,128)S(1)} %get-tuple-element.37, f32[50,16,128]{2,1,0:T(8,128)S(1)} %copy-done.4, f32[50,6,128]{2,1,0:T(8,128)S(1)} %get-tuple-element.35, f32[50,1,128]{2,1,0:T(1,128)S(1)} %slice.223, ...), kind=kLoop, calls=%fused_computation.11 | loop fusion | flops 2457600 | bytes 3191312 | tf_op jit(solution)/shard_map/sub | solution.py:18
  34.1 4.8 %collective-permute-done = f32[200,6,128]{2,0,1:T(8,128)S(1)} collective-permute-done((f32[200,6,128]{2,0,1:T(8,128)S(1)}, f32[200,6,128]{2,0,1:T(8,128)S(1)}, u32[]{:S(2)}, u32[]{:S(2)}) %collective-permute-start) | collective-permute-done | bytes 614432 | tf_op jit(solution)/shard_map/ppermute | solution.py:148
  38.9 0.2 copy.18
  39.0 0.2 copy.20
  39.2 2.3 %maximum_maximum_fusion.adjoint_ref = f32[4,50,32,128]{3,2,1,0:T(8,128)} fusion(f32[4,50,6,128]{3,2,1,0:T(8,128)S(1)} %bitcast.44, f32[4,50,16,128]{3,2,1,0:T(8,128)S(1)} %copy-done.1, f32[4,50,6,128]{3,2,1,0:T(8,128)S(1)} %bitcast.43, f32[32]{0:T(128)S(1)} %pad.46.clone), kind=kLoop, calls=%fused_computation | loop fusion | flops 2457600 | bytes 6144128 | tf_op jit(solution)/shard_map/concatenate | solution.py:156
  41.5 21.8 %shard_map.141 = f32[4,50,16,128]{3,2,1,0:T(8,128)} custom-call(f32[4,50,32,128]{3,2,1,0:T(8,128)} %maximum_maximum_fusion.adjoint_ref, f32[50,32,128]{2,1,0:T(8,128)} %get-tuple-element.29.east_a_ref, f32[50,32,128]{2,1,0:T(8,128)} %get-tuple-element.28.east_b_ref, f32[50,32,128]{2,1,0:T(8,128)} %get-tuple-element.31.north_a_ref, ...), custom_call_target="tpu_custom_call" | custom-call | tf_op jit(solution)/shard_map/pallas_call | solution.py:133
  63.3 1.6 %fusion.1 = f32[50,16,128]{2,1,0:T(8,128)S(1)} fusion(f32[2,2,50,16,128]{4,3,2,1,0:T(8,128)} %bitcast.37), kind=kLoop, calls=%fused_computation.6 | loop fusion | flops 512000 | bytes 2048000 | tf_op jit(solution)/shard_map/reduce_sum | solution.py:213
  64.9 0.5 collective-permute-start.4
  65.5 5.3 %collective-permute-done.4 = f32[400,128]{1,0:T(8,128)S(1)} collective-permute-done((f32[400,128]{1,0:T(8,128)S(1)}, f32[400,128]{1,0:T(8,128)S(1)}, u32[]{:S(2)}, u32[]{:S(2)}) %collective-permute-start.4) | collective-permute-done | bytes 204832 | tf_op jit(solution)/shard_map/ppermute | solution.py:89
  70.8 2.4 %collective-permute-start.5 = (f32[200,128]{1,0:T(8,128)S(1)}, f32[200,128]{1,0:T(8,128)S(1)}, u32[]{:S(2)}, u32[]{:S(2)}) collective-permute-start(f32[200,128]{1,0:T(8,128)S(1)} %slice_select_fusion.2), channel_id=1, source_target_pairs={{0,128},{32,160},{64,192},{96,224},{128,0},{160,32},{192,64},{224,... | collective-permute-start | bytes 307208 | tf_op jit(solution)/shard_map/ppermute | solution.py:89
  73.2 3.9 %collective-permute-done.5 = f32[200,128]{1,0:T(8,128)S(1)} collective-permute-done((f32[200,128]{1,0:T(8,128)S(1)}, f32[200,128]{1,0:T(8,128)S(1)}, u32[]{:S(2)}, u32[]{:S(2)}) %collective-permute-start.5) | collective-permute-done | bytes 102432 | tf_op jit(solution)/shard_map/ppermute | solution.py:89
  77.1 4.6 %collective-permute-start.6 = (f32[100,128]{1,0:T(8,128)S(1)}, f32[100,128]{1,0:T(8,128)S(1)}, u32[]{:S(2)}, u32[]{:S(2)}) collective-permute-start(f32[100,128]{1,0:T(8,128)S(1)} %slice_select_fusion.3), channel_id=1, source_target_pairs={{0,32},{32,0},{64,96},{96,64},{128,160},{160,128},{192,224},{224,1... | collective-permute-start | bytes 153608 | tf_op jit(solution)/shard_map/ppermute | solution.py:89
  81.7 3.6 %collective-permute-done.6 = f32[100,128]{1,0:T(8,128)S(1)} collective-permute-done((f32[100,128]{1,0:T(8,128)S(1)}, f32[100,128]{1,0:T(8,128)S(1)}, u32[]{:S(2)}, u32[]{:S(2)}) %collective-permute-start.6) | collective-permute-done | bytes 51232 | tf_op jit(solution)/shard_map/ppermute | solution.py:89
  85.4 5.2 %collective-permute-start.7 = (f32[100,128]{1,0:T(8,128)S(1)}, f32[100,128]{1,0:T(8,128)S(1)}, u32[]{:S(2)}, u32[]{:S(2)}) collective-permute-start(f32[100,128]{1,0:T(8,128)S(1)} %select_add_fusion.1), channel_id=1, source_target_pairs={{0,32},{32,0},{64,96},{96,64},{128,160},{160,128},{192,224},{224,1... | collective-permute-start | bytes 153608 | tf_op jit(solution)/shard_map/ppermute | solution.py:93
  90.6 0.1 copy.26
  90.8 2.7 %collective-permute-done.7 = f32[100,128]{1,0:T(8,128)S(1)} collective-permute-done((f32[100,128]{1,0:T(8,128)S(1)}, f32[100,128]{1,0:T(8,128)S(1)}, u32[]{:S(2)}, u32[]{:S(2)}) %collective-permute-start.7) | collective-permute-done | bytes 51232 | tf_op jit(solution)/shard_map/ppermute | solution.py:93
  93.5 2.4 %collective-permute-start.8 = (f32[200,128]{1,0:T(8,128)S(1)}, f32[200,128]{1,0:T(8,128)S(1)}, u32[]{:S(2)}, u32[]{:S(2)}) collective-permute-start(f32[200,128]{1,0:T(8,128)S(1)} %maximum_select_fusion.2), channel_id=1, source_target_pairs={{0,128},{32,160},{64,192},{96,224},{128,0},{160,32},{192,64},{224,... | collective-permute-start | bytes 307208 | tf_op jit(solution)/shard_map/ppermute | solution.py:93
  95.9 3.8 %collective-permute-done.8 = f32[200,128]{1,0:T(8,128)S(1)} collective-permute-done((f32[200,128]{1,0:T(8,128)S(1)}, f32[200,128]{1,0:T(8,128)S(1)}, u32[]{:S(2)}, u32[]{:S(2)}) %collective-permute-start.8) | collective-permute-done | bytes 102432 | tf_op jit(solution)/shard_map/ppermute | solution.py:93
  99.8 0.5 collective-permute-start.9
  100.4 5.3 %collective-permute-done.9 = f32[400,128]{1,0:T(8,128)S(1)} collective-permute-done((f32[400,128]{1,0:T(8,128)S(1)}, f32[400,128]{1,0:T(8,128)S(1)}, u32[]{:S(2)}, u32[]{:S(2)}) %collective-permute-start.9) | collective-permute-done | bytes 204832 | tf_op jit(solution)/shard_map/ppermute | solution.py:93
  105.7 0.9 fusion.2
  (50 shorter events, 0.5 us)
Async XLA Ops:
  1.4 9.2 %copy-start.9 = (f32[50]{0:T(128)S(1)}, f32[50]{0:T(128)}, u32[]{:S(2)}) copy-start(f32[50]{0:T(128)} %param.25) | copy-start | bytes 604
  2.7 10.1 %copy-start.5 = (f32[50,16,128]{2,1,0:T(8,128)S(1)}, f32[50,16,128]{2,1,0:T(8,128)}, u32[]{:S(2)}) copy-start(f32[50,16,128]{2,1,0:T(8,128)} %param.24) | copy-start | bytes 1228804
  3.5 22.3 %collective-permute-start.2 = (f32[101,6,128]{2,1,0:T(8,128)}, f32[101,6,128]{2,1,0:T(8,128)}, u32[]{:S(2)}, u32[]{:S(2)}) collective-permute-start(f32[101,6,128]{2,1,0:T(8,128)} %pad_maximum_fusion), channel_id=1, source_target_pairs={{0,1},{1,2},{2,3},{3,4},{4,5},{5,6},{6,7},{7,8},{8,9},{9,10},{10,1... | collective-permute-start | bytes 930824 | tf_op jit(solution)/shard_map/ppermute | solution.py:148
  4.3 22.2 %collective-permute-start.3 = (f32[101,6,128]{2,1,0:T(8,128)}, f32[101,6,128]{2,1,0:T(8,128)}, u32[]{:S(2)}, u32[]{:S(2)}) collective-permute-start(f32[101,6,128]{2,1,0:T(8,128)} %pad_maximum_fusion.1), channel_id=1, source_target_pairs={{1,0},{2,1},{3,2},{4,3},{5,4},{6,5},{7,6},{8,7},{9,8},{10,9},{11,1... | collective-permute-start | bytes 930824 | tf_op jit(solution)/shard_map/ppermute | solution.py:149
  19.8 19.0 %collective-permute-start = (f32[200,6,128]{2,0,1:T(8,128)S(1)}, f32[200,6,128]{2,0,1:T(8,128)S(1)}, u32[]{:S(2)}, u32[]{:S(2)}) collective-permute-start(f32[200,6,128]{2,0,1:T(8,128)S(1)} %copy.23), channel_id=1, source_target_pairs={{0,1},{1,2},{2,3},{3,4},{4,5},{5,6},{6,7},{7,8},{8,9},{9,10},{10,1... | collective-permute-start | bytes 1843208 | tf_op jit(solution)/shard_map/ppermute | solution.py:148
  20.1 19.0 %collective-permute-start.1 = (f32[200,6,128]{2,0,1:T(8,128)S(1)}, f32[200,6,128]{2,0,1:T(8,128)S(1)}, u32[]{:S(2)}, u32[]{:S(2)}) collective-permute-start(f32[200,6,128]{2,0,1:T(8,128)S(1)} %copy.24), channel_id=1, source_target_pairs={{1,0},{2,1},{3,2},{4,3},{5,4},{6,5},{7,6},{8,7},{9,8},{10,9},{11,1... | collective-permute-start | bytes 1843208 | tf_op jit(solution)/shard_map/ppermute | solution.py:149
  29.5 1.0 copy-start.3
  29.5 1.0 copy-start.11
  30.5 1.8 %copy-start.4 = (f32[50,16,128]{2,1,0:T(8,128)S(1)}, f32[50,16,128]{2,1,0:T(8,128)}, u32[]{:S(2)}) copy-start(f32[50,16,128]{2,1,0:T(8,128)} %param.20) | copy-start | bytes 1228804
  30.5 1.8 %copy-start.12 = (f32[50]{0:T(128)S(1)}, f32[50]{0:T(128)}, u32[]{:S(2)}) copy-start(f32[50]{0:T(128)} %param.22) | copy-start | bytes 604
  34.1 5.1 %copy-start.1 = (f32[4,50,16,128]{3,2,1,0:T(8,128)S(1)}, f32[4,50,16,128]{3,2,1,0:T(8,128)}, u32[]{:S(2)}) copy-start(f32[4,50,16,128]{3,2,1,0:T(8,128)} %shard_map.140) | copy-start | bytes 4915204
  64.9 16.8 %copy-start.10 = (f32[16,128]{1,0:T(8,128)S(1)}, f32[16,128]{1,0:T(8,128)}, u32[]{:S(2)}) copy-start(f32[16,128]{1,0:T(8,128)} %param.27) | copy-start | bytes 24580
  64.9 25.7 %copy-start = (f32[4,50,16,128]{3,2,1,0:T(8,128)S(1)}, f32[4,50,16,128]{3,2,1,0:T(8,128)}, u32[]{:S(2)}) copy-start(f32[4,50,16,128]{3,2,1,0:T(8,128)} %shard_map.141) | copy-start | bytes 4915204
  64.9 5.8 %collective-permute-start.4 = (f32[400,128]{1,0:T(8,128)S(1)}, f32[400,128]{1,0:T(8,128)S(1)}, u32[]{:S(2)}, u32[]{:S(2)}) collective-permute-start(f32[400,128]{1,0:T(8,128)S(1)} %bitcast.49), channel_id=1, source_target_pairs={{0,64},{32,96},{64,0},{96,32},{128,192},{160,224},{192,128},{224,1... | collective-permute-start | bytes 614408 | tf_op jit(solution)/shard_map/ppermute | solution.py:89
  70.8 6.3 %collective-permute-start.5 = (f32[200,128]{1,0:T(8,128)S(1)}, f32[200,128]{1,0:T(8,128)S(1)}, u32[]{:S(2)}, u32[]{:S(2)}) collective-permute-start(f32[200,128]{1,0:T(8,128)S(1)} %slice_select_fusion.2), channel_id=1, source_target_pairs={{0,128},{32,160},{64,192},{96,224},{128,0},{160,32},{192,64},{224,... | collective-permute-start | bytes 307208 | tf_op jit(solution)/shard_map/ppermute | solution.py:89
  77.1 8.2 %collective-permute-start.6 = (f32[100,128]{1,0:T(8,128)S(1)}, f32[100,128]{1,0:T(8,128)S(1)}, u32[]{:S(2)}, u32[]{:S(2)}) collective-permute-start(f32[100,128]{1,0:T(8,128)S(1)} %slice_select_fusion.3), channel_id=1, source_target_pairs={{0,32},{32,0},{64,96},{96,64},{128,160},{160,128},{192,224},{224,1... | collective-permute-start | bytes 153608 | tf_op jit(solution)/shard_map/ppermute | solution.py:89
  85.4 8.1 %collective-permute-start.7 = (f32[100,128]{1,0:T(8,128)S(1)}, f32[100,128]{1,0:T(8,128)S(1)}, u32[]{:S(2)}, u32[]{:S(2)}) collective-permute-start(f32[100,128]{1,0:T(8,128)S(1)} %select_add_fusion.1), channel_id=1, source_target_pairs={{0,32},{32,0},{64,96},{96,64},{128,160},{160,128},{192,224},{224,1... | collective-permute-start | bytes 153608 | tf_op jit(solution)/shard_map/ppermute | solution.py:93
  90.6 5.3 %copy-start.7 = (f32[2,16,128]{2,1,0:T(8,128)S(1)}, f32[2,16,128]{2,1,0:T(8,128)}, u32[]{:S(2)}) copy-start(f32[2,16,128]{2,1,0:T(8,128)} %param.19) | copy-start | bytes 49156
  90.6 5.3 %copy-start.8 = (f32[2,16,128]{2,1,0:T(8,128)S(1)}, f32[2,16,128]{2,1,0:T(8,128)}, u32[]{:S(2)}) copy-start(f32[2,16,128]{2,1,0:T(8,128)} %param.18) | copy-start | bytes 49156
  90.8 14.9 %copy-start.6 = (f32[50,16,128]{2,1,0:T(8,128)S(1)}, f32[50,16,128]{2,1,0:T(8,128)}, u32[]{:S(2)}) copy-start(f32[50,16,128]{2,1,0:T(8,128)} %param.26) | copy-start | bytes 1228804
  93.5 6.3 %collective-permute-start.8 = (f32[200,128]{1,0:T(8,128)S(1)}, f32[200,128]{1,0:T(8,128)S(1)}, u32[]{:S(2)}, u32[]{:S(2)}) collective-permute-start(f32[200,128]{1,0:T(8,128)S(1)} %maximum_select_fusion.2), channel_id=1, source_target_pairs={{0,128},{32,160},{64,192},{96,224},{128,0},{160,32},{192,64},{224,... | collective-permute-start | bytes 307208 | tf_op jit(solution)/shard_map/ppermute | solution.py:93
  99.8 5.8 %collective-permute-start.9 = (f32[400,128]{1,0:T(8,128)S(1)}, f32[400,128]{1,0:T(8,128)S(1)}, u32[]{:S(2)}, u32[]{:S(2)}) collective-permute-start(f32[400,128]{1,0:T(8,128)S(1)} %maximum_select_fusion.1), channel_id=1, source_target_pairs={{0,64},{32,96},{64,0},{96,32},{128,192},{160,224},{192,128},{224,1... | collective-permute-start | bytes 614408 | tf_op jit(solution)/shard_map/ppermute | solution.py:93
  100.4 6.2 %copy-start.2 = (f32[2,2,50,16,128]{4,3,2,1,0:T(8,128)}, f32[2,2,50,16,128]{4,3,2,1,0:T(8,128)S(1)}, u32[]{:S(2)}) copy-start(f32[2,2,50,16,128]{4,3,2,1,0:T(8,128)S(1)} %fusion.3) | copy-start | bytes 4915204

commit v5 on v0

--- a/solution.py
+++ b/solution.py
@@ -73,30 +73,12 @@
 
 def scenario_sum(field):
     size = lax.axis_size("scen")
-    index = lax.axis_index("scen")
     shape = field.shape
-    rows = field.reshape(-1, shape[-1])
-    bits = [b for b in (2, 4, 1) if b < size]
-    bits += [b for b in (8, 16, 32) if b < size]
-    kept_bits = []
-    for bit in bits:
-        half = rows.shape[0] // 2
-        upper = (index // bit) % 2 == 1
-        low, high = rows[:half], rows[half:]
-        keep = jnp.where(upper, high, low)
-        send = jnp.where(upper, low, high)
-        pairs = [(i, i ^ bit) for i in range(size)]
-        rows = keep + lax.ppermute(send, "scen", pairs)
-        kept_bits.append((bit, upper))
-    for bit, upper in kept_bits[::-1]:
-        pairs = [(i, i ^ bit) for i in range(size)]
-        other = lax.ppermute(rows, "scen", pairs)
-        rows = jnp.where(
-            upper,
-            jnp.concatenate([other, rows], 0),
-            jnp.concatenate([rows, other], 0),
-        )
-    return rows.reshape(shape)
+    pieces = field.reshape((size, -1, shape[-1]))
+    gathered = lax.all_to_all(pieces, "scen", 0, 0, tiled=True)
+    owned = jnp.sum(gathered, axis=0)
+    spread = jnp.broadcast_to(owned[None], (size,) + owned.shape)
+    return lax.all_to_all(spread, "scen", 0, 0, tiled=True).reshape(shape)
 
 
 def substep_kernel(adjoint_ref, east_a_ref, east_b_ref, north_a_ref, north_b_ref, out_ref):

time: 107 us -> 101 us (0.944)
  blocking collectives: 0 us -> 19.2 us
  waiting for transfers between devices: 29.5 us -> 15.4 us
  starting transfers between devices: 27.7 us -> 17.3 us
  local copies, waits for them, and re-layouts: 8.75 us -> 7.27 us
    ppermute x6 -> x0, waiting for transfers between devices: 24.7 us -> none  [the longest x3 12.8 us: scenario_sum(): rows = keep + lax.ppermute(send, 'scen', pairs)]
    all_to_all x0 -> x1, blocking collectives: none -> 19.2 us  [scenario_sum(): gathered = lax.all_to_all(pieces, 'scen', 0, 0, tiled=True)]
    ppermute x6 -> x0, starting transfers between devices: 15.6 us -> none  [the longest x3 8.14 us: scenario_sum(): other = lax.ppermute(rows, 'scen', pairs)]
    all_to_all x0 -> x1, waiting for transfers between devices: none -> 7.11 us  [scenario_sum(): return lax.all_to_all(spread, 'scen', 0, 0, tiled=True).reshape(shape)]
    all_to_all x0 -> x1, starting transfers between devices: none -> 5.05 us  [scenario_sum(): return lax.all_to_all(spread, 'scen', 0, 0, tiled=True).reshape(shape)]
    ppermute x2, waiting for transfers between devices: 0.01 us -> 3.43 us  [padded_halo(): after = lax.ppermute(initial, 'grid', down)]
    scatter-add x2, other arithmetic: 0.03 us -> 1.96 us  [on_device(): adjoint = adjoint.at[:, 0, 0].add(-exchange_scale * slope_carbon).at[:, 1...]
    slice x2, local copies, waits for them, and re-layouts: 1.74 us -> 0.03 us  [padded_halo(): after[offset:offset + rows]]
  transfers between devices with their start and end apart: 10 -> 5, of which waited for: 7 -> 3; matrix products, arithmetic and copies ran while one was open for 14% -> 13% of each run, Pallas kernels for 3% -> 3%
where the time goes in v5:
time: 101 us; the launch traced here: 100 us
  Pallas kernels  25.3 us (25%)
  blocking collectives  19.2 us (19%)
  starting transfers between devices  17.3 us (17%)
  waiting for transfers between devices  15.4 us (15%)
  other arithmetic  14.8 us (15%)
  local copies, waits for them, and re-layouts  7.27 us (7%)
    pallas_call x1, Pallas kernels, transport_substeps(): pl.pallas_call(substep_kernel, grid=(levels // chunk,), in_specs=[field_b...  21.8 us
    all_to_all x1, blocking collectives, scenario_sum(): gathered = lax.all_to_all(pieces, 'scen', 0, 0, tiled=True)  19.2 us
    ppermute x2, starting transfers between devices, padded_halo(): after = lax.ppermute(initial, 'grid', down)  12 us
    all_to_all x1, waiting for transfers between devices, scenario_sum(): return lax.all_to_all(spread, 'scen', 0, 0, tiled=True).reshape(shape)  7.11 us
    all_to_all x1, starting transfers between devices, scenario_sum(): return lax.all_to_all(spread, 'scen', 0, 0, tiled=True).reshape(shape)  5.05 us
    ppermute x2, waiting for transfers between devices, padded_halo(): before = lax.ppermute(last, 'grid', up)  4.88 us
    sub x2, other arithmetic, face_pairs(): jnp.minimum(moving, 0.0) - mixing  3.56 us
    pallas_call x1, Pallas kernels, transposed_solve(): pl.pallas_call(solve_kernel, out_shape=jax.ShapeDtypeStruct(rhs.shape, jn...  3.48 us
  transfers between devices with their start and end apart: 5, of which 3 were waited for; matrix products, arithmetic and copies ran while one was open for 13% of the time, Pallas kernels for 3%

profile of v5, /device:TPU:8, one launch (start us, length us, event | category | flops | bytes accessed | tf_op | source)
XLA Modules:
  0.0 100.2 jit_solution(3622646833882684316)
XLA Ops:
  0.6 0.7 select_convert_fusion
  1.4 1.3 %fusion.11 = (f32[50,6,128]{2,1,0:T(8,128)S(1)}, f32[50,6,128]{2,1,0:T(8,128)S(1)}, f32[50,6,128]{2,1,0:T(8,128)S(1)}, f32[50,6,128]{2,1,0:T(8,128)S(1)}) fusion(f32[50,16,128]{2,1,0:T(8,128)} %param.20, f32[50,16,128]{2,1,0:T(8,128)} %param.21), kind=kLoop, calls=%fused_computation.41 | loop fusion | bytes 1228800 | tf_op jit(solution)/shard_map/slice | solution.py:126
  2.7 0.0 copy-start.4
  2.7 6.3 %collective-permute-start.3 = (f32[101,6,128]{2,1,0:T(8,128)S(1)}, f32[101,6,128]{2,1,0:T(8,128)S(1)}, u32[]{:S(2)}, u32[]{:S(2)}) collective-permute-start(f32[101,6,128]{2,1,0:T(8,128)S(1)} %pad_maximum_fusion.1), channel_id=1, source_target_pairs={{1,0},{2,1},{3,2},{4,3},{5,4},{6,5},{7,6},{8,7},{9,8},{10,9},{11,1... | collective-permute-start | bytes 930824 | tf_op jit(solution)/shard_map/ppermute | solution.py:129
  9.1 0.1 collective-permute-start.2
  9.2 0.1 fusion.15
  9.3 0.6 fusion.14
  9.9 0.1 compare_convert_fusion.1
  10.0 1.4 %pad_maximum_fusion.2 = (f32[50]{0:T(128)S(1)}, f32[50]{0:T(128)S(1)}) fusion(f32[49]{0:T(128)S(1)} %get-tuple-element.48, f32[1]{0:T(128)} %get-tuple-element.46, f32[1]{0:T(128)} %get-tuple-element.47, f32[49]{0:T(128)S(1)} %get-tuple-element.49), kind=kLoop, calls=%fused_computation.35 | loop fusion | flops 100 | bytes 800 | tf_op jit(solution)/shard_map/concatenate | solution.py:27
  11.4 0.9 negate_divide_fusion
  12.3 1.1 %divide_add_fusion = (f32[50,16,128]{2,1,0:T(8,128)}, f32[50,16,128]{2,1,0:T(8,128)}) fusion(f32[50,16,128]{2,1,0:T(8,128)S(1)} %get-tuple-element.27, f32[49,16,128]{2,1,0:T(8,128)S(1)} %slice.189, f32[50]{0:T(128)S(1)} %copy-done.8, f32[50]{0:T(128)S(1)} %get-tuple-element.50), kind=kLoop, calls=%fused_computation.19 | loop fusion | flops 512000 | bytes 1630608 | tf_op jit(solution)/shard_map/add | solution.py:29
  13.4 3.5 %shard_map.140 = f32[4,50,16,128]{3,2,1,0:T(8,128)} custom-call(f32[4,50,16,128]{3,2,1,0:T(8,128)} %bitcast.41, f32[50,16,128]{2,1,0:T(8,128)} %get-tuple-element.43.below_ref, f32[50,16,128]{2,1,0:T(8,128)} %get-tuple-element.42.diagonal_ref, f32[50,16,128]{2,1,0:T(8,128)} %get-tuple-element.26.above_ref), custom_call_target="tpu_custom_call" | custom-call | tf_op jit(solution)/shard_map/pallas_call | solution.py:56
  16.9 1.5 %fusion.8 = (f32[200,6,128]{2,1,0:T(8,128)S(1)}, f32[200,6,128]{2,1,0:T(8,128)S(1)}) fusion(f32[200,16,128]{2,1,0:T(8,128)} %bitcast.38), kind=kLoop, calls=%fused_computation.38 | loop fusion | bytes 2457600 | tf_op jit(solution)/shard_map/slice | solution.py:126
  18.4 0.1 copy.26
  18.5 5.7 %collective-permute-start.1 = (f32[200,6,128]{2,0,1:T(8,128)S(1)}, f32[200,6,128]{2,0,1:T(8,128)S(1)}, u32[]{:S(2)}, u32[]{:S(2)}) collective-permute-start(f32[200,6,128]{2,0,1:T(8,128)S(1)} %copy.26), channel_id=1, source_target_pairs={{1,0},{2,1},{3,2},{4,3},{5,4},{6,5},{7,6},{8,7},{9,8},{10,9},{11,1... | collective-permute-start | bytes 1843208 | tf_op jit(solution)/shard_map/ppermute | solution.py:129
  24.2 0.1 copy.25
  24.3 0.1 collective-permute-start
  24.4 0.1 pad.34.clone
  24.5 0.0 collective-permute-done.3
  24.5 0.1 maximum_bitcast_fusion
  24.6 0.1 compare_convert_fusion
  24.8 0.0 copy-start.2
  24.8 0.0 copy-start.10
  24.8 0.1 slice.196
  24.9 0.3 slice.200
  25.2 0.6 copy-done.2
  25.8 1.8 %minimum_subtract_fusion = (f32[50,32,128]{2,1,0:T(8,128)}, f32[50,32,128]{2,1,0:T(8,128)}) fusion(f32[50,32,127]{2,1,0:T(8,128)S(1)} %slice.200, f32[50,6,128]{2,1,0:T(8,128)S(1)} %get-tuple-element.36, f32[50,16,128]{2,1,0:T(8,128)S(1)} %copy-done.2, f32[50,6,128]{2,1,0:T(8,128)S(1)} %get-tuple-element.34, f32[32]{0:T(128)S(1)} %pad.34.clone, ...), kind=kLoop, calls=%fused_computation.9 | loop fusion | flops 2252800 | bytes 3184912 | tf_op jit(solution)/shard_map/sub | solution.py:18
  27.7 1.8 %minimum_subtract_fusion.1 = (f32[50,32,128]{2,1,0:T(8,128)}, f32[50,32,128]{2,1,0:T(8,128)}) fusion(f32[32]{0:T(128)S(1)} %pad.34.clone, f32[50,6,128]{2,1,0:T(8,128)S(1)} %get-tuple-element.37, f32[50,16,128]{2,1,0:T(8,128)S(1)} %copy-done.3, f32[50,6,128]{2,1,0:T(8,128)S(1)} %get-tuple-element.35, f32[50,1,128]{2,1,0:T(1,128)S(1)} %slice.197, ...), kind=kLoop, calls=%fused_computation.11 | loop fusion | flops 2457600 | bytes 3191312 | tf_op jit(solution)/shard_map/sub | solution.py:18
  29.4 3.4 %collective-permute-done.1 = f32[200,6,128]{2,0,1:T(8,128)S(1)} collective-permute-done((f32[200,6,128]{2,0,1:T(8,128)S(1)}, f32[200,6,128]{2,0,1:T(8,128)S(1)}, u32[]{:S(2)}, u32[]{:S(2)}) %collective-permute-start.1) | collective-permute-done | bytes 614432 | tf_op jit(solution)/shard_map/ppermute | solution.py:129
  32.8 0.2 copy.22
  33.0 4.9 %collective-permute-done = f32[200,6,128]{2,0,1:T(8,128)S(1)} collective-permute-done((f32[200,6,128]{2,0,1:T(8,128)S(1)}, f32[200,6,128]{2,0,1:T(8,128)S(1)}, u32[]{:S(2)}, u32[]{:S(2)}) %collective-permute-start) | collective-permute-done | bytes 614432 | tf_op jit(solution)/shard_map/ppermute | solution.py:128
  37.9 0.2 copy.20
  38.0 2.3 %maximum_maximum_fusion.adjoint_ref = f32[4,50,32,128]{3,2,1,0:T(8,128)} fusion(f32[4,50,6,128]{3,2,1,0:T(8,128)S(1)} %bitcast.39, f32[4,50,16,128]{3,2,1,0:T(8,128)S(1)} %copy-done.1, f32[4,50,6,128]{3,2,1,0:T(8,128)S(1)} %bitcast.40, f32[32]{0:T(128)S(1)} %pad.34.clone), kind=kLoop, calls=%fused_computation | loop fusion | flops 2457600 | bytes 6144128 | tf_op jit(solution)/shard_map/concatenate | solution.py:136
  40.4 21.8 %shard_map.141 = f32[4,50,16,128]{3,2,1,0:T(8,128)} custom-call(f32[4,50,32,128]{3,2,1,0:T(8,128)} %maximum_maximum_fusion.adjoint_ref, f32[50,32,128]{2,1,0:T(8,128)} %get-tuple-element.29.east_a_ref, f32[50,32,128]{2,1,0:T(8,128)} %get-tuple-element.28.east_b_ref, f32[50,32,128]{2,1,0:T(8,128)} %get-tuple-element.31.north_a_ref, ...), custom_call_target="tpu_custom_call" | custom-call | tf_op jit(solution)/shard_map/pallas_call | solution.py:113
  62.2 1.6 %fusion.1 = f32[50,16,128]{2,1,0:T(8,128)S(1)} fusion(f32[2,2,50,16,128]{4,3,2,1,0:T(8,128)} %bitcast.33), kind=kLoop, calls=%fused_computation.6 | loop fusion | flops 512000 | bytes 2048000 | tf_op jit(solution)/shard_map/reduce_sum | solution.py:193
  63.7 0.0 copy-start.9
  63.8 0.0 copy-start
  63.8 19.2 %all_to_all.10 = f32[8,100,128]{2,1,0:T(8,128)S(1)} all-to-all(f32[8,100,128]{2,1,0:T(8,128)S(1)} %reshape.126), channel_id=1, replica_groups=mesh['scen'=8,'grid'=32] {'scen'}, dimensions={0} | all-to-all | bytes 819200 | tf_op jit(solution)/shard_map/all_to_all | solution.py:78
  83.1 0.8 broadcast_in_dim.13
  83.9 5.1 %all-to-all-start.1 = ((f32[8,100,128]{2,1,0:T(8,128)}), f32[8,100,128]{2,1,0:T(8,128)S(1)}, u32[]{:S(2)}, u32[]{:S(2)}) async-start(f32[8,100,128]{2,1,0:T(8,128)} %broadcast_in_dim.13), calls=%async_computation.1 | async-start | bytes 851968 | tf_op jit(solution)/shard_map/all_to_all | solution.py:81
  88.9 0.0 copy-start.6
  89.0 0.0 copy-start.7
  89.0 0.0 copy-start.5
  89.0 1.2 %copy.28 = f32[2,2,50,16,128]{4,3,2,1,0:T(8,128)} copy(f32[2,2,50,16,128]{4,3,2,1,0:T(8,128)S(1)} %bitcast.34) | data formatting | bytes 3276800
  90.2 0.6 fusion.6
  90.8 1.3 %fusion.3 = f32[2,2,50,16,128]{4,3,2,1,0:T(8,128)} fusion(f32[2,2,50,16,128]{4,3,2,1,0:T(8,128)} %fusion.6, f32[2,16,128]{2,1,0:T(8,128)S(1)} %copy-done.6, f32[2,16,128]{2,1,0:T(8,128)S(1)} %copy-done.7, f32[2,2,50,16,128]{4,3,2,1,0:T(8,128)S(1)} %bitcast.37, f32[16,128]{1,0:T(8,128)S(1)} %fusion.7), kind=kLoop, calls=%fused_computation.24 | loop fusion | flops 53248 | bytes 90112 | tf_op jit(solution)/shard_map/scatter-add | solution.py:202
  92.1 7.1 %all-to-all-done.1 = f32[8,100,128]{2,1,0:T(8,128)S(1)} async-done(((f32[8,100,128]{2,1,0:T(8,128)}), f32[8,100,128]{2,1,0:T(8,128)S(1)}, u32[]{:S(2)}, u32[]{:S(2)}) %all-to-all-start.1) | async-done | bytes 409632 | tf_op jit(solution)/shard_map/all_to_all | solution.py:81
  99.3 0.9 fusion.2
  (34 shorter events, 0.4 us)
Async XLA Ops:
  1.4 7.8 %copy-start.8 = (f32[50]{0:T(128)S(1)}, f32[50]{0:T(128)}, u32[]{:S(2)}) copy-start(f32[50]{0:T(128)} %param.25) | copy-start | bytes 604
  2.7 8.7 %copy-start.4 = (f32[50,16,128]{2,1,0:T(8,128)S(1)}, f32[50,16,128]{2,1,0:T(8,128)}, u32[]{:S(2)}) copy-start(f32[50,16,128]{2,1,0:T(8,128)} %param.24) | copy-start | bytes 1228804
  2.7 21.8 %collective-permute-start.3 = (f32[101,6,128]{2,1,0:T(8,128)S(1)}, f32[101,6,128]{2,1,0:T(8,128)S(1)}, u32[]{:S(2)}, u32[]{:S(2)}) collective-permute-start(f32[101,6,128]{2,1,0:T(8,128)S(1)} %pad_maximum_fusion.1), channel_id=1, source_target_pairs={{1,0},{2,1},{3,2},{4,3},{5,4},{6,5},{7,6},{8,7},{9,8},{10,9},{11,1... | collective-permute-start | bytes 930824 | tf_op jit(solution)/shard_map/ppermute | solution.py:129
  9.1 15.4 %collective-permute-start.2 = (f32[101,6,128]{2,1,0:T(8,128)S(1)}, f32[101,6,128]{2,1,0:T(8,128)S(1)}, u32[]{:S(2)}, u32[]{:S(2)}) collective-permute-start(f32[101,6,128]{2,1,0:T(8,128)S(1)} %pad_maximum_fusion), channel_id=1, source_target_pairs={{0,1},{1,2},{2,3},{3,4},{4,5},{5,6},{6,7},{7,8},{8,9},{9,10},{10,1... | collective-permute-start | bytes 930824 | tf_op jit(solution)/shard_map/ppermute | solution.py:128
  18.5 14.4 %collective-permute-start.1 = (f32[200,6,128]{2,0,1:T(8,128)S(1)}, f32[200,6,128]{2,0,1:T(8,128)S(1)}, u32[]{:S(2)}, u32[]{:S(2)}) collective-permute-start(f32[200,6,128]{2,0,1:T(8,128)S(1)} %copy.26), channel_id=1, source_target_pairs={{1,0},{2,1},{3,2},{4,3},{5,4},{6,5},{7,6},{8,7},{9,8},{10,9},{11,1... | collective-permute-start | bytes 1843208 | tf_op jit(solution)/shard_map/ppermute | solution.py:129
  24.3 13.6 %collective-permute-start = (f32[200,6,128]{2,0,1:T(8,128)S(1)}, f32[200,6,128]{2,0,1:T(8,128)S(1)}, u32[]{:S(2)}, u32[]{:S(2)}) collective-permute-start(f32[200,6,128]{2,0,1:T(8,128)S(1)} %copy.25), channel_id=1, source_target_pairs={{0,1},{1,2},{2,3},{3,4},{4,5},{5,6},{6,7},{7,8},{8,9},{9,10},{10,1... | collective-permute-start | bytes 1843208 | tf_op jit(solution)/shard_map/ppermute | solution.py:128
  24.8 1.0 %copy-start.2 = (f32[50,16,128]{2,1,0:T(8,128)S(1)}, f32[50,16,128]{2,1,0:T(8,128)}, u32[]{:S(2)}) copy-start(f32[50,16,128]{2,1,0:T(8,128)} %param.21) | copy-start | bytes 1228804
  24.8 1.0 copy-start.10
  25.8 1.8 %copy-start.3 = (f32[50,16,128]{2,1,0:T(8,128)S(1)}, f32[50,16,128]{2,1,0:T(8,128)}, u32[]{:S(2)}) copy-start(f32[50,16,128]{2,1,0:T(8,128)} %param.20) | copy-start | bytes 1228804
  25.8 1.8 %copy-start.11 = (f32[50]{0:T(128)S(1)}, f32[50]{0:T(128)}, u32[]{:S(2)}) copy-start(f32[50]{0:T(128)} %param.22) | copy-start | bytes 604
  29.4 8.6 %copy-start.1 = (f32[4,50,16,128]{3,2,1,0:T(8,128)S(1)}, f32[4,50,16,128]{3,2,1,0:T(8,128)}, u32[]{:S(2)}) copy-start(f32[4,50,16,128]{3,2,1,0:T(8,128)} %shard_map.140) | copy-start | bytes 4915204
  63.7 25.2 %copy-start.9 = (f32[16,128]{1,0:T(8,128)S(1)}, f32[16,128]{1,0:T(8,128)}, u32[]{:S(2)}) copy-start(f32[16,128]{1,0:T(8,128)} %param.27) | copy-start | bytes 24580
  63.8 25.2 %copy-start = (f32[4,50,16,128]{3,2,1,0:T(8,128)S(1)}, f32[4,50,16,128]{3,2,1,0:T(8,128)}, u32[]{:S(2)}) copy-start(f32[4,50,16,128]{3,2,1,0:T(8,128)} %shard_map.141) | copy-start | bytes 4915204
  83.9 15.4 %all-to-all-start.1 = ((f32[8,100,128]{2,1,0:T(8,128)}), f32[8,100,128]{2,1,0:T(8,128)S(1)}, u32[]{:S(2)}, u32[]{:S(2)}) async-start(f32[8,100,128]{2,1,0:T(8,128)} %broadcast_in_dim.13), calls=%async_computation.1 | async-start | bytes 851968 | tf_op jit(solution)/shard_map/all_to_all | solution.py:81
  88.9 1.2 %copy-start.6 = (f32[2,16,128]{2,1,0:T(8,128)S(1)}, f32[2,16,128]{2,1,0:T(8,128)}, u32[]{:S(2)}) copy-start(f32[2,16,128]{2,1,0:T(8,128)} %param.19) | copy-start | bytes 49156
  89.0 1.2 %copy-start.7 = (f32[2,16,128]{2,1,0:T(8,128)S(1)}, f32[2,16,128]{2,1,0:T(8,128)}, u32[]{:S(2)}) copy-start(f32[2,16,128]{2,1,0:T(8,128)} %param.18) | copy-start | bytes 49156
  89.0 10.3 %copy-start.5 = (f32[50,16,128]{2,1,0:T(8,128)S(1)}, f32[50,16,128]{2,1,0:T(8,128)}, u32[]{:S(2)}) copy-start(f32[50,16,128]{2,1,0:T(8,128)} %param.26) | copy-start | bytes 1228804

commit v6 on v5

--- a/solution.py
+++ b/solution.py
@@ -161,18 +161,21 @@
     halo = SUBSTEPS
     padded = -(-(width + 2 * halo) // 8) * 8
     wet_bottom = jnp.where(wet_mask > 0, bottom_level, 0).astype(jnp.float32)
+    depth_index = lax.broadcasted_iota(jnp.int32, (levels, padded, wet_bottom.shape[-1]), 0)
+    wet_cube = (depth_index[:, :width] < wet_bottom[None]).astype(jnp.float32)
+
+    below_band, diagonal, above_band = column_coefficients(vertical_mix, thickness, wet_cube)
+    adjoint = transposed_solve(adjoint_in, below_band, diagonal, above_band)
+    adjoint, east_velocity, north_velocity, wet_bottom = lax.optimization_barrier(
+        (adjoint, east_velocity, north_velocity, wet_bottom)
+    )
+    (adjoint,) = padded_halo(
+        [adjoint.reshape((-1,) + adjoint.shape[-2:])], width, halo, padded
+    )
     wide_east, wide_north, wide_bottom = padded_halo(
         [east_velocity, north_velocity, wet_bottom[None]], width, halo, padded
     )
-    depth_index = lax.broadcasted_iota(jnp.int32, (levels,) + wide_bottom.shape[1:], 0)
     wide_wet = (depth_index.astype(jnp.float32) < wide_bottom).astype(jnp.float32)
-    wet_cube = (depth_index[:, :width] < wet_bottom[None]).astype(jnp.float32)
-
-    below_band, diagonal, above_band = column_coefficients(vertical_mix, thickness, wet_cube)
-    adjoint = transposed_solve(adjoint_in, below_band, diagonal, above_band)
-    (adjoint,) = padded_halo(
-        [adjoint.reshape((-1,) + adjoint.shape[-2:])], width, halo, padded
-    )
 
     east_a, east_b = face_pairs(
         wide_east, wide_wet, jnp.roll(wide_wet, -1, axis=1), east_diffusion

time: 101 us -> 108 us (1.069)
  waiting for transfers between devices: 15.4 us -> 20.1 us
  starting transfers between devices: 17.3 us -> 19.8 us
  local copies, waits for them, and re-layouts: 7.27 us -> 5.75 us
    ppermute x2, waiting for transfers between devices: 4.88 us -> 9.97 us  [padded_halo(): before = lax.ppermute(last, 'grid', up)]
    slice x3 -> x5, local copies, waits for them, and re-layouts: 2.8 us -> 0.29 us  [padded_halo(): last = jnp.concatenate([piece[:, width - halo:] for piece in pieces], 0)]
    all_to_all x1, starting transfers between devices: 5.05 us -> 7.56 us  [scenario_sum(): return lax.all_to_all(spread, 'scen', 0, 0, tiled=True).reshape(shape)]
  transfers between devices with their start and end apart: 5 -> 5, of which waited for: 3 -> 4; matrix products, arithmetic and copies ran while one was open for 13% -> 8% of each run, Pallas kernels for 3% -> 0%
where the time goes in v6:
time: 108 us; the launch traced here: 106 us
  Pallas kernels  25.4 us (24%)
  waiting for transfers between devices  20.1 us (19%)
  starting transfers between devices  19.8 us (18%)
  blocking collectives  19.7 us (18%)
  other arithmetic  14.8 us (14%)
  local copies, waits for them, and re-layouts  5.75 us (5%)
    pallas_call x1, Pallas kernels, transport_substeps(): pl.pallas_call(substep_kernel, grid=(levels // chunk,), in_specs=[field_b...  21.8 us
    all_to_all x1, blocking collectives, scenario_sum(): gathered = lax.all_to_all(pieces, 'scen', 0, 0, tiled=True)  19.7 us
    ppermute x2, starting transfers between devices, padded_halo(): after = lax.ppermute(initial, 'grid', down)  12 us
    ppermute x2, waiting for transfers between devices, padded_halo(): before = lax.ppermute(last, 'grid', up)  9.97 us
    all_to_all x1, starting transfers between devices, scenario_sum(): return lax.all_to_all(spread, 'scen', 0, 0, tiled=True).reshape(shape)  7.56 us
    all_to_all x1, waiting for transfers between devices, scenario_sum(): return lax.all_to_all(spread, 'scen', 0, 0, tiled=True).reshape(shape)  7.09 us
    sub x2, other arithmetic, face_pairs(): jnp.minimum(moving, 0.0) - mixing  3.57 us
    pallas_call x1, Pallas kernels, transposed_solve(): pl.pallas_call(solve_kernel, out_shape=jax.ShapeDtypeStruct(rhs.shape, jn...  3.56 us
  transfers between devices with their start and end apart: 5, of which 4 were waited for; matrix products, arithmetic and copies ran while one was open for 8% of the time, Pallas kernels for 0%

profile of v6, /device:TPU:8, one launch (start us, length us, event | category | flops | bytes accessed | tf_op | source)
XLA Modules:
  0.0 106.4 jit_solution(984605863892210655)
XLA Ops:
  0.6 0.8 fusion.15
  1.4 1.3 %fusion.14 = (f32[1]{0:T(128)}, f32[1]{0:T(128)}) fusion(f32[50]{0:T(128)} %param.25), kind=kLoop, calls=%fused_computation.44 | loop fusion | bytes 16 | tf_op jit(solution)/shard_map/slice | solution.py:27
  2.8 0.7 select_convert_fusion
  3.5 0.1 compare_convert_fusion.1
  3.6 0.0 copy-start.8
  3.7 1.4 %pad_maximum_fusion.2 = (f32[50]{0:T(128)S(1)}, f32[50]{0:T(128)S(1)}) fusion(f32[49]{0:T(128)S(1)} %get-tuple-element.56, f32[1]{0:T(128)} %get-tuple-element.54, f32[1]{0:T(128)} %get-tuple-element.55, f32[49]{0:T(128)S(1)} %get-tuple-element.57), kind=kLoop, calls=%fused_computation.35 | loop fusion | flops 100 | bytes 800 | tf_op jit(solution)/shard_map/concatenate | solution.py:27
  5.0 0.9 negate_divide_fusion
  6.0 1.1 divide_add_fusion
  7.0 3.6 %shard_map.140 = f32[4,50,16,128]{3,2,1,0:T(8,128)} custom-call(f32[4,50,16,128]{3,2,1,0:T(8,128)} %bitcast.43, f32[50,16,128]{2,1,0:T(8,128)} %get-tuple-element.51.below_ref, f32[50,16,128]{2,1,0:T(8,128)} %get-tuple-element.50.diagonal_ref, f32[50,16,128]{2,1,0:T(8,128)} %get-tuple-element.34.above_ref), custom_call_target="tpu_custom_call" | custom-call | tf_op jit(solution)/shard_map/pallas_call | solution.py:56
  10.7 6.3 %collective-permute-start.3 = (f32[101,6,128]{2,1,0:T(8,128)S(1)}, f32[101,6,128]{2,1,0:T(8,128)S(1)}, u32[]{:S(2)}, u32[]{:S(2)}) collective-permute-start(f32[101,6,128]{2,1,0:T(8,128)S(1)} %pad_maximum_fusion.1), channel_id=1, source_target_pairs={{1,0},{2,1},{3,2},{4,3},{5,4},{6,5},{7,6},{8,7},{9,8},{10,9},{11,1... | collective-permute-start | bytes 930824 | tf_op jit(solution)/shard_map/ppermute | solution.py:129
  17.1 0.1 collective-permute-start.2
  17.2 0.1 fusion.8
  17.3 0.1 copy.26
  17.4 5.7 %collective-permute-start.1 = (f32[200,6,128]{2,0,1:T(8,128)S(1)}, f32[200,6,128]{2,0,1:T(8,128)S(1)}, u32[]{:S(2)}, u32[]{:S(2)}) collective-permute-start(f32[200,6,128]{2,0,1:T(8,128)S(1)} %copy.26), channel_id=1, source_target_pairs={{1,0},{2,1},{3,2},{4,3},{5,4},{6,5},{7,6},{8,7},{9,8},{10,9},{11,1... | collective-permute-start | bytes 1843208 | tf_op jit(solution)/shard_map/ppermute | solution.py:129
  23.2 0.1 copy.24
  23.3 0.1 collective-permute-start
  23.4 0.1 pad.34.clone
  23.5 3.1 %collective-permute-done.3 = f32[101,6,128]{2,1,0:T(8,128)S(1)} collective-permute-done((f32[101,6,128]{2,1,0:T(8,128)S(1)}, f32[101,6,128]{2,1,0:T(8,128)S(1)}, u32[]{:S(2)}, u32[]{:S(2)}) %collective-permute-start.3) | collective-permute-done | bytes 310304 | tf_op jit(solution)/shard_map/ppermute | solution.py:129
  26.5 6.4 %collective-permute-done.2 = f32[101,6,128]{2,1,0:T(8,128)S(1)} collective-permute-done((f32[101,6,128]{2,1,0:T(8,128)S(1)}, f32[101,6,128]{2,1,0:T(8,128)S(1)}, u32[]{:S(2)}, u32[]{:S(2)}) %collective-permute-start.2) | collective-permute-done | bytes 310304 | tf_op jit(solution)/shard_map/ppermute | solution.py:128
  32.9 0.1 maximum_bitcast_fusion
  33.0 0.1 compare_convert_fusion
  33.3 0.0 copy-start.10
  33.3 0.1 slice.196
  33.4 0.3 slice.200
  33.6 0.3 copy-done.10
  33.9 1.8 %minimum_subtract_fusion = (f32[50,32,128]{2,1,0:T(8,128)}, f32[50,32,128]{2,1,0:T(8,128)}) fusion(f32[50,32,127]{2,1,0:T(8,128)S(1)} %slice.200, f32[50,6,128]{2,1,0:T(8,128)S(1)} %get-tuple-element.44, f32[50,16,128]{2,1,0:T(8,128)S(1)} %copy-done.2, f32[50,6,128]{2,1,0:T(8,128)S(1)} %get-tuple-element.42, f32[32]{0:T(128)S(1)} %pad.34.clone, ...), kind=kLoop, calls=%fused_computation.9 | loop fusion | flops 2252800 | bytes 3184912 | tf_op jit(solution)/shard_map/sub | solution.py:18
  35.7 1.8 %minimum_subtract_fusion.1 = (f32[50,32,128]{2,1,0:T(8,128)}, f32[50,32,128]{2,1,0:T(8,128)}) fusion(f32[32]{0:T(128)S(1)} %pad.34.clone, f32[50,6,128]{2,1,0:T(8,128)S(1)} %get-tuple-element.45, f32[50,16,128]{2,1,0:T(8,128)S(1)} %copy-done.3, f32[50,6,128]{2,1,0:T(8,128)S(1)} %get-tuple-element.43, f32[50,1,128]{2,1,0:T(1,128)S(1)} %slice.197, ...), kind=kLoop, calls=%fused_computation.11 | loop fusion | flops 2457600 | bytes 3191312 | tf_op jit(solution)/shard_map/sub | solution.py:18
  37.5 0.0 collective-permute-done.1
  37.5 0.2 copy.27
  37.7 3.5 %collective-permute-done = f32[200,6,128]{2,0,1:T(8,128)S(1)} collective-permute-done((f32[200,6,128]{2,0,1:T(8,128)S(1)}, f32[200,6,128]{2,0,1:T(8,128)S(1)}, u32[]{:S(2)}, u32[]{:S(2)}) %collective-permute-start) | collective-permute-done | bytes 614432 | tf_op jit(solution)/shard_map/ppermute | solution.py:128
  41.2 0.2 copy.25
  41.4 2.3 %maximum_maximum_fusion.adjoint_ref = f32[4,50,32,128]{3,2,1,0:T(8,128)} fusion(f32[4,50,6,128]{3,2,1,0:T(8,128)S(1)} %bitcast.41, f32[4,50,16,128]{3,2,1,0:T(8,128)S(1)} %copy-done.1, f32[4,50,6,128]{3,2,1,0:T(8,128)S(1)} %bitcast.42, f32[32]{0:T(128)S(1)} %pad.34.clone), kind=kLoop, calls=%fused_computation | loop fusion | flops 2457600 | bytes 6144128 | tf_op jit(solution)/shard_map/concatenate | solution.py:136
  43.7 21.8 %shard_map.141 = f32[4,50,16,128]{3,2,1,0:T(8,128)} custom-call(f32[4,50,32,128]{3,2,1,0:T(8,128)} %maximum_maximum_fusion.adjoint_ref, f32[50,32,128]{2,1,0:T(8,128)} %get-tuple-element.37.east_a_ref, f32[50,32,128]{2,1,0:T(8,128)} %get-tuple-element.36.east_b_ref, f32[50,32,128]{2,1,0:T(8,128)} %get-tuple-element.39.north_a_ref, ...), custom_call_target="tpu_custom_call" | custom-call | tf_op jit(solution)/shard_map/pallas_call | solution.py:113
  65.5 1.6 %fusion.1 = f32[50,16,128]{2,1,0:T(8,128)S(1)} fusion(f32[2,2,50,16,128]{4,3,2,1,0:T(8,128)} %bitcast.35), kind=kLoop, calls=%fused_computation.6 | loop fusion | flops 512000 | bytes 2048000 | tf_op jit(solution)/shard_map/reduce_sum | solution.py:196
  67.1 0.0 copy-start.9
  67.1 0.0 copy-start
  67.1 19.7 %all_to_all.10 = f32[8,100,128]{2,1,0:T(8,128)S(1)} all-to-all(f32[8,100,128]{2,1,0:T(8,128)S(1)} %reshape.134), channel_id=1, replica_groups=mesh['scen'=8,'grid'=32] {'scen'}, dimensions={0} | all-to-all | bytes 819200 | tf_op jit(solution)/shard_map/all_to_all | solution.py:78
  86.8 0.8 broadcast_in_dim.13
  87.6 7.6 %all-to-all-start.1 = ((f32[8,100,128]{2,1,0:T(8,128)}), f32[8,100,128]{2,1,0:T(8,128)S(1)}, u32[]{:S(2)}, u32[]{:S(2)}) async-start(f32[8,100,128]{2,1,0:T(8,128)} %broadcast_in_dim.13), calls=%async_computation.1 | async-start | bytes 851968 | tf_op jit(solution)/shard_map/all_to_all | solution.py:81
  95.2 0.0 copy-done
  95.2 0.0 copy-start.6
  95.2 0.0 copy-start.7
  95.2 0.0 copy-start.5
  95.2 1.2 %copy.31 = f32[2,2,50,16,128]{4,3,2,1,0:T(8,128)} copy(f32[2,2,50,16,128]{4,3,2,1,0:T(8,128)S(1)} %bitcast.36) | data formatting | bytes 3276800
  96.4 0.6 fusion.6
  97.0 1.3 %fusion.3 = f32[2,2,50,16,128]{4,3,2,1,0:T(8,128)} fusion(f32[2,2,50,16,128]{4,3,2,1,0:T(8,128)} %fusion.6, f32[2,16,128]{2,1,0:T(8,128)S(1)} %copy-done.6, f32[2,16,128]{2,1,0:T(8,128)S(1)} %copy-done.7, f32[2,2,50,16,128]{4,3,2,1,0:T(8,128)S(1)} %bitcast.39, f32[16,128]{1,0:T(8,128)S(1)} %fusion.7), kind=kLoop, calls=%fused_computation.24 | loop fusion | flops 53248 | bytes 90112 | tf_op jit(solution)/shard_map/scatter-add | solution.py:205
  98.4 7.1 %all-to-all-done.1 = f32[8,100,128]{2,1,0:T(8,128)S(1)} async-done(((f32[8,100,128]{2,1,0:T(8,128)}), f32[8,100,128]{2,1,0:T(8,128)S(1)}, u32[]{:S(2)}, u32[]{:S(2)}) %all-to-all-start.1) | async-done | bytes 409632 | tf_op jit(solution)/shard_map/all_to_all | solution.py:81
  105.5 0.9 fusion.2
  (35 shorter events, 0.4 us)
Async XLA Ops:
  0.6 4.4 %copy-start.4 = (f32[50,16,128]{2,1,0:T(8,128)S(1)}, f32[50,16,128]{2,1,0:T(8,128)}, u32[]{:S(2)}) copy-start(f32[50,16,128]{2,1,0:T(8,128)} %param.24) | copy-start | bytes 1228804
  3.6 2.3 %copy-start.8 = (f32[50]{0:T(128)S(1)}, f32[50]{0:T(128)}, u32[]{:S(2)}) copy-start(f32[50]{0:T(128)} %param.25) | copy-start | bytes 604
  7.0 3.6 %copy-start.2 = (f32[50,16,128]{2,1,0:T(8,128)S(1)}, f32[50,16,128]{2,1,0:T(8,128)}, u32[]{:S(2)}) copy-start(f32[50,16,128]{2,1,0:T(8,128)} %param.21) | copy-start | bytes 1228804
  7.0 3.6 %copy-start.3 = (f32[50,16,128]{2,1,0:T(8,128)S(1)}, f32[50,16,128]{2,1,0:T(8,128)}, u32[]{:S(2)}) copy-start(f32[50,16,128]{2,1,0:T(8,128)} %param.20) | copy-start | bytes 1228804
  10.6 6.6 %copy-start.1 = (f32[4,50,16,128]{3,2,1,0:T(8,128)S(1)}, f32[4,50,16,128]{3,2,1,0:T(8,128)}, u32[]{:S(2)}) copy-start(f32[4,50,16,128]{3,2,1,0:T(8,128)} %shard_map.140) | copy-start | bytes 4915204
  10.7 15.8 %collective-permute-start.3 = (f32[101,6,128]{2,1,0:T(8,128)S(1)}, f32[101,6,128]{2,1,0:T(8,128)S(1)}, u32[]{:S(2)}, u32[]{:S(2)}) collective-permute-start(f32[101,6,128]{2,1,0:T(8,128)S(1)} %pad_maximum_fusion.1), channel_id=1, source_target_pairs={{1,0},{2,1},{3,2},{4,3},{5,4},{6,5},{7,6},{8,7},{9,8},{10,9},{11,1... | collective-permute-start | bytes 930824 | tf_op jit(solution)/shard_map/ppermute | solution.py:129
  17.1 15.8 %collective-permute-start.2 = (f32[101,6,128]{2,1,0:T(8,128)S(1)}, f32[101,6,128]{2,1,0:T(8,128)S(1)}, u32[]{:S(2)}, u32[]{:S(2)}) collective-permute-start(f32[101,6,128]{2,1,0:T(8,128)S(1)} %pad_maximum_fusion), channel_id=1, source_target_pairs={{0,1},{1,2},{2,3},{3,4},{4,5},{5,6},{6,7},{7,8},{8,9},{9,10},{10,1... | collective-permute-start | bytes 930824 | tf_op jit(solution)/shard_map/ppermute | solution.py:128
  17.4 20.0 %collective-permute-start.1 = (f32[200,6,128]{2,0,1:T(8,128)S(1)}, f32[200,6,128]{2,0,1:T(8,128)S(1)}, u32[]{:S(2)}, u32[]{:S(2)}) collective-permute-start(f32[200,6,128]{2,0,1:T(8,128)S(1)} %copy.26), channel_id=1, source_target_pairs={{1,0},{2,1},{3,2},{4,3},{5,4},{6,5},{7,6},{8,7},{9,8},{10,9},{11,1... | collective-permute-start | bytes 1843208 | tf_op jit(solution)/shard_map/ppermute | solution.py:129
  23.3 17.9 %collective-permute-start = (f32[200,6,128]{2,0,1:T(8,128)S(1)}, f32[200,6,128]{2,0,1:T(8,128)S(1)}, u32[]{:S(2)}, u32[]{:S(2)}) collective-permute-start(f32[200,6,128]{2,0,1:T(8,128)S(1)} %copy.24), channel_id=1, source_target_pairs={{0,1},{1,2},{2,3},{3,4},{4,5},{5,6},{6,7},{7,8},{8,9},{9,10},{10,1... | collective-permute-start | bytes 1843208 | tf_op jit(solution)/shard_map/ppermute | solution.py:128
  33.3 0.7 copy-start.10
  33.9 1.8 %copy-start.11 = (f32[50]{0:T(128)S(1)}, f32[50]{0:T(128)}, u32[]{:S(2)}) copy-start(f32[50]{0:T(128)} %param.22) | copy-start | bytes 604
  67.1 28.1 %copy-start.9 = (f32[16,128]{1,0:T(8,128)S(1)}, f32[16,128]{1,0:T(8,128)}, u32[]{:S(2)}) copy-start(f32[16,128]{1,0:T(8,128)} %param.27) | copy-start | bytes 24580
  67.1 28.1 %copy-start = (f32[4,50,16,128]{3,2,1,0:T(8,128)S(1)}, f32[4,50,16,128]{3,2,1,0:T(8,128)}, u32[]{:S(2)}) copy-start(f32[4,50,16,128]{3,2,1,0:T(8,128)} %shard_map.141) | copy-start | bytes 4915204
  87.6 17.9 %all-to-all-start.1 = ((f32[8,100,128]{2,1,0:T(8,128)}), f32[8,100,128]{2,1,0:T(8,128)S(1)}, u32[]{:S(2)}, u32[]{:S(2)}) async-start(f32[8,100,128]{2,1,0:T(8,128)} %broadcast_in_dim.13), calls=%async_computation.1 | async-start | bytes 851968 | tf_op jit(solution)/shard_map/all_to_all | solution.py:81
  95.2 1.2 %copy-start.6 = (f32[2,16,128]{2,1,0:T(8,128)S(1)}, f32[2,16,128]{2,1,0:T(8,128)}, u32[]{:S(2)}) copy-start(f32[2,16,128]{2,1,0:T(8,128)} %param.19) | copy-start | bytes 49156
  95.2 1.2 %copy-start.7 = (f32[2,16,128]{2,1,0:T(8,128)S(1)}, f32[2,16,128]{2,1,0:T(8,128)}, u32[]{:S(2)}) copy-start(f32[2,16,128]{2,1,0:T(8,128)} %param.18) | copy-start | bytes 49156
  95.2 10.3 %copy-start.5 = (f32[50,16,128]{2,1,0:T(8,128)S(1)}, f32[50,16,128]{2,1,0:T(8,128)}, u32[]{:S(2)}) copy-start(f32[50,16,128]{2,1,0:T(8,128)} %param.26) | copy-start | bytes 1228804

commit v7 on v5

--- a/solution.py
+++ b/solution.py
@@ -107,7 +107,7 @@
 
 def transport_substeps(adjoint, east_a, east_b, north_a, north_b, width):
     fields, levels, columns, lanes = adjoint.shape
-    chunk = 5 if levels % 5 == 0 else levels
+    chunk = 10 if levels % 10 == 0 else levels
     field_block = pl.BlockSpec((fields, chunk, columns, lanes), lambda j: (0, j, 0, 0))
     face_block = pl.BlockSpec((chunk, columns, lanes), lambda j: (j, 0, 0))
     return pl.pallas_call(

time: 101 us -> 94.7 us (0.938)
  Pallas kernels: 25.3 us -> 19.4 us
    pallas_call x1, Pallas kernels: 21.8 us -> 15.9 us  [transport_substeps(): pl.pallas_call(substep_kernel, grid=(levels // chunk,), in_specs=[field_b...]
  transfers between devices with their start and end apart: 5 -> 5, of which waited for: 3 -> 3; matrix products, arithmetic and copies ran while one was open for 13% -> 14% of each run, Pallas kernels for 3% -> 4%
where the time goes in v7:
time: 94.7 us; the launch traced here: 94.2 us
  Pallas kernels  19.4 us (20%)
  blocking collectives  19.2 us (20%)
  starting transfers between devices  17.3 us (18%)
  waiting for transfers between devices  15.4 us (16%)
  other arithmetic  14.8 us (16%)
  local copies, waits for them, and re-layouts  7.27 us (8%)
    all_to_all x1, blocking collectives, scenario_sum(): gathered = lax.all_to_all(pieces, 'scen', 0, 0, tiled=True)  19.2 us
    pallas_call x1, Pallas kernels, transport_substeps(): pl.pallas_call(substep_kernel, grid=(levels // chunk,), in_specs=[field_b...  15.9 us
    ppermute x2, starting transfers between devices, padded_halo(): after = lax.ppermute(initial, 'grid', down)  12 us
    all_to_all x1, waiting for transfers between devices, scenario_sum(): return lax.all_to_all(spread, 'scen', 0, 0, tiled=True).reshape(shape)  7.11 us
    all_to_all x1, starting transfers between devices, scenario_sum(): return lax.all_to_all(spread, 'scen', 0, 0, tiled=True).reshape(shape)  5.05 us
    ppermute x2, waiting for transfers between devices, padded_halo(): before = lax.ppermute(last, 'grid', up)  4.88 us
    sub x2, other arithmetic, face_pairs(): jnp.minimum(moving, 0.0) - mixing  3.56 us
    pallas_call x1, Pallas kernels, transposed_solve(): pl.pallas_call(solve_kernel, out_shape=jax.ShapeDtypeStruct(rhs.shape, jn...  3.48 us
  transfers between devices with their start and end apart: 5, of which 3 were waited for; matrix products, arithmetic and copies ran while one was open for 14% of the time, Pallas kernels for 4%

profile of v7, /device:TPU:8, one launch (start us, length us, event | category | flops | bytes accessed | tf_op | source)
XLA Modules:
  0.0 94.2 jit_solution(12861073393813944588)
XLA Ops:
  0.6 0.7 select_convert_fusion
  1.4 1.3 %fusion.11 = (f32[50,6,128]{2,1,0:T(8,128)S(1)}, f32[50,6,128]{2,1,0:T(8,128)S(1)}, f32[50,6,128]{2,1,0:T(8,128)S(1)}, f32[50,6,128]{2,1,0:T(8,128)S(1)}) fusion(f32[50,16,128]{2,1,0:T(8,128)} %param.20, f32[50,16,128]{2,1,0:T(8,128)} %param.21), kind=kLoop, calls=%fused_computation.41 | loop fusion | bytes 1228800 | tf_op jit(solution)/shard_map/slice | solution.py:126
  2.7 0.0 copy-start.4
  2.7 6.3 %collective-permute-start.3 = (f32[101,6,128]{2,1,0:T(8,128)S(1)}, f32[101,6,128]{2,1,0:T(8,128)S(1)}, u32[]{:S(2)}, u32[]{:S(2)}) collective-permute-start(f32[101,6,128]{2,1,0:T(8,128)S(1)} %pad_maximum_fusion.1), channel_id=1, source_target_pairs={{1,0},{2,1},{3,2},{4,3},{5,4},{6,5},{7,6},{8,7},{9,8},{10,9},{11,1... | collective-permute-start | bytes 930824 | tf_op jit(solution)/shard_map/ppermute | solution.py:129
  9.1 0.1 collective-permute-start.2
  9.2 0.1 fusion.15
  9.3 0.6 fusion.14
  9.9 0.1 compare_convert_fusion.1
  10.0 1.4 %pad_maximum_fusion.2 = (f32[50]{0:T(128)S(1)}, f32[50]{0:T(128)S(1)}) fusion(f32[49]{0:T(128)S(1)} %get-tuple-element.48, f32[1]{0:T(128)} %get-tuple-element.46, f32[1]{0:T(128)} %get-tuple-element.47, f32[49]{0:T(128)S(1)} %get-tuple-element.49), kind=kLoop, calls=%fused_computation.35 | loop fusion | flops 100 | bytes 800 | tf_op jit(solution)/shard_map/concatenate | solution.py:27
  11.4 0.9 negate_divide_fusion
  12.3 1.1 %divide_add_fusion = (f32[50,16,128]{2,1,0:T(8,128)}, f32[50,16,128]{2,1,0:T(8,128)}) fusion(f32[50,16,128]{2,1,0:T(8,128)S(1)} %get-tuple-element.27, f32[49,16,128]{2,1,0:T(8,128)S(1)} %slice.189, f32[50]{0:T(128)S(1)} %copy-done.8, f32[50]{0:T(128)S(1)} %get-tuple-element.50), kind=kLoop, calls=%fused_computation.19 | loop fusion | flops 512000 | bytes 1630608 | tf_op jit(solution)/shard_map/add | solution.py:29
  13.4 3.5 %shard_map.140 = f32[4,50,16,128]{3,2,1,0:T(8,128)} custom-call(f32[4,50,16,128]{3,2,1,0:T(8,128)} %bitcast.41, f32[50,16,128]{2,1,0:T(8,128)} %get-tuple-element.43.below_ref, f32[50,16,128]{2,1,0:T(8,128)} %get-tuple-element.42.diagonal_ref, f32[50,16,128]{2,1,0:T(8,128)} %get-tuple-element.26.above_ref), custom_call_target="tpu_custom_call" | custom-call | tf_op jit(solution)/shard_map/pallas_call | solution.py:56
  16.9 1.5 %fusion.8 = (f32[200,6,128]{2,1,0:T(8,128)S(1)}, f32[200,6,128]{2,1,0:T(8,128)S(1)}) fusion(f32[200,16,128]{2,1,0:T(8,128)} %bitcast.38), kind=kLoop, calls=%fused_computation.38 | loop fusion | bytes 2457600 | tf_op jit(solution)/shard_map/slice | solution.py:126
  18.4 0.1 copy.26
  18.5 5.7 %collective-permute-start.1 = (f32[200,6,128]{2,0,1:T(8,128)S(1)}, f32[200,6,128]{2,0,1:T(8,128)S(1)}, u32[]{:S(2)}, u32[]{:S(2)}) collective-permute-start(f32[200,6,128]{2,0,1:T(8,128)S(1)} %copy.26), channel_id=1, source_target_pairs={{1,0},{2,1},{3,2},{4,3},{5,4},{6,5},{7,6},{8,7},{9,8},{10,9},{11,1... | collective-permute-start | bytes 1843208 | tf_op jit(solution)/shard_map/ppermute | solution.py:129
  24.2 0.1 copy.25
  24.3 0.1 collective-permute-start
  24.4 0.1 pad.34.clone
  24.5 0.0 collective-permute-done.3
  24.5 0.1 maximum_bitcast_fusion
  24.6 0.1 compare_convert_fusion
  24.8 0.0 copy-start.2
  24.8 0.0 copy-start.10
  24.8 0.1 slice.196
  24.9 0.3 slice.200
  25.2 0.6 copy-done.2
  25.8 1.8 %minimum_subtract_fusion = (f32[50,32,128]{2,1,0:T(8,128)}, f32[50,32,128]{2,1,0:T(8,128)}) fusion(f32[50,32,127]{2,1,0:T(8,128)S(1)} %slice.200, f32[50,6,128]{2,1,0:T(8,128)S(1)} %get-tuple-element.36, f32[50,16,128]{2,1,0:T(8,128)S(1)} %copy-done.2, f32[50,6,128]{2,1,0:T(8,128)S(1)} %get-tuple-element.34, f32[32]{0:T(128)S(1)} %pad.34.clone, ...), kind=kLoop, calls=%fused_computation.9 | loop fusion | flops 2252800 | bytes 3184912 | tf_op jit(solution)/shard_map/sub | solution.py:18
  27.7 1.8 %minimum_subtract_fusion.1 = (f32[50,32,128]{2,1,0:T(8,128)}, f32[50,32,128]{2,1,0:T(8,128)}) fusion(f32[32]{0:T(128)S(1)} %pad.34.clone, f32[50,6,128]{2,1,0:T(8,128)S(1)} %get-tuple-element.37, f32[50,16,128]{2,1,0:T(8,128)S(1)} %copy-done.3, f32[50,6,128]{2,1,0:T(8,128)S(1)} %get-tuple-element.35, f32[50,1,128]{2,1,0:T(1,128)S(1)} %slice.197, ...), kind=kLoop, calls=%fused_computation.11 | loop fusion | flops 2457600 | bytes 3191312 | tf_op jit(solution)/shard_map/sub | solution.py:18
  29.4 3.4 %collective-permute-done.1 = f32[200,6,128]{2,0,1:T(8,128)S(1)} collective-permute-done((f32[200,6,128]{2,0,1:T(8,128)S(1)}, f32[200,6,128]{2,0,1:T(8,128)S(1)}, u32[]{:S(2)}, u32[]{:S(2)}) %collective-permute-start.1) | collective-permute-done | bytes 614432 | tf_op jit(solution)/shard_map/ppermute | solution.py:129
  32.8 0.2 copy.22
  33.0 4.9 %collective-permute-done = f32[200,6,128]{2,0,1:T(8,128)S(1)} collective-permute-done((f32[200,6,128]{2,0,1:T(8,128)S(1)}, f32[200,6,128]{2,0,1:T(8,128)S(1)}, u32[]{:S(2)}, u32[]{:S(2)}) %collective-permute-start) | collective-permute-done | bytes 614432 | tf_op jit(solution)/shard_map/ppermute | solution.py:128
  37.9 0.2 copy.20
  38.0 2.3 %maximum_maximum_fusion.adjoint_ref = f32[4,50,32,128]{3,2,1,0:T(8,128)} fusion(f32[4,50,6,128]{3,2,1,0:T(8,128)S(1)} %bitcast.39, f32[4,50,16,128]{3,2,1,0:T(8,128)S(1)} %copy-done.1, f32[4,50,6,128]{3,2,1,0:T(8,128)S(1)} %bitcast.40, f32[32]{0:T(128)S(1)} %pad.34.clone), kind=kLoop, calls=%fused_computation | loop fusion | flops 2457600 | bytes 6144128 | tf_op jit(solution)/shard_map/concatenate | solution.py:136
  40.4 15.9 %shard_map.141 = f32[4,50,16,128]{3,2,1,0:T(8,128)} custom-call(f32[4,50,32,128]{3,2,1,0:T(8,128)} %maximum_maximum_fusion.adjoint_ref, f32[50,32,128]{2,1,0:T(8,128)} %get-tuple-element.29.east_a_ref, f32[50,32,128]{2,1,0:T(8,128)} %get-tuple-element.28.east_b_ref, f32[50,32,128]{2,1,0:T(8,128)} %get-tuple-element.31.north_a_ref, ...), custom_call_target="tpu_custom_call" | custom-call | tf_op jit(solution)/shard_map/pallas_call | solution.py:113
  56.3 1.6 %fusion.1 = f32[50,16,128]{2,1,0:T(8,128)S(1)} fusion(f32[2,2,50,16,128]{4,3,2,1,0:T(8,128)} %bitcast.33), kind=kLoop, calls=%fused_computation.6 | loop fusion | flops 512000 | bytes 2048000 | tf_op jit(solution)/shard_map/reduce_sum | solution.py:193
  57.8 0.0 copy-start.9
  57.9 0.0 copy-start
  57.9 19.2 %all_to_all.10 = f32[8,100,128]{2,1,0:T(8,128)S(1)} all-to-all(f32[8,100,128]{2,1,0:T(8,128)S(1)} %reshape.126), channel_id=1, replica_groups=mesh['scen'=8,'grid'=32] {'scen'}, dimensions={0} | all-to-all | bytes 819200 | tf_op jit(solution)/shard_map/all_to_all | solution.py:78
  77.2 0.8 broadcast_in_dim.13
  78.0 5.1 %all-to-all-start.1 = ((f32[8,100,128]{2,1,0:T(8,128)}), f32[8,100,128]{2,1,0:T(8,128)S(1)}, u32[]{:S(2)}, u32[]{:S(2)}) async-start(f32[8,100,128]{2,1,0:T(8,128)} %broadcast_in_dim.13), calls=%async_computation.1 | async-start | bytes 851968 | tf_op jit(solution)/shard_map/all_to_all | solution.py:81
  83.0 0.0 copy-start.6
  83.0 0.0 copy-start.7
  83.1 0.0 copy-start.5
  83.1 1.2 %copy.28 = f32[2,2,50,16,128]{4,3,2,1,0:T(8,128)} copy(f32[2,2,50,16,128]{4,3,2,1,0:T(8,128)S(1)} %bitcast.34) | data formatting | bytes 3276800
  84.3 0.6 fusion.6
  84.9 1.3 %fusion.3 = f32[2,2,50,16,128]{4,3,2,1,0:T(8,128)} fusion(f32[2,2,50,16,128]{4,3,2,1,0:T(8,128)} %fusion.6, f32[2,16,128]{2,1,0:T(8,128)S(1)} %copy-done.6, f32[2,16,128]{2,1,0:T(8,128)S(1)} %copy-done.7, f32[2,2,50,16,128]{4,3,2,1,0:T(8,128)S(1)} %bitcast.37, f32[16,128]{1,0:T(8,128)S(1)} %fusion.7), kind=kLoop, calls=%fused_computation.24 | loop fusion | flops 53248 | bytes 90112 | tf_op jit(solution)/shard_map/scatter-add | solution.py:202
  86.2 7.1 %all-to-all-done.1 = f32[8,100,128]{2,1,0:T(8,128)S(1)} async-done(((f32[8,100,128]{2,1,0:T(8,128)}), f32[8,100,128]{2,1,0:T(8,128)S(1)}, u32[]{:S(2)}, u32[]{:S(2)}) %all-to-all-start.1) | async-done | bytes 409632 | tf_op jit(solution)/shard_map/all_to_all | solution.py:81
  93.4 0.9 fusion.2
  (34 shorter events, 0.4 us)
Async XLA Ops:
  1.4 7.8 %copy-start.8 = (f32[50]{0:T(128)S(1)}, f32[50]{0:T(128)}, u32[]{:S(2)}) copy-start(f32[50]{0:T(128)} %param.25) | copy-start | bytes 604
  2.7 8.7 %copy-start.4 = (f32[50,16,128]{2,1,0:T(8,128)S(1)}, f32[50,16,128]{2,1,0:T(8,128)}, u32[]{:S(2)}) copy-start(f32[50,16,128]{2,1,0:T(8,128)} %param.24) | copy-start | bytes 1228804
  2.7 21.8 %collective-permute-start.3 = (f32[101,6,128]{2,1,0:T(8,128)S(1)}, f32[101,6,128]{2,1,0:T(8,128)S(1)}, u32[]{:S(2)}, u32[]{:S(2)}) collective-permute-start(f32[101,6,128]{2,1,0:T(8,128)S(1)} %pad_maximum_fusion.1), channel_id=1, source_target_pairs={{1,0},{2,1},{3,2},{4,3},{5,4},{6,5},{7,6},{8,7},{9,8},{10,9},{11,1... | collective-permute-start | bytes 930824 | tf_op jit(solution)/shard_map/ppermute | solution.py:129
  9.1 15.4 %collective-permute-start.2 = (f32[101,6,128]{2,1,0:T(8,128)S(1)}, f32[101,6,128]{2,1,0:T(8,128)S(1)}, u32[]{:S(2)}, u32[]{:S(2)}) collective-permute-start(f32[101,6,128]{2,1,0:T(8,128)S(1)} %pad_maximum_fusion), channel_id=1, source_target_pairs={{0,1},{1,2},{2,3},{3,4},{4,5},{5,6},{6,7},{7,8},{8,9},{9,10},{10,1... | collective-permute-start | bytes 930824 | tf_op jit(solution)/shard_map/ppermute | solution.py:128
  18.5 14.4 %collective-permute-start.1 = (f32[200,6,128]{2,0,1:T(8,128)S(1)}, f32[200,6,128]{2,0,1:T(8,128)S(1)}, u32[]{:S(2)}, u32[]{:S(2)}) collective-permute-start(f32[200,6,128]{2,0,1:T(8,128)S(1)} %copy.26), channel_id=1, source_target_pairs={{1,0},{2,1},{3,2},{4,3},{5,4},{6,5},{7,6},{8,7},{9,8},{10,9},{11,1... | collective-permute-start | bytes 1843208 | tf_op jit(solution)/shard_map/ppermute | solution.py:129
  24.3 13.6 %collective-permute-start = (f32[200,6,128]{2,0,1:T(8,128)S(1)}, f32[200,6,128]{2,0,1:T(8,128)S(1)}, u32[]{:S(2)}, u32[]{:S(2)}) collective-permute-start(f32[200,6,128]{2,0,1:T(8,128)S(1)} %copy.25), channel_id=1, source_target_pairs={{0,1},{1,2},{2,3},{3,4},{4,5},{5,6},{6,7},{7,8},{8,9},{9,10},{10,1... | collective-permute-start | bytes 1843208 | tf_op jit(solution)/shard_map/ppermute | solution.py:128
  24.8 1.0 %copy-start.2 = (f32[50,16,128]{2,1,0:T(8,128)S(1)}, f32[50,16,128]{2,1,0:T(8,128)}, u32[]{:S(2)}) copy-start(f32[50,16,128]{2,1,0:T(8,128)} %param.21) | copy-start | bytes 1228804
  24.8 1.0 %copy-start.10 = (f32[50]{0:T(128)S(1)}, f32[50]{0:T(128)}, u32[]{:S(2)}) copy-start(f32[50]{0:T(128)} %param.23) | copy-start | bytes 604
  25.8 1.8 %copy-start.3 = (f32[50,16,128]{2,1,0:T(8,128)S(1)}, f32[50,16,128]{2,1,0:T(8,128)}, u32[]{:S(2)}) copy-start(f32[50,16,128]{2,1,0:T(8,128)} %param.20) | copy-start | bytes 1228804
  25.8 1.8 %copy-start.11 = (f32[50]{0:T(128)S(1)}, f32[50]{0:T(128)}, u32[]{:S(2)}) copy-start(f32[50]{0:T(128)} %param.22) | copy-start | bytes 604
  29.4 8.6 %copy-start.1 = (f32[4,50,16,128]{3,2,1,0:T(8,128)S(1)}, f32[4,50,16,128]{3,2,1,0:T(8,128)}, u32[]{:S(2)}) copy-start(f32[4,50,16,128]{3,2,1,0:T(8,128)} %shard_map.140) | copy-start | bytes 4915204
  57.8 25.2 %copy-start.9 = (f32[16,128]{1,0:T(8,128)S(1)}, f32[16,128]{1,0:T(8,128)}, u32[]{:S(2)}) copy-start(f32[16,128]{1,0:T(8,128)} %param.27) | copy-start | bytes 24580
  57.9 25.2 %copy-start = (f32[4,50,16,128]{3,2,1,0:T(8,128)S(1)}, f32[4,50,16,128]{3,2,1,0:T(8,128)}, u32[]{:S(2)}) copy-start(f32[4,50,16,128]{3,2,1,0:T(8,128)} %shard_map.141) | copy-start | bytes 4915204
  78.0 15.4 %all-to-all-start.1 = ((f32[8,100,128]{2,1,0:T(8,128)}), f32[8,100,128]{2,1,0:T(8,128)S(1)}, u32[]{:S(2)}, u32[]{:S(2)}) async-start(f32[8,100,128]{2,1,0:T(8,128)} %broadcast_in_dim.13), calls=%async_computation.1 | async-start | bytes 851968 | tf_op jit(solution)/shard_map/all_to_all | solution.py:81
  83.0 1.2 %copy-start.6 = (f32[2,16,128]{2,1,0:T(8,128)S(1)}, f32[2,16,128]{2,1,0:T(8,128)}, u32[]{:S(2)}) copy-start(f32[2,16,128]{2,1,0:T(8,128)} %param.19) | copy-start | bytes 49156
  83.0 1.2 %copy-start.7 = (f32[2,16,128]{2,1,0:T(8,128)S(1)}, f32[2,16,128]{2,1,0:T(8,128)}, u32[]{:S(2)}) copy-start(f32[2,16,128]{2,1,0:T(8,128)} %param.18) | copy-start | bytes 49156
  83.1 10.3 %copy-start.5 = (f32[50,16,128]{2,1,0:T(8,128)S(1)}, f32[50,16,128]{2,1,0:T(8,128)}, u32[]{:S(2)}) copy-start(f32[50,16,128]{2,1,0:T(8,128)} %param.26) | copy-start | bytes 1228804

commit v8 on v7

--- a/solution.py
+++ b/solution.py
@@ -107,7 +107,7 @@
 
 def transport_substeps(adjoint, east_a, east_b, north_a, north_b, width):
     fields, levels, columns, lanes = adjoint.shape
-    chunk = 10 if levels % 10 == 0 else levels
+    chunk = 25 if levels % 25 == 0 else levels
     field_block = pl.BlockSpec((fields, chunk, columns, lanes), lambda j: (0, j, 0, 0))
     face_block = pl.BlockSpec((chunk, columns, lanes), lambda j: (j, 0, 0))
     return pl.pallas_call(

time: 94.7 us -> 92.8 us (0.980)
  Pallas kernels: 19.4 us -> 17.3 us
    pallas_call x1, Pallas kernels: 15.9 us -> 13.8 us  [transport_substeps(): pl.pallas_call(substep_kernel, grid=(levels // chunk,), in_specs=[field_b...]
  transfers between devices with their start and end apart: 5 -> 5, of which waited for: 3 -> 3; matrix products, arithmetic and copies ran while one was open for 14% -> 15% of each run, Pallas kernels for 4% -> 4%
where the time goes in v8:
time: 92.8 us; the launch traced here: 92.3 us
  blocking collectives  19.2 us (21%)
  starting transfers between devices  17.4 us (19%)
  Pallas kernels  17.3 us (19%)
  waiting for transfers between devices  15.4 us (17%)
  other arithmetic  14.8 us (16%)
  local copies, waits for them, and re-layouts  7.27 us (8%)
    all_to_all x1, blocking collectives, scenario_sum(): gathered = lax.all_to_all(pieces, 'scen', 0, 0, tiled=True)  19.2 us
    pallas_call x1, Pallas kernels, transport_substeps(): pl.pallas_call(substep_kernel, grid=(levels // chunk,), in_specs=[field_b...  13.8 us
    ppermute x2, starting transfers between devices, padded_halo(): after = lax.ppermute(initial, 'grid', down)  12 us
    all_to_all x1, waiting for transfers between devices, scenario_sum(): return lax.all_to_all(spread, 'scen', 0, 0, tiled=True).reshape(shape)  7.11 us
    all_to_all x1, starting transfers between devices, scenario_sum(): return lax.all_to_all(spread, 'scen', 0, 0, tiled=True).reshape(shape)  5.05 us
    ppermute x2, waiting for transfers between devices, padded_halo(): before = lax.ppermute(last, 'grid', up)  4.88 us
    sub x2, other arithmetic, face_pairs(): jnp.minimum(moving, 0.0) - mixing  3.56 us
    pallas_call x1, Pallas kernels, transposed_solve(): pl.pallas_call(solve_kernel, out_shape=jax.ShapeDtypeStruct(rhs.shape, jn...  3.48 us
  transfers between devices with their start and end apart: 5, of which 3 were waited for; matrix products, arithmetic and copies ran while one was open for 15% of the time, Pallas kernels for 4%

profile of v8, /device:TPU:8, one launch (start us, length us, event | category | flops | bytes accessed | tf_op | source)
XLA Modules:
  0.0 92.3 jit_solution(17823987973137929673)
XLA Ops:
  0.6 0.7 select_convert_fusion
  1.4 1.3 %fusion.11 = (f32[50,6,128]{2,1,0:T(8,128)S(1)}, f32[50,6,128]{2,1,0:T(8,128)S(1)}, f32[50,6,128]{2,1,0:T(8,128)S(1)}, f32[50,6,128]{2,1,0:T(8,128)S(1)}) fusion(f32[50,16,128]{2,1,0:T(8,128)} %param.20, f32[50,16,128]{2,1,0:T(8,128)} %param.21), kind=kLoop, calls=%fused_computation.41 | loop fusion | bytes 1228800 | tf_op jit(solution)/shard_map/slice | solution.py:126
  2.7 0.0 copy-start.4
  2.7 6.3 %collective-permute-start.3 = (f32[101,6,128]{2,1,0:T(8,128)S(1)}, f32[101,6,128]{2,1,0:T(8,128)S(1)}, u32[]{:S(2)}, u32[]{:S(2)}) collective-permute-start(f32[101,6,128]{2,1,0:T(8,128)S(1)} %pad_maximum_fusion.1), channel_id=1, source_target_pairs={{1,0},{2,1},{3,2},{4,3},{5,4},{6,5},{7,6},{8,7},{9,8},{10,9},{11,1... | collective-permute-start | bytes 930824 | tf_op jit(solution)/shard_map/ppermute | solution.py:129
  9.1 0.1 collective-permute-start.2
  9.2 0.1 fusion.15
  9.3 0.6 fusion.14
  9.9 0.1 compare_convert_fusion.1
  10.0 1.4 %pad_maximum_fusion.2 = (f32[50]{0:T(128)S(1)}, f32[50]{0:T(128)S(1)}) fusion(f32[49]{0:T(128)S(1)} %get-tuple-element.48, f32[1]{0:T(128)} %get-tuple-element.46, f32[1]{0:T(128)} %get-tuple-element.47, f32[49]{0:T(128)S(1)} %get-tuple-element.49), kind=kLoop, calls=%fused_computation.35 | loop fusion | flops 100 | bytes 800 | tf_op jit(solution)/shard_map/concatenate | solution.py:27
  11.4 0.9 negate_divide_fusion
  12.3 1.1 %divide_add_fusion = (f32[50,16,128]{2,1,0:T(8,128)}, f32[50,16,128]{2,1,0:T(8,128)}) fusion(f32[50,16,128]{2,1,0:T(8,128)S(1)} %get-tuple-element.27, f32[49,16,128]{2,1,0:T(8,128)S(1)} %slice.189, f32[50]{0:T(128)S(1)} %copy-done.8, f32[50]{0:T(128)S(1)} %get-tuple-element.50), kind=kLoop, calls=%fused_computation.19 | loop fusion | flops 512000 | bytes 1630608 | tf_op jit(solution)/shard_map/add | solution.py:29
  13.4 3.5 %shard_map.140 = f32[4,50,16,128]{3,2,1,0:T(8,128)} custom-call(f32[4,50,16,128]{3,2,1,0:T(8,128)} %bitcast.41, f32[50,16,128]{2,1,0:T(8,128)} %get-tuple-element.43.below_ref, f32[50,16,128]{2,1,0:T(8,128)} %get-tuple-element.42.diagonal_ref, f32[50,16,128]{2,1,0:T(8,128)} %get-tuple-element.26.above_ref), custom_call_target="tpu_custom_call" | custom-call | tf_op jit(solution)/shard_map/pallas_call | solution.py:56
  16.9 1.5 %fusion.8 = (f32[200,6,128]{2,1,0:T(8,128)S(1)}, f32[200,6,128]{2,1,0:T(8,128)S(1)}) fusion(f32[200,16,128]{2,1,0:T(8,128)} %bitcast.38), kind=kLoop, calls=%fused_computation.38 | loop fusion | bytes 2457600 | tf_op jit(solution)/shard_map/slice | solution.py:126
  18.4 0.1 copy.26
  18.5 5.7 %collective-permute-start.1 = (f32[200,6,128]{2,0,1:T(8,128)S(1)}, f32[200,6,128]{2,0,1:T(8,128)S(1)}, u32[]{:S(2)}, u32[]{:S(2)}) collective-permute-start(f32[200,6,128]{2,0,1:T(8,128)S(1)} %copy.26), channel_id=1, source_target_pairs={{1,0},{2,1},{3,2},{4,3},{5,4},{6,5},{7,6},{8,7},{9,8},{10,9},{11,1... | collective-permute-start | bytes 1843208 | tf_op jit(solution)/shard_map/ppermute | solution.py:129
  24.2 0.1 copy.25
  24.3 0.3 collective-permute-start
  24.6 0.1 pad.34.clone
  24.7 0.0 collective-permute-done.3
  24.7 0.1 maximum_bitcast_fusion
  24.8 0.1 compare_convert_fusion
  25.0 0.0 copy-start.2
  25.0 0.0 copy-start.10
  25.0 0.1 slice.196
  25.1 0.3 slice.200
  25.4 0.6 copy-done.2
  26.0 1.8 %minimum_subtract_fusion = (f32[50,32,128]{2,1,0:T(8,128)}, f32[50,32,128]{2,1,0:T(8,128)}) fusion(f32[50,32,127]{2,1,0:T(8,128)S(1)} %slice.200, f32[50,6,128]{2,1,0:T(8,128)S(1)} %get-tuple-element.36, f32[50,16,128]{2,1,0:T(8,128)S(1)} %copy-done.2, f32[50,6,128]{2,1,0:T(8,128)S(1)} %get-tuple-element.34, f32[32]{0:T(128)S(1)} %pad.34.clone, ...), kind=kLoop, calls=%fused_computation.9 | loop fusion | flops 2252800 | bytes 3184912 | tf_op jit(solution)/shard_map/sub | solution.py:18
  27.8 1.8 %minimum_subtract_fusion.1 = (f32[50,32,128]{2,1,0:T(8,128)}, f32[50,32,128]{2,1,0:T(8,128)}) fusion(f32[32]{0:T(128)S(1)} %pad.34.clone, f32[50,6,128]{2,1,0:T(8,128)S(1)} %get-tuple-element.37, f32[50,16,128]{2,1,0:T(8,128)S(1)} %copy-done.3, f32[50,6,128]{2,1,0:T(8,128)S(1)} %get-tuple-element.35, f32[50,1,128]{2,1,0:T(1,128)S(1)} %slice.197, ...), kind=kLoop, calls=%fused_computation.11 | loop fusion | flops 2457600 | bytes 3191312 | tf_op jit(solution)/shard_map/sub | solution.py:18
  29.6 3.4 %collective-permute-done.1 = f32[200,6,128]{2,0,1:T(8,128)S(1)} collective-permute-done((f32[200,6,128]{2,0,1:T(8,128)S(1)}, f32[200,6,128]{2,0,1:T(8,128)S(1)}, u32[]{:S(2)}, u32[]{:S(2)}) %collective-permute-start.1) | collective-permute-done | bytes 614432 | tf_op jit(solution)/shard_map/ppermute | solution.py:129
  33.0 0.2 copy.22
  33.2 4.9 %collective-permute-done = f32[200,6,128]{2,0,1:T(8,128)S(1)} collective-permute-done((f32[200,6,128]{2,0,1:T(8,128)S(1)}, f32[200,6,128]{2,0,1:T(8,128)S(1)}, u32[]{:S(2)}, u32[]{:S(2)}) %collective-permute-start) | collective-permute-done | bytes 614432 | tf_op jit(solution)/shard_map/ppermute | solution.py:128
  38.1 0.2 copy.20
  38.2 2.3 %maximum_maximum_fusion.adjoint_ref = f32[4,50,32,128]{3,2,1,0:T(8,128)} fusion(f32[4,50,6,128]{3,2,1,0:T(8,128)S(1)} %bitcast.39, f32[4,50,16,128]{3,2,1,0:T(8,128)S(1)} %copy-done.1, f32[4,50,6,128]{3,2,1,0:T(8,128)S(1)} %bitcast.40, f32[32]{0:T(128)S(1)} %pad.34.clone), kind=kLoop, calls=%fused_computation | loop fusion | flops 2457600 | bytes 6144128 | tf_op jit(solution)/shard_map/concatenate | solution.py:136
  40.5 13.8 %shard_map.141 = f32[4,50,16,128]{3,2,1,0:T(8,128)} custom-call(f32[4,50,32,128]{3,2,1,0:T(8,128)} %maximum_maximum_fusion.adjoint_ref, f32[50,32,128]{2,1,0:T(8,128)} %get-tuple-element.29.east_a_ref, f32[50,32,128]{2,1,0:T(8,128)} %get-tuple-element.28.east_b_ref, f32[50,32,128]{2,1,0:T(8,128)} %get-tuple-element.31.north_a_ref, ...), custom_call_target="tpu_custom_call" | custom-call | tf_op jit(solution)/shard_map/pallas_call | solution.py:113
  54.3 1.6 %fusion.1 = f32[50,16,128]{2,1,0:T(8,128)S(1)} fusion(f32[2,2,50,16,128]{4,3,2,1,0:T(8,128)} %bitcast.33), kind=kLoop, calls=%fused_computation.6 | loop fusion | flops 512000 | bytes 2048000 | tf_op jit(solution)/shard_map/reduce_sum | solution.py:193
  55.9 0.0 copy-start.9
  55.9 0.0 copy-start
  55.9 19.2 %all_to_all.10 = f32[8,100,128]{2,1,0:T(8,128)S(1)} all-to-all(f32[8,100,128]{2,1,0:T(8,128)S(1)} %reshape.126), channel_id=1, replica_groups=mesh['scen'=8,'grid'=32] {'scen'}, dimensions={0} | all-to-all | bytes 819200 | tf_op jit(solution)/shard_map/all_to_all | solution.py:78
  75.2 0.8 broadcast_in_dim.13
  76.0 5.1 %all-to-all-start.1 = ((f32[8,100,128]{2,1,0:T(8,128)}), f32[8,100,128]{2,1,0:T(8,128)S(1)}, u32[]{:S(2)}, u32[]{:S(2)}) async-start(f32[8,100,128]{2,1,0:T(8,128)} %broadcast_in_dim.13), calls=%async_computation.1 | async-start | bytes 851968 | tf_op jit(solution)/shard_map/all_to_all | solution.py:81
  81.1 0.0 copy-start.6
  81.1 0.0 copy-start.7
  81.1 0.0 copy-start.5
  81.1 1.2 %copy.28 = f32[2,2,50,16,128]{4,3,2,1,0:T(8,128)} copy(f32[2,2,50,16,128]{4,3,2,1,0:T(8,128)S(1)} %bitcast.34) | data formatting | bytes 3276800
  82.3 0.6 fusion.6
  82.9 1.3 %fusion.3 = f32[2,2,50,16,128]{4,3,2,1,0:T(8,128)} fusion(f32[2,2,50,16,128]{4,3,2,1,0:T(8,128)} %fusion.6, f32[2,16,128]{2,1,0:T(8,128)S(1)} %copy-done.6, f32[2,16,128]{2,1,0:T(8,128)S(1)} %copy-done.7, f32[2,2,50,16,128]{4,3,2,1,0:T(8,128)S(1)} %bitcast.37, f32[16,128]{1,0:T(8,128)S(1)} %fusion.7), kind=kLoop, calls=%fused_computation.24 | loop fusion | flops 53248 | bytes 90112 | tf_op jit(solution)/shard_map/scatter-add | solution.py:202
  84.3 7.1 %all-to-all-done.1 = f32[8,100,128]{2,1,0:T(8,128)S(1)} async-done(((f32[8,100,128]{2,1,0:T(8,128)}), f32[8,100,128]{2,1,0:T(8,128)S(1)}, u32[]{:S(2)}, u32[]{:S(2)}) %all-to-all-start.1) | async-done | bytes 409632 | tf_op jit(solution)/shard_map/all_to_all | solution.py:81
  91.4 0.9 fusion.2
  (34 shorter events, 0.4 us)
Async XLA Ops:
  1.4 7.8 %copy-start.8 = (f32[50]{0:T(128)S(1)}, f32[50]{0:T(128)}, u32[]{:S(2)}) copy-start(f32[50]{0:T(128)} %param.25) | copy-start | bytes 604
  2.7 8.7 %copy-start.4 = (f32[50,16,128]{2,1,0:T(8,128)S(1)}, f32[50,16,128]{2,1,0:T(8,128)}, u32[]{:S(2)}) copy-start(f32[50,16,128]{2,1,0:T(8,128)} %param.24) | copy-start | bytes 1228804
  2.7 22.0 %collective-permute-start.3 = (f32[101,6,128]{2,1,0:T(8,128)S(1)}, f32[101,6,128]{2,1,0:T(8,128)S(1)}, u32[]{:S(2)}, u32[]{:S(2)}) collective-permute-start(f32[101,6,128]{2,1,0:T(8,128)S(1)} %pad_maximum_fusion.1), channel_id=1, source_target_pairs={{1,0},{2,1},{3,2},{4,3},{5,4},{6,5},{7,6},{8,7},{9,8},{10,9},{11,1... | collective-permute-start | bytes 930824 | tf_op jit(solution)/shard_map/ppermute | solution.py:129
  9.1 15.6 %collective-permute-start.2 = (f32[101,6,128]{2,1,0:T(8,128)S(1)}, f32[101,6,128]{2,1,0:T(8,128)S(1)}, u32[]{:S(2)}, u32[]{:S(2)}) collective-permute-start(f32[101,6,128]{2,1,0:T(8,128)S(1)} %pad_maximum_fusion), channel_id=1, source_target_pairs={{0,1},{1,2},{2,3},{3,4},{4,5},{5,6},{6,7},{7,8},{8,9},{9,10},{10,1... | collective-permute-start | bytes 930824 | tf_op jit(solution)/shard_map/ppermute | solution.py:128
  18.5 14.5 %collective-permute-start.1 = (f32[200,6,128]{2,0,1:T(8,128)S(1)}, f32[200,6,128]{2,0,1:T(8,128)S(1)}, u32[]{:S(2)}, u32[]{:S(2)}) collective-permute-start(f32[200,6,128]{2,0,1:T(8,128)S(1)} %copy.26), channel_id=1, source_target_pairs={{1,0},{2,1},{3,2},{4,3},{5,4},{6,5},{7,6},{8,7},{9,8},{10,9},{11,1... | collective-permute-start | bytes 1843208 | tf_op jit(solution)/shard_map/ppermute | solution.py:129
  24.3 13.7 %collective-permute-start = (f32[200,6,128]{2,0,1:T(8,128)S(1)}, f32[200,6,128]{2,0,1:T(8,128)S(1)}, u32[]{:S(2)}, u32[]{:S(2)}) collective-permute-start(f32[200,6,128]{2,0,1:T(8,128)S(1)} %copy.25), channel_id=1, source_target_pairs={{0,1},{1,2},{2,3},{3,4},{4,5},{5,6},{6,7},{7,8},{8,9},{9,10},{10,1... | collective-permute-start | bytes 1843208 | tf_op jit(solution)/shard_map/ppermute | solution.py:128
  25.0 1.0 %copy-start.2 = (f32[50,16,128]{2,1,0:T(8,128)S(1)}, f32[50,16,128]{2,1,0:T(8,128)}, u32[]{:S(2)}) copy-start(f32[50,16,128]{2,1,0:T(8,128)} %param.21) | copy-start | bytes 1228804
  25.0 1.0 %copy-start.10 = (f32[50]{0:T(128)S(1)}, f32[50]{0:T(128)}, u32[]{:S(2)}) copy-start(f32[50]{0:T(128)} %param.23) | copy-start | bytes 604
  26.0 1.8 %copy-start.3 = (f32[50,16,128]{2,1,0:T(8,128)S(1)}, f32[50,16,128]{2,1,0:T(8,128)}, u32[]{:S(2)}) copy-start(f32[50,16,128]{2,1,0:T(8,128)} %param.20) | copy-start | bytes 1228804
  26.0 1.8 %copy-start.11 = (f32[50]{0:T(128)S(1)}, f32[50]{0:T(128)}, u32[]{:S(2)}) copy-start(f32[50]{0:T(128)} %param.22) | copy-start | bytes 604
  29.6 8.6 %copy-start.1 = (f32[4,50,16,128]{3,2,1,0:T(8,128)S(1)}, f32[4,50,16,128]{3,2,1,0:T(8,128)}, u32[]{:S(2)}) copy-start(f32[4,50,16,128]{3,2,1,0:T(8,128)} %shard_map.140) | copy-start | bytes 4915204
  55.9 25.2 %copy-start.9 = (f32[16,128]{1,0:T(8,128)S(1)}, f32[16,128]{1,0:T(8,128)}, u32[]{:S(2)}) copy-start(f32[16,128]{1,0:T(8,128)} %param.27) | copy-start | bytes 24580
  55.9 25.2 %copy-start = (f32[4,50,16,128]{3,2,1,0:T(8,128)S(1)}, f32[4,50,16,128]{3,2,1,0:T(8,128)}, u32[]{:S(2)}) copy-start(f32[4,50,16,128]{3,2,1,0:T(8,128)} %shard_map.141) | copy-start | bytes 4915204
  76.0 15.4 %all-to-all-start.1 = ((f32[8,100,128]{2,1,0:T(8,128)}), f32[8,100,128]{2,1,0:T(8,128)S(1)}, u32[]{:S(2)}, u32[]{:S(2)}) async-start(f32[8,100,128]{2,1,0:T(8,128)} %broadcast_in_dim.13), calls=%async_computation.1 | async-start | bytes 851968 | tf_op jit(solution)/shard_map/all_to_all | solution.py:81
  81.1 1.2 %copy-start.6 = (f32[2,16,128]{2,1,0:T(8,128)S(1)}, f32[2,16,128]{2,1,0:T(8,128)}, u32[]{:S(2)}) copy-start(f32[2,16,128]{2,1,0:T(8,128)} %param.19) | copy-start | bytes 49156
  81.1 1.2 %copy-start.7 = (f32[2,16,128]{2,1,0:T(8,128)S(1)}, f32[2,16,128]{2,1,0:T(8,128)}, u32[]{:S(2)}) copy-start(f32[2,16,128]{2,1,0:T(8,128)} %param.18) | copy-start | bytes 49156
  81.1 10.3 %copy-start.5 = (f32[50,16,128]{2,1,0:T(8,128)S(1)}, f32[50,16,128]{2,1,0:T(8,128)}, u32[]{:S(2)}) copy-start(f32[50,16,128]{2,1,0:T(8,128)} %param.26) | copy-start | bytes 1228804

commit v9 on v8

--- a/solution.py
+++ b/solution.py
@@ -107,7 +107,7 @@
 
 def transport_substeps(adjoint, east_a, east_b, north_a, north_b, width):
     fields, levels, columns, lanes = adjoint.shape
-    chunk = 25 if levels % 25 == 0 else levels
+    chunk = levels
     field_block = pl.BlockSpec((fields, chunk, columns, lanes), lambda j: (0, j, 0, 0))
     face_block = pl.BlockSpec((chunk, columns, lanes), lambda j: (j, 0, 0))
     return pl.pallas_call(

time: 92.8 us -> 95.7 us (1.031)
  Pallas kernels: 17.3 us -> 20.2 us
    pallas_call x1, Pallas kernels: 13.8 us -> 16.7 us  [transport_substeps(): pl.pallas_call(substep_kernel, grid=(levels // chunk,), in_specs=[field_b...]
  transfers between devices with their start and end apart: 5 -> 5, of which waited for: 3 -> 3; matrix products, arithmetic and copies ran while one was open for 15% -> 14% of each run, Pallas kernels for 4% -> 4%
where the time goes in v9:
time: 95.7 us; the launch traced here: 95.2 us
  Pallas kernels  20.2 us (21%)
  blocking collectives  19.2 us (20%)
  starting transfers between devices  17.4 us (18%)
  waiting for transfers between devices  15.4 us (16%)
  other arithmetic  14.8 us (15%)
  local copies, waits for them, and re-layouts  7.27 us (8%)
    all_to_all x1, blocking collectives, scenario_sum(): gathered = lax.all_to_all(pieces, 'scen', 0, 0, tiled=True)  19.2 us
    pallas_call x1, Pallas kernels, transport_substeps(): pl.pallas_call(substep_kernel, grid=(levels // chunk,), in_specs=[field_b...  16.7 us
    ppermute x2, starting transfers between devices, padded_halo(): after = lax.ppermute(initial, 'grid', down)  12 us
    all_to_all x1, waiting for transfers between devices, scenario_sum(): return lax.all_to_all(spread, 'scen', 0, 0, tiled=True).reshape(shape)  7.11 us
    all_to_all x1, starting transfers between devices, scenario_sum(): return lax.all_to_all(spread, 'scen', 0, 0, tiled=True).reshape(shape)  5.05 us
    ppermute x2, waiting for transfers between devices, padded_halo(): before = lax.ppermute(last, 'grid', up)  4.88 us
    sub x2, other arithmetic, face_pairs(): jnp.minimum(moving, 0.0) - mixing  3.56 us
    pallas_call x1, Pallas kernels, transposed_solve(): pl.pallas_call(solve_kernel, out_shape=jax.ShapeDtypeStruct(rhs.shape, jn...  3.48 us
  transfers between devices with their start and end apart: 5, of which 3 were waited for; matrix products, arithmetic and copies ran while one was open for 14% of the time, Pallas kernels for 4%

profile of v9, /device:TPU:8, one launch (start us, length us, event | category | flops | bytes accessed | tf_op | source)
XLA Modules:
  0.0 95.2 jit_solution(13894671135294762099)
XLA Ops:
  0.6 0.7 select_convert_fusion
  1.4 1.3 %fusion.11 = (f32[50,6,128]{2,1,0:T(8,128)S(1)}, f32[50,6,128]{2,1,0:T(8,128)S(1)}, f32[50,6,128]{2,1,0:T(8,128)S(1)}, f32[50,6,128]{2,1,0:T(8,128)S(1)}) fusion(f32[50,16,128]{2,1,0:T(8,128)} %param.20, f32[50,16,128]{2,1,0:T(8,128)} %param.21), kind=kLoop, calls=%fused_computation.41 | loop fusion | bytes 1228800 | tf_op jit(solution)/shard_map/slice | solution.py:126
  2.7 0.0 copy-start.4
  2.7 6.3 %collective-permute-start.3 = (f32[101,6,128]{2,1,0:T(8,128)S(1)}, f32[101,6,128]{2,1,0:T(8,128)S(1)}, u32[]{:S(2)}, u32[]{:S(2)}) collective-permute-start(f32[101,6,128]{2,1,0:T(8,128)S(1)} %pad_maximum_fusion.1), channel_id=1, source_target_pairs={{1,0},{2,1},{3,2},{4,3},{5,4},{6,5},{7,6},{8,7},{9,8},{10,9},{11,1... | collective-permute-start | bytes 930824 | tf_op jit(solution)/shard_map/ppermute | solution.py:129
  9.1 0.1 collective-permute-start.2
  9.2 0.1 fusion.15
  9.3 0.6 fusion.14
  9.9 0.1 compare_convert_fusion.1
  10.0 1.4 %pad_maximum_fusion.2 = (f32[50]{0:T(128)S(1)}, f32[50]{0:T(128)S(1)}) fusion(f32[49]{0:T(128)S(1)} %get-tuple-element.48, f32[1]{0:T(128)} %get-tuple-element.46, f32[1]{0:T(128)} %get-tuple-element.47, f32[49]{0:T(128)S(1)} %get-tuple-element.49), kind=kLoop, calls=%fused_computation.35 | loop fusion | flops 100 | bytes 800 | tf_op jit(solution)/shard_map/concatenate | solution.py:27
  11.4 0.9 negate_divide_fusion
  12.3 1.1 %divide_add_fusion = (f32[50,16,128]{2,1,0:T(8,128)}, f32[50,16,128]{2,1,0:T(8,128)}) fusion(f32[50,16,128]{2,1,0:T(8,128)S(1)} %get-tuple-element.27, f32[49,16,128]{2,1,0:T(8,128)S(1)} %slice.189, f32[50]{0:T(128)S(1)} %copy-done.8, f32[50]{0:T(128)S(1)} %get-tuple-element.50), kind=kLoop, calls=%fused_computation.19 | loop fusion | flops 512000 | bytes 1630608 | tf_op jit(solution)/shard_map/add | solution.py:29
  13.4 3.5 %shard_map.140 = f32[4,50,16,128]{3,2,1,0:T(8,128)} custom-call(f32[4,50,16,128]{3,2,1,0:T(8,128)} %bitcast.41, f32[50,16,128]{2,1,0:T(8,128)} %get-tuple-element.43.below_ref, f32[50,16,128]{2,1,0:T(8,128)} %get-tuple-element.42.diagonal_ref, f32[50,16,128]{2,1,0:T(8,128)} %get-tuple-element.26.above_ref), custom_call_target="tpu_custom_call" | custom-call | tf_op jit(solution)/shard_map/pallas_call | solution.py:56
  16.9 1.5 %fusion.8 = (f32[200,6,128]{2,1,0:T(8,128)S(1)}, f32[200,6,128]{2,1,0:T(8,128)S(1)}) fusion(f32[200,16,128]{2,1,0:T(8,128)} %bitcast.38), kind=kLoop, calls=%fused_computation.38 | loop fusion | bytes 2457600 | tf_op jit(solution)/shard_map/slice | solution.py:126
  18.4 0.1 copy.26
  18.5 5.7 %collective-permute-start.1 = (f32[200,6,128]{2,0,1:T(8,128)S(1)}, f32[200,6,128]{2,0,1:T(8,128)S(1)}, u32[]{:S(2)}, u32[]{:S(2)}) collective-permute-start(f32[200,6,128]{2,0,1:T(8,128)S(1)} %copy.26), channel_id=1, source_target_pairs={{1,0},{2,1},{3,2},{4,3},{5,4},{6,5},{7,6},{8,7},{9,8},{10,9},{11,1... | collective-permute-start | bytes 1843208 | tf_op jit(solution)/shard_map/ppermute | solution.py:129
  24.2 0.1 copy.25
  24.3 0.3 collective-permute-start
  24.6 0.1 pad.34.clone
  24.7 0.0 collective-permute-done.3
  24.7 0.1 maximum_bitcast_fusion
  24.8 0.1 compare_convert_fusion
  25.0 0.0 copy-start.2
  25.0 0.0 copy-start.10
  25.0 0.1 slice.196
  25.1 0.3 slice.200
  25.4 0.6 copy-done.2
  26.0 1.8 %minimum_subtract_fusion = (f32[50,32,128]{2,1,0:T(8,128)}, f32[50,32,128]{2,1,0:T(8,128)}) fusion(f32[50,32,127]{2,1,0:T(8,128)S(1)} %slice.200, f32[50,6,128]{2,1,0:T(8,128)S(1)} %get-tuple-element.36, f32[50,16,128]{2,1,0:T(8,128)S(1)} %copy-done.2, f32[50,6,128]{2,1,0:T(8,128)S(1)} %get-tuple-element.34, f32[32]{0:T(128)S(1)} %pad.34.clone, ...), kind=kLoop, calls=%fused_computation.9 | loop fusion | flops 2252800 | bytes 3184912 | tf_op jit(solution)/shard_map/sub | solution.py:18
  27.8 1.8 %minimum_subtract_fusion.1 = (f32[50,32,128]{2,1,0:T(8,128)}, f32[50,32,128]{2,1,0:T(8,128)}) fusion(f32[32]{0:T(128)S(1)} %pad.34.clone, f32[50,6,128]{2,1,0:T(8,128)S(1)} %get-tuple-element.37, f32[50,16,128]{2,1,0:T(8,128)S(1)} %copy-done.3, f32[50,6,128]{2,1,0:T(8,128)S(1)} %get-tuple-element.35, f32[50,1,128]{2,1,0:T(1,128)S(1)} %slice.197, ...), kind=kLoop, calls=%fused_computation.11 | loop fusion | flops 2457600 | bytes 3191312 | tf_op jit(solution)/shard_map/sub | solution.py:18
  29.6 3.4 %collective-permute-done.1 = f32[200,6,128]{2,0,1:T(8,128)S(1)} collective-permute-done((f32[200,6,128]{2,0,1:T(8,128)S(1)}, f32[200,6,128]{2,0,1:T(8,128)S(1)}, u32[]{:S(2)}, u32[]{:S(2)}) %collective-permute-start.1) | collective-permute-done | bytes 614432 | tf_op jit(solution)/shard_map/ppermute | solution.py:129
  33.0 0.2 copy.22
  33.2 4.9 %collective-permute-done = f32[200,6,128]{2,0,1:T(8,128)S(1)} collective-permute-done((f32[200,6,128]{2,0,1:T(8,128)S(1)}, f32[200,6,128]{2,0,1:T(8,128)S(1)}, u32[]{:S(2)}, u32[]{:S(2)}) %collective-permute-start) | collective-permute-done | bytes 614432 | tf_op jit(solution)/shard_map/ppermute | solution.py:128
  38.1 0.2 copy.20
  38.2 2.3 %maximum_maximum_fusion.adjoint_ref = f32[4,50,32,128]{3,2,1,0:T(8,128)} fusion(f32[4,50,6,128]{3,2,1,0:T(8,128)S(1)} %bitcast.39, f32[4,50,16,128]{3,2,1,0:T(8,128)S(1)} %copy-done.1, f32[4,50,6,128]{3,2,1,0:T(8,128)S(1)} %bitcast.40, f32[32]{0:T(128)S(1)} %pad.34.clone), kind=kLoop, calls=%fused_computation | loop fusion | flops 2457600 | bytes 6144128 | tf_op jit(solution)/shard_map/concatenate | solution.py:136
  40.5 16.7 %shard_map.141 = f32[4,50,16,128]{3,2,1,0:T(8,128)} custom-call(f32[4,50,32,128]{3,2,1,0:T(8,128)} %maximum_maximum_fusion.adjoint_ref, f32[50,32,128]{2,1,0:T(8,128)} %get-tuple-element.29.east_a_ref, f32[50,32,128]{2,1,0:T(8,128)} %get-tuple-element.28.east_b_ref, f32[50,32,128]{2,1,0:T(8,128)} %get-tuple-element.31.north_a_ref, ...), custom_call_target="tpu_custom_call" | custom-call | tf_op jit(solution)/shard_map/pallas_call | solution.py:113
  57.2 1.6 %fusion.1 = f32[50,16,128]{2,1,0:T(8,128)S(1)} fusion(f32[2,2,50,16,128]{4,3,2,1,0:T(8,128)} %bitcast.33), kind=kLoop, calls=%fused_computation.6 | loop fusion | flops 512000 | bytes 2048000 | tf_op jit(solution)/shard_map/reduce_sum | solution.py:193
  58.8 0.0 copy-start.9
  58.8 0.0 copy-start
  58.9 19.2 %all_to_all.10 = f32[8,100,128]{2,1,0:T(8,128)S(1)} all-to-all(f32[8,100,128]{2,1,0:T(8,128)S(1)} %reshape.126), channel_id=1, replica_groups=mesh['scen'=8,'grid'=32] {'scen'}, dimensions={0} | all-to-all | bytes 819200 | tf_op jit(solution)/shard_map/all_to_all | solution.py:78
  78.1 0.8 broadcast_in_dim.13
  78.9 5.1 %all-to-all-start.1 = ((f32[8,100,128]{2,1,0:T(8,128)}), f32[8,100,128]{2,1,0:T(8,128)S(1)}, u32[]{:S(2)}, u32[]{:S(2)}) async-start(f32[8,100,128]{2,1,0:T(8,128)} %broadcast_in_dim.13), calls=%async_computation.1 | async-start | bytes 851968 | tf_op jit(solution)/shard_map/all_to_all | solution.py:81
  84.0 0.0 copy-start.6
  84.0 0.0 copy-start.7
  84.0 0.0 copy-start.5
  84.0 1.2 %copy.28 = f32[2,2,50,16,128]{4,3,2,1,0:T(8,128)} copy(f32[2,2,50,16,128]{4,3,2,1,0:T(8,128)S(1)} %bitcast.34) | data formatting | bytes 3276800
  85.2 0.6 fusion.6
  85.8 1.3 %fusion.3 = f32[2,2,50,16,128]{4,3,2,1,0:T(8,128)} fusion(f32[2,2,50,16,128]{4,3,2,1,0:T(8,128)} %fusion.6, f32[2,16,128]{2,1,0:T(8,128)S(1)} %copy-done.6, f32[2,16,128]{2,1,0:T(8,128)S(1)} %copy-done.7, f32[2,2,50,16,128]{4,3,2,1,0:T(8,128)S(1)} %bitcast.37, f32[16,128]{1,0:T(8,128)S(1)} %fusion.7), kind=kLoop, calls=%fused_computation.24 | loop fusion | flops 53248 | bytes 90112 | tf_op jit(solution)/shard_map/scatter-add | solution.py:202
  87.2 7.1 %all-to-all-done.1 = f32[8,100,128]{2,1,0:T(8,128)S(1)} async-done(((f32[8,100,128]{2,1,0:T(8,128)}), f32[8,100,128]{2,1,0:T(8,128)S(1)}, u32[]{:S(2)}, u32[]{:S(2)}) %all-to-all-start.1) | async-done | bytes 409632 | tf_op jit(solution)/shard_map/all_to_all | solution.py:81
  94.3 0.9 fusion.2
  (34 shorter events, 0.4 us)
Async XLA Ops:
  1.4 7.8 %copy-start.8 = (f32[50]{0:T(128)S(1)}, f32[50]{0:T(128)}, u32[]{:S(2)}) copy-start(f32[50]{0:T(128)} %param.25) | copy-start | bytes 604
  2.7 8.7 %copy-start.4 = (f32[50,16,128]{2,1,0:T(8,128)S(1)}, f32[50,16,128]{2,1,0:T(8,128)}, u32[]{:S(2)}) copy-start(f32[50,16,128]{2,1,0:T(8,128)} %param.24) | copy-start | bytes 1228804
  2.7 22.0 %collective-permute-start.3 = (f32[101,6,128]{2,1,0:T(8,128)S(1)}, f32[101,6,128]{2,1,0:T(8,128)S(1)}, u32[]{:S(2)}, u32[]{:S(2)}) collective-permute-start(f32[101,6,128]{2,1,0:T(8,128)S(1)} %pad_maximum_fusion.1), channel_id=1, source_target_pairs={{1,0},{2,1},{3,2},{4,3},{5,4},{6,5},{7,6},{8,7},{9,8},{10,9},{11,1... | collective-permute-start | bytes 930824 | tf_op jit(solution)/shard_map/ppermute | solution.py:129
  9.1 15.6 %collective-permute-start.2 = (f32[101,6,128]{2,1,0:T(8,128)S(1)}, f32[101,6,128]{2,1,0:T(8,128)S(1)}, u32[]{:S(2)}, u32[]{:S(2)}) collective-permute-start(f32[101,6,128]{2,1,0:T(8,128)S(1)} %pad_maximum_fusion), channel_id=1, source_target_pairs={{0,1},{1,2},{2,3},{3,4},{4,5},{5,6},{6,7},{7,8},{8,9},{9,10},{10,1... | collective-permute-start | bytes 930824 | tf_op jit(solution)/shard_map/ppermute | solution.py:128
  18.5 14.5 %collective-permute-start.1 = (f32[200,6,128]{2,0,1:T(8,128)S(1)}, f32[200,6,128]{2,0,1:T(8,128)S(1)}, u32[]{:S(2)}, u32[]{:S(2)}) collective-permute-start(f32[200,6,128]{2,0,1:T(8,128)S(1)} %copy.26), channel_id=1, source_target_pairs={{1,0},{2,1},{3,2},{4,3},{5,4},{6,5},{7,6},{8,7},{9,8},{10,9},{11,1... | collective-permute-start | bytes 1843208 | tf_op jit(solution)/shard_map/ppermute | solution.py:129
  24.3 13.7 %collective-permute-start = (f32[200,6,128]{2,0,1:T(8,128)S(1)}, f32[200,6,128]{2,0,1:T(8,128)S(1)}, u32[]{:S(2)}, u32[]{:S(2)}) collective-permute-start(f32[200,6,128]{2,0,1:T(8,128)S(1)} %copy.25), channel_id=1, source_target_pairs={{0,1},{1,2},{2,3},{3,4},{4,5},{5,6},{6,7},{7,8},{8,9},{9,10},{10,1... | collective-permute-start | bytes 1843208 | tf_op jit(solution)/shard_map/ppermute | solution.py:128
  25.0 1.0 %copy-start.2 = (f32[50,16,128]{2,1,0:T(8,128)S(1)}, f32[50,16,128]{2,1,0:T(8,128)}, u32[]{:S(2)}) copy-start(f32[50,16,128]{2,1,0:T(8,128)} %param.21) | copy-start | bytes 1228804
  25.0 1.0 %copy-start.10 = (f32[50]{0:T(128)S(1)}, f32[50]{0:T(128)}, u32[]{:S(2)}) copy-start(f32[50]{0:T(128)} %param.23) | copy-start | bytes 604
  26.0 1.8 %copy-start.3 = (f32[50,16,128]{2,1,0:T(8,128)S(1)}, f32[50,16,128]{2,1,0:T(8,128)}, u32[]{:S(2)}) copy-start(f32[50,16,128]{2,1,0:T(8,128)} %param.20) | copy-start | bytes 1228804
  26.0 1.8 %copy-start.11 = (f32[50]{0:T(128)S(1)}, f32[50]{0:T(128)}, u32[]{:S(2)}) copy-start(f32[50]{0:T(128)} %param.22) | copy-start | bytes 604
  29.6 8.6 %copy-start.1 = (f32[4,50,16,128]{3,2,1,0:T(8,128)S(1)}, f32[4,50,16,128]{3,2,1,0:T(8,128)}, u32[]{:S(2)}) copy-start(f32[4,50,16,128]{3,2,1,0:T(8,128)} %shard_map.140) | copy-start | bytes 4915204
  58.8 25.2 %copy-start.9 = (f32[16,128]{1,0:T(8,128)S(1)}, f32[16,128]{1,0:T(8,128)}, u32[]{:S(2)}) copy-start(f32[16,128]{1,0:T(8,128)} %param.27) | copy-start | bytes 24580
  58.8 25.2 %copy-start = (f32[4,50,16,128]{3,2,1,0:T(8,128)S(1)}, f32[4,50,16,128]{3,2,1,0:T(8,128)}, u32[]{:S(2)}) copy-start(f32[4,50,16,128]{3,2,1,0:T(8,128)} %shard_map.141) | copy-start | bytes 4915204
  78.9 15.4 %all-to-all-start.1 = ((f32[8,100,128]{2,1,0:T(8,128)}), f32[8,100,128]{2,1,0:T(8,128)S(1)}, u32[]{:S(2)}, u32[]{:S(2)}) async-start(f32[8,100,128]{2,1,0:T(8,128)} %broadcast_in_dim.13), calls=%async_computation.1 | async-start | bytes 851968 | tf_op jit(solution)/shard_map/all_to_all | solution.py:81
  84.0 1.2 %copy-start.6 = (f32[2,16,128]{2,1,0:T(8,128)S(1)}, f32[2,16,128]{2,1,0:T(8,128)}, u32[]{:S(2)}) copy-start(f32[2,16,128]{2,1,0:T(8,128)} %param.19) | copy-start | bytes 49156
  84.0 1.2 %copy-start.7 = (f32[2,16,128]{2,1,0:T(8,128)S(1)}, f32[2,16,128]{2,1,0:T(8,128)}, u32[]{:S(2)}) copy-start(f32[2,16,128]{2,1,0:T(8,128)} %param.18) | copy-start | bytes 49156
  84.0 10.3 %copy-start.5 = (f32[50,16,128]{2,1,0:T(8,128)S(1)}, f32[50,16,128]{2,1,0:T(8,128)}, u32[]{:S(2)}) copy-start(f32[50,16,128]{2,1,0:T(8,128)} %param.26) | copy-start | bytes 1228804

commit v10 on v9

--- a/solution.py
+++ b/solution.py
@@ -107,14 +107,13 @@
 
 def transport_substeps(adjoint, east_a, east_b, north_a, north_b, width):
     fields, levels, columns, lanes = adjoint.shape
-    chunk = levels
-    field_block = pl.BlockSpec((fields, chunk, columns, lanes), lambda j: (0, j, 0, 0))
-    face_block = pl.BlockSpec((chunk, columns, lanes), lambda j: (j, 0, 0))
+    field_block = pl.BlockSpec((1, levels, columns, lanes), lambda j: (j, 0, 0, 0))
+    face_block = pl.BlockSpec((levels, columns, lanes), lambda j: (0, 0, 0))
     return pl.pallas_call(
         substep_kernel,
-        grid=(levels // chunk,),
+        grid=(fields,),
         in_specs=[field_block, face_block, face_block, face_block, face_block],
-        out_specs=pl.BlockSpec((fields, chunk, width, lanes), lambda j: (0, j, 0, 0)),
+        out_specs=pl.BlockSpec((1, levels, width, lanes), lambda j: (j, 0, 0, 0)),
         out_shape=jax.ShapeDtypeStruct((fields, levels, width, lanes), jnp.float32),
     )(adjoint, east_a, east_b, north_a, north_b)
 

time: 95.7 us -> 95.3 us (level)
  no operation moved by 1% of the time
where the time goes in v10:
time: 95.3 us; the launch traced here: 94.8 us
  Pallas kernels  20 us (21%)
  blocking collectives  19.2 us (20%)
  starting transfers between devices  17.3 us (18%)
  waiting for transfers between devices  15.4 us (16%)
  other arithmetic  14.8 us (16%)
  local copies, waits for them, and re-layouts  7.27 us (8%)
    all_to_all x1, blocking collectives, scenario_sum(): gathered = lax.all_to_all(pieces, 'scen', 0, 0, tiled=True)  19.2 us
    pallas_call x1, Pallas kernels, transport_substeps(): pl.pallas_call(substep_kernel, grid=(fields,), in_specs=[field_block, fac...  16.5 us
    ppermute x2, starting transfers between devices, padded_halo(): after = lax.ppermute(initial, 'grid', down)  12 us
    all_to_all x1, waiting for transfers between devices, scenario_sum(): return lax.all_to_all(spread, 'scen', 0, 0, tiled=True).reshape(shape)  7.11 us
    all_to_all x1, starting transfers between devices, scenario_sum(): return lax.all_to_all(spread, 'scen', 0, 0, tiled=True).reshape(shape)  5.05 us
    ppermute x2, waiting for transfers between devices, padded_halo(): before = lax.ppermute(last, 'grid', up)  4.88 us
    sub x2, other arithmetic, face_pairs(): jnp.minimum(moving, 0.0) - mixing  3.56 us
    pallas_call x1, Pallas kernels, transposed_solve(): pl.pallas_call(solve_kernel, out_shape=jax.ShapeDtypeStruct(rhs.shape, jn...  3.48 us
  transfers between devices with their start and end apart: 5, of which 3 were waited for; matrix products, arithmetic and copies ran while one was open for 14% of the time, Pallas kernels for 4%

profile of v10, /device:TPU:8, one launch (start us, length us, event | category | flops | bytes accessed | tf_op | source)
XLA Modules:
  0.0 94.8 jit_solution(1728227970798034746)
XLA Ops:
  0.6 0.7 select_convert_fusion
  1.4 1.3 %fusion.11 = (f32[50,6,128]{2,1,0:T(8,128)S(1)}, f32[50,6,128]{2,1,0:T(8,128)S(1)}, f32[50,6,128]{2,1,0:T(8,128)S(1)}, f32[50,6,128]{2,1,0:T(8,128)S(1)}) fusion(f32[50,16,128]{2,1,0:T(8,128)} %param.20, f32[50,16,128]{2,1,0:T(8,128)} %param.21), kind=kLoop, calls=%fused_computation.41 | loop fusion | bytes 1228800 | tf_op jit(solution)/shard_map/slice | solution.py:125
  2.7 0.0 copy-start.4
  2.7 6.3 %collective-permute-start.3 = (f32[101,6,128]{2,1,0:T(8,128)S(1)}, f32[101,6,128]{2,1,0:T(8,128)S(1)}, u32[]{:S(2)}, u32[]{:S(2)}) collective-permute-start(f32[101,6,128]{2,1,0:T(8,128)S(1)} %pad_maximum_fusion.1), channel_id=1, source_target_pairs={{1,0},{2,1},{3,2},{4,3},{5,4},{6,5},{7,6},{8,7},{9,8},{10,9},{11,1... | collective-permute-start | bytes 930824 | tf_op jit(solution)/shard_map/ppermute | solution.py:128
  9.1 0.1 collective-permute-start.2
  9.2 0.1 fusion.15
  9.3 0.6 fusion.14
  9.9 0.1 compare_convert_fusion.1
  10.0 1.4 %pad_maximum_fusion.2 = (f32[50]{0:T(128)S(1)}, f32[50]{0:T(128)S(1)}) fusion(f32[49]{0:T(128)S(1)} %get-tuple-element.48, f32[1]{0:T(128)} %get-tuple-element.46, f32[1]{0:T(128)} %get-tuple-element.47, f32[49]{0:T(128)S(1)} %get-tuple-element.49), kind=kLoop, calls=%fused_computation.35 | loop fusion | flops 100 | bytes 800 | tf_op jit(solution)/shard_map/concatenate | solution.py:27
  11.4 0.9 negate_divide_fusion
  12.3 1.1 %divide_add_fusion = (f32[50,16,128]{2,1,0:T(8,128)}, f32[50,16,128]{2,1,0:T(8,128)}) fusion(f32[50,16,128]{2,1,0:T(8,128)S(1)} %get-tuple-element.27, f32[49,16,128]{2,1,0:T(8,128)S(1)} %slice.189, f32[50]{0:T(128)S(1)} %copy-done.8, f32[50]{0:T(128)S(1)} %get-tuple-element.50), kind=kLoop, calls=%fused_computation.19 | loop fusion | flops 512000 | bytes 1630608 | tf_op jit(solution)/shard_map/add | solution.py:29
  13.4 3.5 %shard_map.140 = f32[4,50,16,128]{3,2,1,0:T(8,128)} custom-call(f32[4,50,16,128]{3,2,1,0:T(8,128)} %bitcast.41, f32[50,16,128]{2,1,0:T(8,128)} %get-tuple-element.43.below_ref, f32[50,16,128]{2,1,0:T(8,128)} %get-tuple-element.42.diagonal_ref, f32[50,16,128]{2,1,0:T(8,128)} %get-tuple-element.26.above_ref), custom_call_target="tpu_custom_call" | custom-call | tf_op jit(solution)/shard_map/pallas_call | solution.py:56
  16.9 1.5 %fusion.8 = (f32[200,6,128]{2,1,0:T(8,128)S(1)}, f32[200,6,128]{2,1,0:T(8,128)S(1)}) fusion(f32[200,16,128]{2,1,0:T(8,128)} %bitcast.38), kind=kLoop, calls=%fused_computation.38 | loop fusion | bytes 2457600 | tf_op jit(solution)/shard_map/slice | solution.py:125
  18.4 0.1 copy.26
  18.5 5.7 %collective-permute-start.1 = (f32[200,6,128]{2,0,1:T(8,128)S(1)}, f32[200,6,128]{2,0,1:T(8,128)S(1)}, u32[]{:S(2)}, u32[]{:S(2)}) collective-permute-start(f32[200,6,128]{2,0,1:T(8,128)S(1)} %copy.26), channel_id=1, source_target_pairs={{1,0},{2,1},{3,2},{4,3},{5,4},{6,5},{7,6},{8,7},{9,8},{10,9},{11,1... | collective-permute-start | bytes 1843208 | tf_op jit(solution)/shard_map/ppermute | solution.py:128
  24.2 0.1 copy.25
  24.3 0.1 collective-permute-start
  24.4 0.1 pad.34.clone
  24.5 0.0 collective-permute-done.3
  24.5 0.1 maximum_bitcast_fusion
  24.6 0.1 compare_convert_fusion
  24.8 0.0 copy-start.2
  24.8 0.0 copy-start.10
  24.8 0.1 slice.196
  24.9 0.3 slice.200
  25.2 0.6 copy-done.2
  25.8 1.8 %minimum_subtract_fusion = (f32[50,32,128]{2,1,0:T(8,128)}, f32[50,32,128]{2,1,0:T(8,128)}) fusion(f32[50,32,127]{2,1,0:T(8,128)S(1)} %slice.200, f32[50,6,128]{2,1,0:T(8,128)S(1)} %get-tuple-element.36, f32[50,16,128]{2,1,0:T(8,128)S(1)} %copy-done.2, f32[50,6,128]{2,1,0:T(8,128)S(1)} %get-tuple-element.34, f32[32]{0:T(128)S(1)} %pad.34.clone, ...), kind=kLoop, calls=%fused_computation.9 | loop fusion | flops 2252800 | bytes 3184912 | tf_op jit(solution)/shard_map/sub | solution.py:18
  27.7 1.8 %minimum_subtract_fusion.1 = (f32[50,32,128]{2,1,0:T(8,128)}, f32[50,32,128]{2,1,0:T(8,128)}) fusion(f32[32]{0:T(128)S(1)} %pad.34.clone, f32[50,6,128]{2,1,0:T(8,128)S(1)} %get-tuple-element.37, f32[50,16,128]{2,1,0:T(8,128)S(1)} %copy-done.3, f32[50,6,128]{2,1,0:T(8,128)S(1)} %get-tuple-element.35, f32[50,1,128]{2,1,0:T(1,128)S(1)} %slice.197, ...), kind=kLoop, calls=%fused_computation.11 | loop fusion | flops 2457600 | bytes 3191312 | tf_op jit(solution)/shard_map/sub | solution.py:18
  29.4 3.4 %collective-permute-done.1 = f32[200,6,128]{2,0,1:T(8,128)S(1)} collective-permute-done((f32[200,6,128]{2,0,1:T(8,128)S(1)}, f32[200,6,128]{2,0,1:T(8,128)S(1)}, u32[]{:S(2)}, u32[]{:S(2)}) %collective-permute-start.1) | collective-permute-done | bytes 614432 | tf_op jit(solution)/shard_map/ppermute | solution.py:128
  32.8 0.2 copy.22
  33.0 4.9 %collective-permute-done = f32[200,6,128]{2,0,1:T(8,128)S(1)} collective-permute-done((f32[200,6,128]{2,0,1:T(8,128)S(1)}, f32[200,6,128]{2,0,1:T(8,128)S(1)}, u32[]{:S(2)}, u32[]{:S(2)}) %collective-permute-start) | collective-permute-done | bytes 614432 | tf_op jit(solution)/shard_map/ppermute | solution.py:127
  37.9 0.2 copy.20
  38.0 2.3 %maximum_maximum_fusion.adjoint_ref = f32[4,50,32,128]{3,2,1,0:T(8,128)} fusion(f32[4,50,6,128]{3,2,1,0:T(8,128)S(1)} %bitcast.39, f32[4,50,16,128]{3,2,1,0:T(8,128)S(1)} %copy-done.1, f32[4,50,6,128]{3,2,1,0:T(8,128)S(1)} %bitcast.40, f32[32]{0:T(128)S(1)} %pad.34.clone), kind=kLoop, calls=%fused_computation | loop fusion | flops 2457600 | bytes 6144128 | tf_op jit(solution)/shard_map/concatenate | solution.py:135
  40.4 16.5 %shard_map.141 = f32[4,50,16,128]{3,2,1,0:T(8,128)} custom-call(f32[4,50,32,128]{3,2,1,0:T(8,128)} %maximum_maximum_fusion.adjoint_ref, f32[50,32,128]{2,1,0:T(8,128)} %get-tuple-element.29.east_a_ref, f32[50,32,128]{2,1,0:T(8,128)} %get-tuple-element.28.east_b_ref, f32[50,32,128]{2,1,0:T(8,128)} %get-tuple-element.31.north_a_ref, ...), custom_call_target="tpu_custom_call" | custom-call | tf_op jit(solution)/shard_map/pallas_call | solution.py:112
  56.9 1.6 %fusion.1 = f32[50,16,128]{2,1,0:T(8,128)S(1)} fusion(f32[2,2,50,16,128]{4,3,2,1,0:T(8,128)} %bitcast.33), kind=kLoop, calls=%fused_computation.6 | loop fusion | flops 512000 | bytes 2048000 | tf_op jit(solution)/shard_map/reduce_sum | solution.py:192
  58.4 0.0 copy-start.9
  58.4 0.0 copy-start
  58.5 19.2 %all_to_all.10 = f32[8,100,128]{2,1,0:T(8,128)S(1)} all-to-all(f32[8,100,128]{2,1,0:T(8,128)S(1)} %reshape.126), channel_id=1, replica_groups=mesh['scen'=8,'grid'=32] {'scen'}, dimensions={0} | all-to-all | bytes 819200 | tf_op jit(solution)/shard_map/all_to_all | solution.py:78
  77.7 0.8 broadcast_in_dim.13
  78.5 5.1 %all-to-all-start.1 = ((f32[8,100,128]{2,1,0:T(8,128)}), f32[8,100,128]{2,1,0:T(8,128)S(1)}, u32[]{:S(2)}, u32[]{:S(2)}) async-start(f32[8,100,128]{2,1,0:T(8,128)} %broadcast_in_dim.13), calls=%async_computation.1 | async-start | bytes 851968 | tf_op jit(solution)/shard_map/all_to_all | solution.py:81
  83.6 0.0 copy-start.6
  83.6 0.0 copy-start.7
  83.6 0.0 copy-start.5
  83.6 1.2 %copy.28 = f32[2,2,50,16,128]{4,3,2,1,0:T(8,128)} copy(f32[2,2,50,16,128]{4,3,2,1,0:T(8,128)S(1)} %bitcast.34) | data formatting | bytes 3276800
  84.8 0.6 fusion.6
  85.5 1.3 %fusion.3 = f32[2,2,50,16,128]{4,3,2,1,0:T(8,128)} fusion(f32[2,2,50,16,128]{4,3,2,1,0:T(8,128)} %fusion.6, f32[2,16,128]{2,1,0:T(8,128)S(1)} %copy-done.6, f32[2,16,128]{2,1,0:T(8,128)S(1)} %copy-done.7, f32[2,2,50,16,128]{4,3,2,1,0:T(8,128)S(1)} %bitcast.37, f32[16,128]{1,0:T(8,128)S(1)} %fusion.7), kind=kLoop, calls=%fused_computation.24 | loop fusion | flops 53248 | bytes 90112 | tf_op jit(solution)/shard_map/scatter-add | solution.py:201
  86.8 7.1 %all-to-all-done.1 = f32[8,100,128]{2,1,0:T(8,128)S(1)} async-done(((f32[8,100,128]{2,1,0:T(8,128)}), f32[8,100,128]{2,1,0:T(8,128)S(1)}, u32[]{:S(2)}, u32[]{:S(2)}) %all-to-all-start.1) | async-done | bytes 409632 | tf_op jit(solution)/shard_map/all_to_all | solution.py:81
  94.0 0.9 fusion.2
  (34 shorter events, 0.4 us)
Async XLA Ops:
  1.4 7.8 %copy-start.8 = (f32[50]{0:T(128)S(1)}, f32[50]{0:T(128)}, u32[]{:S(2)}) copy-start(f32[50]{0:T(128)} %param.25) | copy-start | bytes 604
  2.7 8.7 %copy-start.4 = (f32[50,16,128]{2,1,0:T(8,128)S(1)}, f32[50,16,128]{2,1,0:T(8,128)}, u32[]{:S(2)}) copy-start(f32[50,16,128]{2,1,0:T(8,128)} %param.24) | copy-start | bytes 1228804
  2.7 21.8 %collective-permute-start.3 = (f32[101,6,128]{2,1,0:T(8,128)S(1)}, f32[101,6,128]{2,1,0:T(8,128)S(1)}, u32[]{:S(2)}, u32[]{:S(2)}) collective-permute-start(f32[101,6,128]{2,1,0:T(8,128)S(1)} %pad_maximum_fusion.1), channel_id=1, source_target_pairs={{1,0},{2,1},{3,2},{4,3},{5,4},{6,5},{7,6},{8,7},{9,8},{10,9},{11,1... | collective-permute-start | bytes 930824 | tf_op jit(solution)/shard_map/ppermute | solution.py:128
  9.1 15.4 %collective-permute-start.2 = (f32[101,6,128]{2,1,0:T(8,128)S(1)}, f32[101,6,128]{2,1,0:T(8,128)S(1)}, u32[]{:S(2)}, u32[]{:S(2)}) collective-permute-start(f32[101,6,128]{2,1,0:T(8,128)S(1)} %pad_maximum_fusion), channel_id=1, source_target_pairs={{0,1},{1,2},{2,3},{3,4},{4,5},{5,6},{6,7},{7,8},{8,9},{9,10},{10,1... | collective-permute-start | bytes 930824 | tf_op jit(solution)/shard_map/ppermute | solution.py:127
  18.5 14.4 %collective-permute-start.1 = (f32[200,6,128]{2,0,1:T(8,128)S(1)}, f32[200,6,128]{2,0,1:T(8,128)S(1)}, u32[]{:S(2)}, u32[]{:S(2)}) collective-permute-start(f32[200,6,128]{2,0,1:T(8,128)S(1)} %copy.26), channel_id=1, source_target_pairs={{1,0},{2,1},{3,2},{4,3},{5,4},{6,5},{7,6},{8,7},{9,8},{10,9},{11,1... | collective-permute-start | bytes 1843208 | tf_op jit(solution)/shard_map/ppermute | solution.py:128
  24.3 13.6 %collective-permute-start = (f32[200,6,128]{2,0,1:T(8,128)S(1)}, f32[200,6,128]{2,0,1:T(8,128)S(1)}, u32[]{:S(2)}, u32[]{:S(2)}) collective-permute-start(f32[200,6,128]{2,0,1:T(8,128)S(1)} %copy.25), channel_id=1, source_target_pairs={{0,1},{1,2},{2,3},{3,4},{4,5},{5,6},{6,7},{7,8},{8,9},{9,10},{10,1... | collective-permute-start | bytes 1843208 | tf_op jit(solution)/shard_map/ppermute | solution.py:127
  24.8 1.0 %copy-start.2 = (f32[50,16,128]{2,1,0:T(8,128)S(1)}, f32[50,16,128]{2,1,0:T(8,128)}, u32[]{:S(2)}) copy-start(f32[50,16,128]{2,1,0:T(8,128)} %param.21) | copy-start | bytes 1228804
  24.8 1.0 %copy-start.10 = (f32[50]{0:T(128)S(1)}, f32[50]{0:T(128)}, u32[]{:S(2)}) copy-start(f32[50]{0:T(128)} %param.23) | copy-start | bytes 604
  25.8 1.8 %copy-start.3 = (f32[50,16,128]{2,1,0:T(8,128)S(1)}, f32[50,16,128]{2,1,0:T(8,128)}, u32[]{:S(2)}) copy-start(f32[50,16,128]{2,1,0:T(8,128)} %param.20) | copy-start | bytes 1228804
  25.8 1.8 %copy-start.11 = (f32[50]{0:T(128)S(1)}, f32[50]{0:T(128)}, u32[]{:S(2)}) copy-start(f32[50]{0:T(128)} %param.22) | copy-start | bytes 604
  29.4 8.6 %copy-start.1 = (f32[4,50,16,128]{3,2,1,0:T(8,128)S(1)}, f32[4,50,16,128]{3,2,1,0:T(8,128)}, u32[]{:S(2)}) copy-start(f32[4,50,16,128]{3,2,1,0:T(8,128)} %shard_map.140) | copy-start | bytes 4915204
  58.4 25.2 %copy-start.9 = (f32[16,128]{1,0:T(8,128)S(1)}, f32[16,128]{1,0:T(8,128)}, u32[]{:S(2)}) copy-start(f32[16,128]{1,0:T(8,128)} %param.27) | copy-start | bytes 24580
  58.4 25.2 %copy-start = (f32[4,50,16,128]{3,2,1,0:T(8,128)S(1)}, f32[4,50,16,128]{3,2,1,0:T(8,128)}, u32[]{:S(2)}) copy-start(f32[4,50,16,128]{3,2,1,0:T(8,128)} %shard_map.141) | copy-start | bytes 4915204
  78.5 15.4 %all-to-all-start.1 = ((f32[8,100,128]{2,1,0:T(8,128)}), f32[8,100,128]{2,1,0:T(8,128)S(1)}, u32[]{:S(2)}, u32[]{:S(2)}) async-start(f32[8,100,128]{2,1,0:T(8,128)} %broadcast_in_dim.13), calls=%async_computation.1 | async-start | bytes 851968 | tf_op jit(solution)/shard_map/all_to_all | solution.py:81
  83.6 1.2 %copy-start.6 = (f32[2,16,128]{2,1,0:T(8,128)S(1)}, f32[2,16,128]{2,1,0:T(8,128)}, u32[]{:S(2)}) copy-start(f32[2,16,128]{2,1,0:T(8,128)} %param.19) | copy-start | bytes 49156
  83.6 1.2 %copy-start.7 = (f32[2,16,128]{2,1,0:T(8,128)S(1)}, f32[2,16,128]{2,1,0:T(8,128)}, u32[]{:S(2)}) copy-start(f32[2,16,128]{2,1,0:T(8,128)} %param.18) | copy-start | bytes 49156
  83.6 10.3 %copy-start.5 = (f32[50,16,128]{2,1,0:T(8,128)S(1)}, f32[50,16,128]{2,1,0:T(8,128)}, u32[]{:S(2)}) copy-start(f32[50,16,128]{2,1,0:T(8,128)} %param.26) | copy-start | bytes 1228804
